TPU v7x, 256 devices: a whole 4x4x8 slice. The times are simulated.
256 devices in a mesh: group: 8 (over z), dom: 32 (over x, y, core).
Axes of the slice: x: 4, y: 4, z: 8, core: 2. Of those that a mesh axis runs over, the one named last changes fastest.
Arguments:
- feats: bfloat16 [32768, 1024], P(('group', 'dom')), may hold values from -6 to 6
- history: bfloat16 [32768, 1024], P(('group', 'dom')), may hold values from -0.25 to 2
- grad_out: bfloat16 [32768, 1024], P(('group', 'dom')), may hold values from -24 to 24
- w_first: bfloat16 [1024, 1024], replicated, may hold values from -0.1875 to 0.1875
- w_second: bfloat16 [1024, 1024], replicated, may hold values from -0.1875 to 0.1875
- send_index: int32 [256, 32, 16], P(('group', 'dom')), may hold values from 0 to 127, as said below
- halo_index: int32 [131072], P(('group', 'dom')), may hold values from 0 to 511
- hub_rows: int32 [256, 32], P(('group', 'dom')), may hold values from 0 to 127
- tile_cols: int32 [256, 4], P(('group', 'dom')), may hold values from 0 to 6
- tile_vals: bfloat16 [256, 4, 128, 128], P(('group', 'dom')), may hold values from -0.25 to 0.25
Outputs:
- new_history: bfloat16 [32768, 1024], P(('group', 'dom'))
- embed_grad: bfloat16 [32768, 1024], P(('group', 'dom'))
- grad_first: float32 [1024, 1024], P(('group', 'dom'))
- grad_second: float32 [1024, 1024], P(('group', 'dom'))
Inputs may be any that keep to these rules, and one draw needn't show every extreme that they name: `send_index`: for each device and each dom peer the 16 rows are distinct. `halo_index`: A value q names slot q % 16 of the rows received from dom peer q // 16 of the same group; values may repeat. `hub_rows`: rows may repeat. `tile_cols`: source tile 0 is the device's own rows, tiles 1 to 4 are halo tiles, tiles 5 and 6 are hub tiles; values may repeat in a row.
All inputs are finite; a program needn't handle non-finite values.
Results may differ from a plain program's by a relative error of at most 0.006.
Values may be sent and summed in bfloat16 or wider, within the bound.
No kernel may reach another device: no remote copies, remote signals or barrier semaphores. Data moves between devices by JAX's collectives and lax.ppermute only.
A program may use at most 64 MiB of HBM per device.

v0:
```python
import math

import jax
import jax.numpy as jnp
from jax import lax
from jax.sharding import PartitionSpec as P

D = 1024
V_DEV = 128
TILE = 128
HALO = 512


def combine_tiles(own_rows, halo_rows, hub_panel, tile_cols, tile_vals):
    source = jnp.concatenate([own_rows, halo_rows, hub_panel], axis=0)
    feature_width = source.shape[1]
    picked = source.reshape(-1, tile_vals.shape[2], feature_width)[tile_cols]
    summed = jnp.einsum("rtij,rtjd->rid", tile_vals, picked, preferred_element_type=jnp.float32)
    return summed.reshape(-1, feature_width).astype(jnp.bfloat16)


def reduce_weight(left_rows, right_rows):
    factor = 1.0 / math.sqrt(left_rows.shape[0] * lax.axis_size("group") * lax.axis_size("dom"))
    product = lax.dot_general(
        left_rows, right_rows, (((0,), (0,)), ((), ())), preferred_element_type=jnp.float32
    )
    summed = lax.psum_scatter(product, ("group", "dom"), scatter_dimension=0, tiled=True)
    return summed * factor


def on_device(
    feats,
    history,
    grad_out,
    w_first,
    w_second,
    send_index,
    halo_index,
    hub_rows,
    tile_cols,
    tile_vals,
):
    routes = send_index[0]
    owned_hubs = hub_rows[0]
    feat_slots = lax.all_to_all(feats[routes], "dom", split_axis=0, concat_axis=0, tiled=True)
    feat_halo = feat_slots.reshape(-1, D)[halo_index]
    hub_first = lax.all_gather(feats[owned_hubs], "group", axis=0, tiled=True)
    agg_first = combine_tiles(feats, feat_halo, hub_first, tile_cols, tile_vals)
    z_first = jnp.dot(agg_first, w_first, preferred_element_type=jnp.float32)
    new_history = jax.nn.silu(z_first).astype(jnp.bfloat16)
    hist_slots = lax.all_to_all(history[routes], "dom", split_axis=0, concat_axis=0, tiled=True)
    hist_halo = hist_slots.reshape(-1, D)[halo_index]
    hub_second = lax.all_gather(new_history[owned_hubs], "group", axis=0, tiled=True)
    agg_second = combine_tiles(new_history, hist_halo, hub_second, tile_cols, tile_vals)
    grad_second = reduce_weight(grad_out, agg_second)
    agg_grad = lax.dot_general(
        grad_out, w_second, (((1,), (1,)), ((), ())), preferred_element_type=jnp.float32
    ).astype(jnp.bfloat16)
    source_tiles = (V_DEV + HALO + hub_second.shape[0]) // TILE
    tile_terms = jnp.einsum(
        "rtij,rid->rtjd",
        tile_vals,
        agg_grad.reshape(-1, TILE, D),
        preferred_element_type=jnp.float32,
    )
    selector = (
        tile_cols[:, :, None] == jnp.arange(source_tiles, dtype=jnp.int32)[None, None, :]
    ).astype(jnp.float32)
    spread = jnp.einsum(
        "rts,rtjd->sjd", selector, tile_terms, precision=lax.Precision.HIGHEST
    ).reshape(-1, D)
    own_grad = spread[:V_DEV]
    hub_grad = lax.psum_scatter(spread[V_DEV + HALO :], "group", scatter_dimension=0, tiled=True)
    vertex_grad = own_grad.at[owned_hubs].add(hub_grad)
    gate_value = jax.nn.sigmoid(z_first)
    dz_first = (vertex_grad * gate_value * (1.0 + z_first * (1.0 - gate_value))).astype(
        jnp.bfloat16
    )
    grad_first = reduce_weight(dz_first, agg_first)
    return (new_history, vertex_grad.astype(jnp.bfloat16), grad_first, grad_second)


def solution(mesh):
    placed = (
        P(("group", "dom"), None),
        P(("group", "dom"), None),
        P(("group", "dom"), None),
        P(),
        P(),
        P(("group", "dom"), None, None),
        P(("group", "dom")),
        P(("group", "dom"), None),
        P(("group", "dom"), None),
        P(("group", "dom"), None, None, None),
    )
    return jax.shard_map(
        on_device,
        mesh=mesh,
        in_specs=placed,
        out_specs=(
            P(("group", "dom"), None),
            P(("group", "dom"), None),
            P(("group", "dom"), None),
            P(("group", "dom"), None),
        ),
        check_vma=False,
    )
```

profile of v0, /device:TPU:1, one launch (start us, length us, event | category | flops | bytes accessed | tf_op | source)
XLA Modules:
  0.0 430.5 jit_solution(8071109135785780543)
XLA Ops:
  7.2 0.8 compare_select_fusion
  8.2 4.5 %gather_fusion = bf16[512,1024]{1,0:T(8,128)(2,1)} fusion(bf16[128,1024]{1,0:T(8,128)(2,1)} %param.10, s32[1024]{0:T(1024)S(1)} %pad_clamp_fusion.3), kind=kCustom, calls=%fused_computation | custom fusion | bytes 2099200 | tf_op jit(solution)/shard_map/gather | solution.py:45
  12.7 8.8 %all-to-all-start = ((bf16[32,16,1024]{2,1,0:T(8,128)(2,1)}), bf16[32,16,1024]{2,1,0:T(8,128)(2,1)}, u32[]{:S(2)}, u32[]{:S(2)}) async-start(bf16[32,16,1024]{2,1,0:T(8,128)(2,1)} %bitcast.1), calls=%async_computation | async-start | bytes 2097152 | tf_op jit(solution)/shard_map/all_to_all | solution.py:45
  21.5 2.5 convolution_bitcast_fusion.1
  24.0 3.1 copy.32
  27.1 4.2 fusion.10
  31.9 1.3 copy-done.4
  33.2 1.4 copy.34
  34.7 1.3 gather_fusion.2
  36.0 0.9 copy.43
  36.9 2.8 gather_fusion.4
  40.2 7.4 %all-to-all-start.1 = ((bf16[32,16,1024]{2,1,0:T(8,128)(2,1)}), bf16[32,16,1024]{2,1,0:T(8,128)(2,1)S(1)}, u32[]{:S(2)}, u32[]{:S(2)}) async-start(bf16[32,16,1024]{2,1,0:T(8,128)(2,1)} %bitcast.63), calls=%async_computation.2 | async-start | bytes 2097152 | tf_op jit(solution)/shard_map/all_to_all | solution.py:51
  47.6 0.7 pad_clamp_fusion
  48.3 27.2 %all-gather = bf16[256,1024]{1,0:T(8,128)(2,1)} all-gather(bf16[32,1024]{1,0:T(8,128)(2,1)} %gather_fusion.2), channel_id=2, replica_groups=mesh['group'=8,'dom'=32] {'group'}, dimensions={0}, use_global_device_ids=true | all-gather | bytes 589824 | tf_op jit(solution)/shard_map/all_gather | solution.py:47
  75.5 4.8 %gather_fusion.1 = bf16[512,1024]{1,0:T(8,128)(2,1)} fusion(bf16[512,1024]{1,0:T(8,128)(2,1)} %bitcast.2, s32[1024]{0:T(1024)S(1)} %pad_clamp_fusion.2), kind=kCustom, calls=%fused_computation.1 | custom fusion | bytes 2099200 | tf_op jit(solution)/shard_map/gather | solution.py:46
  80.3 2.8 pad_maximum_fusion
  83.1 3.1 gather_fusion.3
  86.2 1.7 fusion
  87.9 0.7 copy-done.9
  88.6 2.9 multiply_convert_fusion.1
  91.5 1.3 gather_fusion.6
  92.8 2.8 gather_fusion.5
  95.6 20.0 %all-gather.1 = bf16[256,1024]{1,0:T(8,128)(2,1)S(1)} all-gather(bf16[32,1024]{1,0:T(8,128)(2,1)} %gather_fusion.6), channel_id=3, replica_groups=mesh['group'=8,'dom'=32] {'group'}, dimensions={0}, use_global_device_ids=true | all-gather | bytes 589824 | tf_op jit(solution)/shard_map/all_gather | solution.py:53
  115.6 2.7 pad_maximum_fusion.1
  118.3 2.1 gather_fusion.7
  120.4 3.4 convolution_bitcast_fusion
  123.8 5.4 %copy.36 = f32[1024,1024]{1,0:T(8,128)} copy(f32[1024,1024]{0,1:T(8,128)} %convolution_bitcast_fusion) | data formatting | bytes 8388608 | tf_op jit(solution)/shard_map/dot_general | solution.py:24
  129.2 1.5 scatter_fusion
  130.8 2.7 fusion.3
  133.5 0.7 convert_element_type.24
  134.3 288.0 %all-reduce.5.cloned.1.call-done = (f32[1024,1024]{1,0:T(8,128)}, f32[1024,1024]{1,0:T(8,128)}) async-done(((f32[1024,1024]{1,0:T(8,128)}, f32[1024,1024]{1,0:T(8,128)}), (f32[1024,1024]{1,0:T(8,128)}, f32[1024,1024]{1,0:T(8,128)})) %all-reduce.5.cloned.1.call-update) | async-done | bytes 8388624
  422.3 1.4 dynamic-slice_multiply_fusion
  (46 shorter events, 1.5 us)
Async XLA Ops:
  7.2 14.3 %copy-start = (bf16[1024,1024]{1,0:T(8,128)(2,1)S(1)}, bf16[1024,1024]{1,0:T(8,128)(2,1)}, u32[]{:S(2)}) copy-start(bf16[1024,1024]{1,0:T(8,128)(2,1)} %param.14) | copy-start | bytes 6291460
  12.7 8.8 %copy-start.6 = (bf16[1,4,128,128]{3,2,1,0:T(8,128)(2,1)S(1)}, bf16[1,4,128,128]{3,2,1,0:T(8,128)(2,1)}, u32[]{:S(2)}) copy-start(bf16[1,4,128,128]{3,2,1,0:T(8,128)(2,1)} %param.19) | copy-start | bytes 393220
  12.7 8.8 %copy-start.7 = (bf16[128,1024]{1,0:T(8,128)(2,1)S(1)}, bf16[128,1024]{1,0:T(8,128)(2,1)}, u32[]{:S(2)}) copy-start(bf16[128,1024]{1,0:T(8,128)(2,1)} %param.12) | copy-start | bytes 786436
  12.7 27.5 %all-to-all-start = ((bf16[32,16,1024]{2,1,0:T(8,128)(2,1)}), bf16[32,16,1024]{2,1,0:T(8,128)(2,1)}, u32[]{:S(2)}, u32[]{:S(2)}) async-start(bf16[32,16,1024]{2,1,0:T(8,128)(2,1)} %bitcast.1), calls=%async_computation | async-start | bytes 2097152 | tf_op jit(solution)/shard_map/all_to_all | solution.py:45
  21.4 107.8 %reduce-scatter.2.cloned.1.call-start = ((), (), s32[]{:S(2)}) async-start(), calls=%async_computation.3 | async-start | bytes 1179648 | tf_op jit(solution)/shard_map/reduce_scatter | solution.py:73
  24.0 3.1 copy-start.13
  31.3 1.9 copy-start.4
  33.2 1.4 copy-start.14
  33.2 1.4 copy-start.12
  33.2 1.5 copy-start.1
  34.6 1.4 slice-start
  34.6 2.3 copy-start.2
  40.2 52.6 %all-to-all-start.1 = ((bf16[32,16,1024]{2,1,0:T(8,128)(2,1)}), bf16[32,16,1024]{2,1,0:T(8,128)(2,1)S(1)}, u32[]{:S(2)}, u32[]{:S(2)}) async-start(bf16[32,16,1024]{2,1,0:T(8,128)(2,1)} %bitcast.63), calls=%async_computation.2 | async-start | bytes 2097152 | tf_op jit(solution)/shard_map/all_to_all | solution.py:51
  47.6 374.7 %all-reduce.5.cloned.1.call-start = ((), (), s32[]{:S(2)}) async-start(), calls=%async_computation.4 | async-start | bytes 16777216
  87.9 0.7 copy-start.9
  91.5 24.0 %copy-start.5 = (bf16[128,1024]{1,0:T(8,128)(2,1)}, bf16[128,1024]{1,0:T(8,128)(2,1)S(1)}, u32[]{:S(2)}) copy-start(bf16[128,1024]{1,0:T(8,128)(2,1)S(1)} %get-tuple-element.6) | copy-start | bytes 786436
  115.6 4.9 %copy-start.8 = (bf16[128,1024]{1,0:T(8,128)(2,1)S(1)}, bf16[128,1024]{1,0:T(8,128)(2,1)}, u32[]{:S(2)}) copy-start(bf16[128,1024]{1,0:T(8,128)(2,1)} %param.12) | copy-start | bytes 786436
  123.8 5.4 %copy-start.3 = (f32[1,128,1024]{2,1,0:T(8,128)S(1)}, f32[1,128,1024]{2,1,0:T(8,128)}, u32[]{:S(2)}) copy-start(f32[1,128,1024]{2,1,0:T(8,128)} %copy.43) | copy-start | bytes 1572868
  129.2 1.5 copy-start.10
  129.2 1.5 copy-start.11
Sparse Core Ops, SparseCore 0:
  34.8 39.0 reduce-scatter.1
  133.6 288.5 all-reduce.4
where the time goes:
time: 432 us; the launch traced here: 431 us
  waiting for transfers between devices  288 us (67%)
  blocking collectives  47.2 us (11%)
  local copies, waits for them, and re-layouts  36.2 us (8%)
  matrix products  17.4 us (4%)
  starting transfers between devices  16.2 us (4%)
  between operations  14.2 us (3%)
  other arithmetic  11.3 us (3%)
    unnamed x3, waiting for transfers between devices  288 us
    all_gather x1, blocking collectives, on_device(): hub_first = lax.all_gather(feats[owned_hubs], 'group', axis=0, tiled=True)  27.2 us
    all_gather x1, blocking collectives, on_device(): lax.all_gather(new_history[owned_hubs], 'group', axis=0, tiled=True)  20 us
    all_to_all x1, starting transfers between devices, on_device(): lax.all_to_all(feats[routes], 'dom', split_axis=0, concat_axis=0, tiled=T...  8.76 us
  transfers between devices with their start and end apart: 4, of which 1 were waited for; matrix products, arithmetic and copies ran while one was open for 12% of the time, Pallas kernels for 0%

commit v1 on v0

--- a/solution.py
+++ b/solution.py
@@ -19,13 +19,27 @@
     return summed.reshape(-1, feature_width).astype(jnp.bfloat16)
 
 
-def reduce_weight(left_rows, right_rows):
-    factor = 1.0 / math.sqrt(left_rows.shape[0] * lax.axis_size("group") * lax.axis_size("dom"))
-    product = lax.dot_general(
+def weight_product(left_rows, right_rows):
+    return lax.dot_general(
         left_rows, right_rows, (((0,), (0,)), ((), ())), preferred_element_type=jnp.float32
     )
-    summed = lax.psum_scatter(product, ("group", "dom"), scatter_dimension=0, tiled=True)
-    return summed * factor
+
+
+def reduce_weight(product, rows_per_device):
+    factor = 1.0 / math.sqrt(rows_per_device * lax.axis_size("group") * lax.axis_size("dom"))
+    n_dom = lax.axis_size("dom")
+    in_group = lax.psum_scatter(product, "group", scatter_dimension=0, tiled=True)
+    pieces = lax.all_to_all(
+        in_group.reshape(n_dom, -1, in_group.shape[1]), "dom", split_axis=0, concat_axis=0, tiled=True
+    )
+    return pieces.sum(axis=0) * factor
+
+
+def gather_hubs(hub_rows):
+    n_group = lax.axis_size("group")
+    copies = jnp.broadcast_to(hub_rows[None], (n_group,) + hub_rows.shape)
+    spread = lax.all_to_all(copies, "group", split_axis=0, concat_axis=0, tiled=True)
+    return spread.reshape(-1, hub_rows.shape[1])
 
 
 def on_device(
@@ -42,21 +56,13 @@
 ):
     routes = send_index[0]
     owned_hubs = hub_rows[0]
-    feat_slots = lax.all_to_all(feats[routes], "dom", split_axis=0, concat_axis=0, tiled=True)
-    feat_halo = feat_slots.reshape(-1, D)[halo_index]
-    hub_first = lax.all_gather(feats[owned_hubs], "group", axis=0, tiled=True)
-    agg_first = combine_tiles(feats, feat_halo, hub_first, tile_cols, tile_vals)
-    z_first = jnp.dot(agg_first, w_first, preferred_element_type=jnp.float32)
-    new_history = jax.nn.silu(z_first).astype(jnp.bfloat16)
-    hist_slots = lax.all_to_all(history[routes], "dom", split_axis=0, concat_axis=0, tiled=True)
-    hist_halo = hist_slots.reshape(-1, D)[halo_index]
-    hub_second = lax.all_gather(new_history[owned_hubs], "group", axis=0, tiled=True)
-    agg_second = combine_tiles(new_history, hist_halo, hub_second, tile_cols, tile_vals)
-    grad_second = reduce_weight(grad_out, agg_second)
+    rows = feats.shape[0]
+
     agg_grad = lax.dot_general(
         grad_out, w_second, (((1,), (1,)), ((), ())), preferred_element_type=jnp.float32
     ).astype(jnp.bfloat16)
-    source_tiles = (V_DEV + HALO + hub_second.shape[0]) // TILE
+    n_hub = lax.axis_size("group") * owned_hubs.shape[0]
+    source_tiles = (V_DEV + HALO + n_hub) // TILE
     tile_terms = jnp.einsum(
         "rtij,rid->rtjd",
         tile_vals,
@@ -72,11 +78,26 @@
     own_grad = spread[:V_DEV]
     hub_grad = lax.psum_scatter(spread[V_DEV + HALO :], "group", scatter_dimension=0, tiled=True)
     vertex_grad = own_grad.at[owned_hubs].add(hub_grad)
+
+    feat_slots = lax.all_to_all(feats[routes], "dom", split_axis=0, concat_axis=0, tiled=True)
+    hist_slots = lax.all_to_all(history[routes], "dom", split_axis=0, concat_axis=0, tiled=True)
+    hub_first = gather_hubs(feats[owned_hubs])
+    feat_halo = feat_slots.reshape(-1, D)[halo_index]
+    agg_first = combine_tiles(feats, feat_halo, hub_first, tile_cols, tile_vals)
+    z_first = jnp.dot(agg_first, w_first, preferred_element_type=jnp.float32)
+    new_history = jax.nn.silu(z_first).astype(jnp.bfloat16)
     gate_value = jax.nn.sigmoid(z_first)
     dz_first = (vertex_grad * gate_value * (1.0 + z_first * (1.0 - gate_value))).astype(
         jnp.bfloat16
     )
-    grad_first = reduce_weight(dz_first, agg_first)
+    product_first = weight_product(dz_first, agg_first)
+    product_first, new_history = lax.optimization_barrier((product_first, new_history))
+    grad_first = reduce_weight(product_first, rows)
+
+    hist_halo = hist_slots.reshape(-1, D)[halo_index]
+    hub_second = gather_hubs(new_history[owned_hubs])
+    agg_second = combine_tiles(new_history, hist_halo, hub_second, tile_cols, tile_vals)
+    grad_second = reduce_weight(weight_product(grad_out, agg_second), rows)
     return (new_history, vertex_grad.astype(jnp.bfloat16), grad_first, grad_second)
 
 

time: 432 us -> 242 us (0.56)
  waiting for transfers between devices: 288 us -> 110 us
  blocking collectives: 47.2 us -> 0 us
  starting transfers between devices: 16.2 us -> 46.6 us
  local copies, waits for them, and re-layouts: 36.2 us -> 41.5 us
    unnamed x3, waiting for transfers between devices: 288 us -> 0.05 us
    all_gather x2 -> x0, blocking collectives: 47.2 us -> none  [the longest x1 27.2 us: on_device(): hub_first = lax.all_gather(feats[owned_hubs], 'group', axis=0, tiled=True)]
    reduce_scatter x0 -> x2, waiting for transfers between devices: none -> 46.8 us  [reduce_weight(): lax.psum_scatter(product, 'group', scatter_dimension=0, tiled=True)]
    all_to_all x0 -> x4, waiting for transfers between devices: none -> 44.4 us  [the longest x2 34.3 us: gather_hubs(): lax.all_to_all(copies, 'group', split_axis=0, concat_axis=0, tiled=True)]
    all_to_all x0 -> x4, starting transfers between devices: none -> 27.5 us  [the longest x2 14.6 us: reduce_weight(): lax.all_to_all(in_group.reshape(n_dom, -1, in_group.shape[1]), 'dom', spl...]
    all_to_all x1, waiting for transfers between devices: 0.01 us -> 15.7 us  [on_device(): lax.all_to_all(history[routes], 'dom', split_axis=0, concat_axis=0, tiled...]
    dot_general x1 -> x0, local copies, waits for them, and re-layouts: 5.4 us -> none  [reduce_weight(): lax.dot_general(left_rows, right_rows, (((0,), (0,)), ((), ())), preferre...]
  transfers between devices with their start and end apart: 4 -> 9, of which waited for: 1 -> 7; matrix products, arithmetic and copies ran while one was open for 12% -> 23% of each run, Pallas kernels for 0% -> 0%
where the time goes in v1:
time: 242 us; the launch traced here: 241 us
  waiting for transfers between devices  110 us (45%)
  starting transfers between devices  46.6 us (19%)
  local copies, waits for them, and re-layouts  41.5 us (17%)
  matrix products  17.4 us (7%)
  between operations  14 us (6%)
  other arithmetic  11.8 us (5%)
    reduce_scatter x2, waiting for transfers between devices, reduce_weight(): lax.psum_scatter(product, 'group', scatter_dimension=0, tiled=True)  46.8 us
    all_to_all x2, waiting for transfers between devices, gather_hubs(): lax.all_to_all(copies, 'group', split_axis=0, concat_axis=0, tiled=True)  34.3 us
    all_to_all x1, waiting for transfers between devices, on_device(): lax.all_to_all(history[routes], 'dom', split_axis=0, concat_axis=0, tiled...  15.7 us
    all_to_all x2, starting transfers between devices, reduce_weight(): lax.all_to_all(in_group.reshape(n_dom, -1, in_group.shape[1]), 'dom', spl...  14.6 us
    all_to_all x2, starting transfers between devices, gather_hubs(): lax.all_to_all(copies, 'group', split_axis=0, concat_axis=0, tiled=True)  12.9 us
    all_to_all x1, starting transfers between devices, on_device(): lax.all_to_all(history[routes], 'dom', split_axis=0, concat_axis=0, tiled...  10.2 us
    all_to_all x2, waiting for transfers between devices, reduce_weight(): lax.all_to_all(in_group.reshape(n_dom, -1, in_group.shape[1]), 'dom', spl...  10.2 us
    all_to_all x1, starting transfers between devices, on_device(): lax.all_to_all(feats[routes], 'dom', split_axis=0, concat_axis=0, tiled=T...  8.71 us
  transfers between devices with their start and end apart: 9, of which 7 were waited for; matrix products, arithmetic and copies ran while one was open for 23% of the time, Pallas kernels for 0%

profile of v1, /device:TPU:1, one launch (start us, length us, event | category | flops | bytes accessed | tf_op | source)
XLA Modules:
  0.0 241.0 jit_solution(13111292970836994064)
XLA Ops:
  8.2 4.5 %gather_fusion = bf16[512,1024]{1,0:T(8,128)(2,1)} fusion(bf16[128,1024]{1,0:T(8,128)(2,1)} %param.10, s32[1024]{0:T(1024)S(1)} %pad_clamp_fusion.3), kind=kCustom, calls=%fused_computation | custom fusion | bytes 2099200 | tf_op jit(solution)/shard_map/gather | solution.py:82
  12.7 8.7 %all-to-all-start = ((bf16[32,16,1024]{2,1,0:T(8,128)(2,1)}), bf16[32,16,1024]{2,1,0:T(8,128)(2,1)S(1)}, u32[]{:S(2)}, u32[]{:S(2)}) async-start(bf16[32,16,1024]{2,1,0:T(8,128)(2,1)} %bitcast.66), calls=%async_computation.1 | async-start | bytes 2097152 | tf_op jit(solution)/shard_map/all_to_all | solution.py:82
  21.5 2.5 %fusion.5 = f32[1024,4,128]{2,0,1:T(8,128)} fusion(bf16[128,1024]{1,0:T(8,128)(2,1)S(1)} %copy-done.9, bf16[1024,1024]{1,0:T(8,128)(2,1)S(1)} %copy-done, bf16[1,4,128,128]{3,2,1,0:T(8,128)(2,1)S(1)} %copy-done.8), kind=kOutput, calls=%fused_computation.20 | convolution fusion | flops 402784256 | bytes 4587520 | tf_op jit(solution)/shard_map/rtij,rid->rtjd/dot_general | solution.py:66
  23.9 3.1 %copy.18 = f32[1024,4,128]{0,1,2:T(4,128)} copy(f32[1024,4,128]{2,0,1:T(8,128)} %fusion.5) | data formatting | bytes 4194304 | tf_op jit(solution)/shard_map/rtij,rid->rtjd/dot_general | solution.py:66
  27.0 4.2 %fusion = f32[7,128,1024]{2,0,1:T(8,128)S(1)} fusion(f32[1024,4,128]{0,1,2:T(4,128)} %copy.18, s32[4]{0:T(128)S(1)} %bitcast.69), kind=kOutput, calls=%fused_computation.10 | convolution fusion | flops 44040220 | bytes 5767184 | tf_op jit(solution)/shard_map/rts,rtjd->sjd/dot_general | solution.py:75
  31.2 1.9 copy-done.6
  36.5 1.8 all-to-all-done
  40.0 8.2 %all-to-all-start.1 = ((bf16[8,32,1024]{2,1,0:T(8,128)(2,1)}), bf16[8,32,1024]{2,1,0:T(8,128)(2,1)}, u32[]{:S(2)}, u32[]{:S(2)}) async-start(bf16[8,32,1024]{2,1,0:T(8,128)(2,1)} %broadcast_in_dim.9), calls=%async_computation.2 | async-start | bytes 1048576 | tf_op jit(solution)/shard_map/all_to_all | solution.py:41
  48.2 2.7 %slice.32 = f32[1,128,1024]{2,0,1:T(1,128)S(1)} slice(f32[7,128,1024]{2,0,1:T(8,128)} %copy-done.6), slice={[0:1], [0:128], [0:1024]} | slice | bytes 1048576 | tf_op jit(solution)/shard_map/slice | solution.py:78
  52.6 2.8 %gather_fusion.1 = bf16[512,1024]{1,0:T(8,128)(2,1)} fusion(bf16[512,1024]{1,0:T(8,128)(2,1)S(1)} %bitcast.61, s32[1024]{0:T(1024)S(1)} %pad_clamp_fusion.2), kind=kCustom, calls=%fused_computation.1 | custom fusion | bytes 2099200 | tf_op jit(solution)/shard_map/gather | solution.py:85
  55.3 13.5 %all-to-all-done.1 = bf16[8,32,1024]{2,1,0:T(8,128)(2,1)} async-done(((bf16[8,32,1024]{2,1,0:T(8,128)(2,1)}), bf16[8,32,1024]{2,1,0:T(8,128)(2,1)}, u32[]{:S(2)}, u32[]{:S(2)}) %all-to-all-start.1) | async-done | bytes 524320 | tf_op jit(solution)/shard_map/all_to_all | solution.py:41
  68.8 2.8 %pad_maximum_fusion = bf16[896,1024]{1,0:T(8,128)(2,1)} fusion(bf16[256,1024]{1,0:T(8,128)(2,1)} %bitcast.11, bf16[512,1024]{1,0:T(8,128)(2,1)} %gather_fusion.1, bf16[128,1024]{1,0:T(8,128)(2,1)S(1)} %copy-done.1), kind=kLoop, calls=%fused_computation.12 | loop fusion | flops 5505024 | bytes 3670016 | tf_op jit(solution)/shard_map/concatenate | solution.py:15
  71.6 2.1 gather_fusion.3
  74.9 2.9 %multiply_convert_fusion = (bf16[128,1024]{1,0:T(8,128)(2,1)S(1)}, f32[128,1024]{1,0:T(8,128)}) fusion(bf16[1024,128]{1,0:T(8,128)(2,1)S(1)} %fusion.2, bf16[1024,1024]{1,0:T(8,128)(2,1)} %param.13), kind=kOutput, calls=%fused_computation.22 | convolution fusion | flops 269090816 | bytes 3145728 | tf_op jit(solution)/shard_map/dot_general | solution.py:87
  80.2 3.9 %fusion.6 = f32[1024,1024]{1,0:T(8,128)} fusion(bf16[1024,128]{1,0:T(8,128)(2,1)S(1)} %copy-done.12, f32[128,1024]{1,0:T(8,128)} %get-tuple-element.9, f32[128,1024]{1,0:T(8,128)S(1)} %scatter_fusion), kind=kOutput, calls=%fused_computation.25 | convolution fusion | flops 269615104 | bytes 5505024 | tf_op jit(solution)/shard_map/dot_general | solution.py:23
  85.1 2.8 %gather_fusion.4 = bf16[512,1024]{1,0:T(8,128)(2,1)} fusion(bf16[128,1024]{1,0:T(8,128)(2,1)S(1)} %copy-done.2, s32[1024]{0:T(1024)S(1)} %pad_clamp_fusion.3), kind=kCustom, calls=%fused_computation.4 | custom fusion | bytes 2099200 | tf_op jit(solution)/shard_map/gather | solution.py:83
  87.9 10.2 %all-to-all-start.3 = ((bf16[32,16,1024]{2,1,0:T(8,128)(2,1)}), bf16[32,16,1024]{2,1,0:T(8,128)(2,1)S(1)}, u32[]{:S(2)}, u32[]{:S(2)}) async-start(bf16[32,16,1024]{2,1,0:T(8,128)(2,1)} %bitcast.67), calls=%async_computation.5 | async-start | bytes 2097152 | tf_op jit(solution)/shard_map/all_to_all | solution.py:83
  99.4 15.7 %all-to-all-done.3 = bf16[32,16,1024]{2,1,0:T(8,128)(2,1)S(1)} async-done(((bf16[32,16,1024]{2,1,0:T(8,128)(2,1)}), bf16[32,16,1024]{2,1,0:T(8,128)(2,1)S(1)}, u32[]{:S(2)}, u32[]{:S(2)}) %all-to-all-start.3) | async-done | bytes 1048608 | tf_op jit(solution)/shard_map/all_to_all | solution.py:83
  115.1 1.7 broadcast_in_dim.11
  116.8 4.7 %all-to-all-start.4 = ((bf16[8,32,1024]{2,1,0:T(8,128)(2,1)}), bf16[8,32,1024]{2,1,0:T(8,128)(2,1)}, u32[]{:S(2)}, u32[]{:S(2)}) async-start(bf16[8,32,1024]{2,1,0:T(8,128)(2,1)} %broadcast_in_dim.11), calls=%async_computation.6 | async-start | bytes 1048576 | tf_op jit(solution)/shard_map/all_to_all | solution.py:41
  121.6 2.8 %gather_fusion.5 = bf16[512,1024]{1,0:T(8,128)(2,1)} fusion(bf16[512,1024]{1,0:T(8,128)(2,1)S(1)} %bitcast.62, s32[1024]{0:T(1024)S(1)} %pad_clamp_fusion.2), kind=kCustom, calls=%fused_computation.5 | custom fusion | bytes 2099200 | tf_op jit(solution)/shard_map/gather | solution.py:97
  124.4 20.8 %all-to-all-done.4 = bf16[8,32,1024]{2,1,0:T(8,128)(2,1)} async-done(((bf16[8,32,1024]{2,1,0:T(8,128)(2,1)}), bf16[8,32,1024]{2,1,0:T(8,128)(2,1)}, u32[]{:S(2)}, u32[]{:S(2)}) %all-to-all-start.4) | async-done | bytes 524320 | tf_op jit(solution)/shard_map/all_to_all | solution.py:41
  145.2 2.8 %pad_maximum_fusion.1 = bf16[896,1024]{1,0:T(8,128)(2,1)} fusion(bf16[256,1024]{1,0:T(8,128)(2,1)} %bitcast.17, bf16[512,1024]{1,0:T(8,128)(2,1)} %gather_fusion.5, bf16[128,1024]{1,0:T(8,128)(2,1)S(1)} %get-tuple-element.2), kind=kLoop, calls=%fused_computation.13 | loop fusion | flops 5505024 | bytes 3670016 | tf_op jit(solution)/shard_map/concatenate | solution.py:15
  148.0 2.2 gather_fusion.7
  150.2 3.4 %convolution_bitcast_fusion = f32[1024,1024]{0,1:T(8,128)} fusion(bf16[128,1024]{1,0:T(8,128)(2,1)S(1)} %copy-done.10, bf16[4,128,1024]{2,1,0:T(8,128)(2,1)S(1)} %gather_fusion.7, bf16[1,4,128,128]{3,2,1,0:T(8,128)(2,1)S(1)} %copy-done.8), kind=kOutput, calls=%fused_computation.9 | convolution fusion | flops 402784256 | bytes 5636096 | tf_op jit(solution)/shard_map/dot_general | solution.py:23
  153.6 2.0 reshape.153
  155.6 7.0 %all-to-all-start.2 = ((f32[32,4,1024]{2,1,0:T(4,128)}), f32[32,4,1024]{2,1,0:T(4,128)S(1)}, u32[]{:S(2)}, u32[]{:S(2)}) async-start(f32[32,4,1024]{2,1,0:T(4,128)} %reshape.153), calls=%async_computation.4 | async-start | bytes 1048576 | tf_op jit(solution)/shard_map/all_to_all | solution.py:32
  162.6 46.8 %reduce-scatter.8.cloned.1.call-done = f32[128,1024]{0,1:T(8,128)} async-done(((f32[1024,1024]{0,1:T(8,128)}), f32[128,1024]{0,1:T(8,128)}) %reduce-scatter.8.cloned.1.call-update) | async-done | bytes 524304 | tf_op jit(solution)/shard_map/reduce_scatter | solution.py:31
  209.4 2.0 copy.17
  211.4 2.0 reshape.158
  213.4 7.6 %all-to-all-start.5 = ((f32[32,4,1024]{2,1,0:T(4,128)}), f32[32,4,1024]{2,1,0:T(4,128)}, u32[]{:S(2)}, u32[]{:S(2)}) async-start(f32[32,4,1024]{2,1,0:T(4,128)} %reshape.158), calls=%async_computation.8 | async-start | bytes 1048576 | tf_op jit(solution)/shard_map/all_to_all | solution.py:32
  222.5 10.2 %all-to-all-done.5 = f32[32,4,1024]{2,1,0:T(4,128)} async-done(((f32[32,4,1024]{2,1,0:T(4,128)}), f32[32,4,1024]{2,1,0:T(4,128)}, u32[]{:S(2)}, u32[]{:S(2)}) %all-to-all-start.5) | async-done | bytes 524320 | tf_op jit(solution)/shard_map/all_to_all | solution.py:32
  (67 shorter events, 16.6 us)
Async XLA Ops:
  7.2 14.3 %copy-start = (bf16[1024,1024]{1,0:T(8,128)(2,1)S(1)}, bf16[1024,1024]{1,0:T(8,128)(2,1)}, u32[]{:S(2)}) copy-start(bf16[1024,1024]{1,0:T(8,128)(2,1)} %param.14) | copy-start | bytes 6291460
  12.7 8.8 %copy-start.8 = (bf16[1,4,128,128]{3,2,1,0:T(8,128)(2,1)S(1)}, bf16[1,4,128,128]{3,2,1,0:T(8,128)(2,1)}, u32[]{:S(2)}) copy-start(bf16[1,4,128,128]{3,2,1,0:T(8,128)(2,1)} %param.19) | copy-start | bytes 393220
  12.7 8.8 %copy-start.9 = (bf16[128,1024]{1,0:T(8,128)(2,1)S(1)}, bf16[128,1024]{1,0:T(8,128)(2,1)}, u32[]{:S(2)}) copy-start(bf16[128,1024]{1,0:T(8,128)(2,1)} %param.12) | copy-start | bytes 786436
  12.7 25.6 %all-to-all-start = ((bf16[32,16,1024]{2,1,0:T(8,128)(2,1)}), bf16[32,16,1024]{2,1,0:T(8,128)(2,1)S(1)}, u32[]{:S(2)}, u32[]{:S(2)}) async-start(bf16[32,16,1024]{2,1,0:T(8,128)(2,1)} %bitcast.66), calls=%async_computation.1 | async-start | bytes 2097152 | tf_op jit(solution)/shard_map/all_to_all | solution.py:82
  21.4 57.4 %reduce-scatter.4.cloned.1.call-start = ((), (), s32[]{:S(2)}) async-start(), calls=%async_computation.9 | async-start | bytes 1179648 | tf_op jit(solution)/shard_map/reduce_scatter | solution.py:79
  23.9 3.1 %copy-start.16 = (s32[1,4]{1,0:T(1,128)S(1)}, s32[1,4]{1,0:T(1,128)}, u32[]{:S(2)}) copy-start(s32[1,4]{1,0:T(1,128)} %param.18) | copy-start | bytes 52
  31.2 1.9 copy-start.6
  33.8 1.4 copy-start.17
  33.8 1.4 copy-start.1
  35.2 16.7 %copy-start.13 = (s32[32]{0:T(128)}, s32[32]{0:T(128)S(1)}, u32[]{:S(2)}) copy-start(s32[32]{0:T(128)S(1)} %fusion.15) | copy-start | bytes 388
  35.2 16.7 %copy-start.15 = (s32[512]{0:T(512)S(1)}, s32[512]{0:T(512)}, u32[]{:S(2)}) copy-start(s32[512]{0:T(512)} %param.16) | copy-start | bytes 6148
  40.0 28.8 %all-to-all-start.1 = ((bf16[8,32,1024]{2,1,0:T(8,128)(2,1)}), bf16[8,32,1024]{2,1,0:T(8,128)(2,1)}, u32[]{:S(2)}, u32[]{:S(2)}) async-start(bf16[8,32,1024]{2,1,0:T(8,128)(2,1)} %broadcast_in_dim.9), calls=%async_computation.2 | async-start | bytes 1048576 | tf_op jit(solution)/shard_map/all_to_all | solution.py:41
  48.2 105.4 %reduce-scatter.6.cloned.1.call-start = ((), (), s32[]{:S(2)}) async-start(), calls=%async_computation.10 | async-start | bytes 4718592 | tf_op jit(solution)/shard_map/reduce_scatter | solution.py:31
  74.2 0.7 copy-start.11
  74.9 3.8 %copy-start.3 = (f32[1,128,1024]{2,1,0:T(8,128)S(1)}, f32[1,128,1024]{2,1,0:T(8,128)}, u32[]{:S(2)}) copy-start(f32[1,128,1024]{2,1,0:T(8,128)} %copy.22) | copy-start | bytes 1572868
  74.9 3.8 %copy-start.14 = (s32[32]{0:T(128)S(1)}, s32[32]{0:T(128)}, u32[]{:S(2)}) copy-start(s32[32]{0:T(128)} %copy-done.13) | copy-start | bytes 388
  77.9 67.3 %copy-start.7 = (bf16[128,1024]{1,0:T(8,128)(2,1)}, bf16[128,1024]{1,0:T(8,128)(2,1)S(1)}, u32[]{:S(2)}) copy-start(bf16[128,1024]{1,0:T(8,128)(2,1)S(1)} %get-tuple-element.2) | copy-start | bytes 786436
  77.9 2.4 copy-start.12
  80.2 4.0 %copy-start.4 = (f32[128,1024]{1,0:T(8,128)}, f32[128,1024]{1,0:T(8,128)S(1)}, u32[]{:S(2)}) copy-start(f32[128,1024]{1,0:T(8,128)S(1)} %scatter_fusion) | copy-start | bytes 1572868
  84.2 1.0 copy-start.2
  87.9 27.2 %all-to-all-start.3 = ((bf16[32,16,1024]{2,1,0:T(8,128)(2,1)}), bf16[32,16,1024]{2,1,0:T(8,128)(2,1)S(1)}, u32[]{:S(2)}, u32[]{:S(2)}) async-start(bf16[32,16,1024]{2,1,0:T(8,128)(2,1)} %bitcast.67), calls=%async_computation.5 | async-start | bytes 2097152 | tf_op jit(solution)/shard_map/all_to_all | solution.py:83
  116.8 28.4 %all-to-all-start.4 = ((bf16[8,32,1024]{2,1,0:T(8,128)(2,1)}), bf16[8,32,1024]{2,1,0:T(8,128)(2,1)}, u32[]{:S(2)}, u32[]{:S(2)}) async-start(bf16[8,32,1024]{2,1,0:T(8,128)(2,1)} %broadcast_in_dim.11), calls=%async_computation.6 | async-start | bytes 1048576 | tf_op jit(solution)/shard_map/all_to_all | solution.py:41
  121.5 87.9 %reduce-scatter.8.cloned.1.call-start = ((), (), s32[]{:S(2)}) async-start(), calls=%async_computation.11 | async-start | bytes 4718592 | tf_op jit(solution)/shard_map/reduce_scatter | solution.py:31
  148.0 2.2 copy-start.10
  155.6 65.5 %copy-start.5 = (f32[128,1024]{1,0:T(8,128)S(1)}, f32[128,1024]{1,0:T(8,128)}, u32[]{:S(2)}) copy-start(f32[128,1024]{1,0:T(8,128)} %copy-done.4) | copy-start | bytes 1572868
  155.6 57.8 %all-to-all-start.2 = ((f32[32,4,1024]{2,1,0:T(4,128)}), f32[32,4,1024]{2,1,0:T(4,128)S(1)}, u32[]{:S(2)}, u32[]{:S(2)}) async-start(f32[32,4,1024]{2,1,0:T(4,128)} %reshape.153), calls=%async_computation.4 | async-start | bytes 1048576 | tf_op jit(solution)/shard_map/all_to_all | solution.py:32
  213.4 19.3 %all-to-all-start.5 = ((f32[32,4,1024]{2,1,0:T(4,128)}), f32[32,4,1024]{2,1,0:T(4,128)}, u32[]{:S(2)}, u32[]{:S(2)}) async-start(f32[32,4,1024]{2,1,0:T(4,128)} %reshape.158), calls=%async_computation.8 | async-start | bytes 1048576 | tf_op jit(solution)/shard_map/all_to_all | solution.py:32
Sparse Core Ops, SparseCore 0:
  35.3 43.4 reduce-scatter.3
  84.3 68.4 reduce-scatter.5
  155.4 53.9 reduce-scatter.7

commit v2 on v1

--- a/solution.py
+++ b/solution.py
@@ -27,11 +27,19 @@
 
 def reduce_weight(product, rows_per_device):
     factor = 1.0 / math.sqrt(rows_per_device * lax.axis_size("group") * lax.axis_size("dom"))
+    n_group = lax.axis_size("group")
     n_dom = lax.axis_size("dom")
-    in_group = lax.psum_scatter(product, "group", scatter_dimension=0, tiled=True)
-    pieces = lax.all_to_all(
-        in_group.reshape(n_dom, -1, in_group.shape[1]), "dom", split_axis=0, concat_axis=0, tiled=True
-    )
+    width = product.shape[1]
+    blocks = product.reshape(n_group, n_dom // 2, 2, -1, width)
+    core = lax.axis_index("dom") % 2
+    keep = lax.dynamic_index_in_dim(blocks, core, axis=2, keepdims=False)
+    give = lax.dynamic_index_in_dim(blocks, 1 - core, axis=2, keepdims=False)
+    pair = keep + lax.ppermute(give, "dom", [(i, i ^ 1) for i in range(n_dom)])
+    in_group = lax.psum_scatter(pair, "group", scatter_dimension=0, tiled=True)
+    chunks = in_group.reshape(n_dom // 2, 1, -1, width)
+    slot = jnp.arange(2, dtype=jnp.int32)[None, :, None, None] == core
+    outgoing = jnp.where(slot, chunks, 0.0).reshape(n_dom, -1, width)
+    pieces = lax.all_to_all(outgoing, "dom", split_axis=0, concat_axis=0, tiled=True)
     return pieces.sum(axis=0) * factor
 
 
@@ -79,8 +87,11 @@
     hub_grad = lax.psum_scatter(spread[V_DEV + HALO :], "group", scatter_dimension=0, tiled=True)
     vertex_grad = own_grad.at[owned_hubs].add(hub_grad)
 
-    feat_slots = lax.all_to_all(feats[routes], "dom", split_axis=0, concat_axis=0, tiled=True)
-    hist_slots = lax.all_to_all(history[routes], "dom", split_axis=0, concat_axis=0, tiled=True)
+    both_slots = lax.all_to_all(
+        jnp.stack([feats[routes], history[routes]], axis=1), "dom", split_axis=0, concat_axis=0, tiled=True
+    )
+    feat_slots = both_slots[:, 0]
+    hist_slots = both_slots[:, 1]
     hub_first = gather_hubs(feats[owned_hubs])
     feat_halo = feat_slots.reshape(-1, D)[halo_index]
     agg_first = combine_tiles(feats, feat_halo, hub_first, tile_cols, tile_vals)

time: 242 us -> 272 us (1.12)
  blocking collectives: 0 us -> 23.7 us
  starting transfers between devices: 46.6 us -> 29 us
  local copies, waits for them, and re-layouts: 41.5 us -> 51.3 us
  waiting for transfers between devices: 110 us -> 119 us
  other arithmetic: 11.8 us -> 18.8 us
    all_to_all x0 -> x1, blocking collectives: none -> 23.7 us  [reduce_weight(): lax.all_to_all(outgoing, 'dom', split_axis=0, concat_axis=0, tiled=True)]
    all_to_all x4 -> x2, starting transfers between devices: 33.6 us -> 12.4 us  [the longest x1 8.76 us: on_device(): lax.all_to_all(jnp.stack([feats[routes], history[routes]], axis=1), 'dom'...]
    reduce_scatter x2, waiting for transfers between devices: 46.8 us -> 65.5 us  [reduce_weight(): in_group = lax.psum_scatter(pair, 'group', scatter_dimension=0, tiled=True)]
    all_to_all x2, waiting for transfers between devices: 34.3 us -> 20.5 us  [gather_hubs(): lax.all_to_all(copies, 'group', split_axis=0, concat_axis=0, tiled=True)]
    dynamic_slice x0 -> x3, local copies, waits for them, and re-layouts: none -> 11.3 us  [the longest x1 7.34 us: reduce_weight(): keep = lax.dynamic_index_in_dim(blocks, core, axis=2, keepdims=False)]
    ppermute x0 -> x2, waiting for transfers between devices: none -> 7.57 us  [reduce_weight(): pair = keep + lax.ppermute(give, 'dom', [(i, i ^ 1) for i in range(n_dom)])]
    reshape x2, local copies, waits for them, and re-layouts: 3.98 us -> 10.4 us  [reduce_weight(): blocks = product.reshape(n_group, n_dom // 2, 2, -1, width)]
    add x0 -> x2, other arithmetic: none -> 5.37 us  [reduce_weight(): pair = keep + lax.ppermute(give, 'dom', [(i, i ^ 1) for i in range(n_dom)])]
  transfers between devices with their start and end apart: 9 -> 9, of which waited for: 7 -> 8; matrix products, arithmetic and copies ran while one was open for 23% -> 15% of each run, Pallas kernels for 0% -> 0%
where the time goes in v2:
time: 272 us; the launch traced here: 271 us
  waiting for transfers between devices  119 us (44%)
  local copies, waits for them, and re-layouts  51.3 us (19%)
  starting transfers between devices  29 us (11%)
  blocking collectives  23.7 us (9%)
  other arithmetic  18.8 us (7%)
  matrix products  15.2 us (6%)
  between operations  14.1 us (5%)
    reduce_scatter x2, waiting for transfers between devices, reduce_weight(): in_group = lax.psum_scatter(pair, 'group', scatter_dimension=0, tiled=True)  65.5 us
    all_to_all x1, blocking collectives, reduce_weight(): lax.all_to_all(outgoing, 'dom', split_axis=0, concat_axis=0, tiled=True)  23.7 us
    all_to_all x2, waiting for transfers between devices, gather_hubs(): lax.all_to_all(copies, 'group', split_axis=0, concat_axis=0, tiled=True)  20.5 us
    all_to_all x1, waiting for transfers between devices, on_device(): lax.all_to_all(jnp.stack([feats[routes], history[routes]], axis=1), 'dom'...  15.9 us
    all_to_all x2, starting transfers between devices, gather_hubs(): lax.all_to_all(copies, 'group', split_axis=0, concat_axis=0, tiled=True)  12 us
    reshape x2, local copies, waits for them, and re-layouts, reduce_weight(): blocks = product.reshape(n_group, n_dom // 2, 2, -1, width)  10.4 us
    all_to_all x1, waiting for transfers between devices, reduce_weight(): lax.all_to_all(outgoing, 'dom', split_axis=0, concat_axis=0, tiled=True)  9.05 us
    all_to_all x1, starting transfers between devices, on_device(): lax.all_to_all(jnp.stack([feats[routes], history[routes]], axis=1), 'dom'...  8.76 us
  transfers between devices with their start and end apart: 9, of which 8 were waited for; matrix products, arithmetic and copies ran while one was open for 15% of the time, Pallas kernels for 0%

profile of v2, /device:TPU:1, one launch (start us, length us, event | category | flops | bytes accessed | tf_op | source)
XLA Modules:
  0.0 270.7 jit_solution(11055073765685417833)
XLA Ops:
  8.2 3.8 %gather_fusion.1 = bf16[512,1024]{1,0:T(8,128)(2,1)S(1)} fusion(bf16[128,1024]{1,0:T(8,128)(2,1)} %param.11, s32[1024]{0:T(1024)S(1)} %pad_clamp_fusion.3), kind=kCustom, calls=%fused_computation.1 | custom fusion | bytes 2099200 | tf_op jit(solution)/shard_map/gather | solution.py:91
  12.0 2.8 %gather_fusion = bf16[512,1024]{1,0:T(8,128)(2,1)} fusion(bf16[128,1024]{1,0:T(8,128)(2,1)S(1)} %copy-done.2, s32[1024]{0:T(1024)S(1)} %pad_clamp_fusion.3), kind=kCustom, calls=%fused_computation | custom fusion | bytes 2099200 | tf_op jit(solution)/shard_map/gather | solution.py:91
  14.8 2.8 %pad_maximum_fusion = bf16[32,2,16,1024]{3,2,1,0:T(8,128)(2,1)} fusion(bf16[32,1,16,1024]{3,2,1,0:T(8,128)(2,1)S(1)} %bitcast.87, bf16[32,1,16,1024]{3,2,1,0:T(8,128)(2,1)} %bitcast.88), kind=kLoop, calls=%fused_computation.10 | loop fusion | flops 1048576 | bytes 4194304 | tf_op jit(solution)/shard_map/stack | solution.py:91
  17.6 8.8 %all-to-all-start = ((bf16[32,2,16,1024]{3,2,1,0:T(8,128)(2,1)}), bf16[32,2,16,1024]{3,2,1,0:T(8,128)(2,1)}, u32[]{:S(2)}, u32[]{:S(2)}) async-start(bf16[32,2,16,1024]{3,2,1,0:T(8,128)(2,1)} %pad_maximum_fusion), calls=%async_computation.1 | async-start | bytes 4194304 | tf_op jit(solution)/shard_map/all_to_all | solution.py:90
  26.4 2.5 convolution_bitcast_fusion.1
  28.9 2.4 copy.57
  31.3 2.7 fusion.10
  38.8 15.9 %all-to-all-done = bf16[32,2,16,1024]{3,2,1,0:T(8,128)(2,1)} async-done(((bf16[32,2,16,1024]{3,2,1,0:T(8,128)(2,1)}), bf16[32,2,16,1024]{3,2,1,0:T(8,128)(2,1)}, u32[]{:S(2)}, u32[]{:S(2)}) %all-to-all-start) | async-done | bytes 2097184 | tf_op jit(solution)/shard_map/all_to_all | solution.py:90
  55.6 8.2 %all-to-all-start.1 = ((bf16[8,32,1024]{2,1,0:T(8,128)(2,1)}), bf16[8,32,1024]{2,1,0:T(8,128)(2,1)S(1)}, u32[]{:S(2)}, u32[]{:S(2)}) async-start(bf16[8,32,1024]{2,1,0:T(8,128)(2,1)} %broadcast_in_dim.71), calls=%async_computation.2 | async-start | bytes 1048576 | tf_op jit(solution)/shard_map/all_to_all | solution.py:49
  65.7 2.8 %gather_fusion.2 = bf16[512,1024]{1,0:T(8,128)(2,1)} fusion(bf16[512,1024]{1,0:T(8,128)(2,1)S(1)} %bitcast.82, s32[1024]{0:T(1024)S(1)} %pad_clamp_fusion.2), kind=kCustom, calls=%fused_computation.2 | custom fusion | bytes 2099200 | tf_op jit(solution)/shard_map/gather | solution.py:96
  68.5 13.8 %all-to-all-done.1 = bf16[8,32,1024]{2,1,0:T(8,128)(2,1)S(1)} async-done(((bf16[8,32,1024]{2,1,0:T(8,128)(2,1)}), bf16[8,32,1024]{2,1,0:T(8,128)(2,1)S(1)}, u32[]{:S(2)}, u32[]{:S(2)}) %all-to-all-start.1) | async-done | bytes 524320 | tf_op jit(solution)/shard_map/all_to_all | solution.py:49
  82.2 2.6 pad_maximum_fusion.1
  87.5 2.1 multiply_convert_fusion
  91.1 2.8 %fusion.3 = f32[1024,1024]{1,0:T(8,128)} fusion(bf16[1024,128]{1,0:T(8,128)(2,1)S(1)} %fusion, f32[128,1024]{1,0:T(8,128)S(1)} %get-tuple-element.17, f32[128,1024]{1,0:T(8,128)S(1)} %scatter_fusion), kind=kOutput, calls=%fused_computation.30 | convolution fusion | flops 269615104 | bytes 5505024 | tf_op jit(solution)/shard_map/dot_general | solution.py:23
  95.3 3.9 %all-to-all-start.3 = ((bf16[8,32,1024]{2,1,0:T(8,128)(2,1)}), bf16[8,32,1024]{2,1,0:T(8,128)(2,1)S(1)}, u32[]{:S(2)}, u32[]{:S(2)}) async-start(bf16[8,32,1024]{2,1,0:T(8,128)(2,1)} %broadcast_in_dim.80), calls=%async_computation.5 | async-start | bytes 1048576 | tf_op jit(solution)/shard_map/all_to_all | solution.py:49
  99.5 2.8 %gather_fusion.5 = bf16[512,1024]{1,0:T(8,128)(2,1)} fusion(bf16[512,1024]{1,0:T(8,128)(2,1)S(1)} %bitcast.81, s32[1024]{0:T(1024)S(1)} %pad_clamp_fusion.2), kind=kCustom, calls=%fused_computation.5 | custom fusion | bytes 2099200 | tf_op jit(solution)/shard_map/gather | solution.py:108
  102.2 5.2 %reshape.161 = f32[8,16,2,4,1024]{4,3,2,1,0:T(4,128)} reshape(f32[1024,1024]{1,0:T(8,128)} %fusion.3) | data formatting | bytes 8388608 | tf_op jit(solution)/shard_map/reshape | solution.py:33
  107.4 6.8 %all-to-all-done.3 = bf16[8,32,1024]{2,1,0:T(8,128)(2,1)S(1)} async-done(((bf16[8,32,1024]{2,1,0:T(8,128)(2,1)}), bf16[8,32,1024]{2,1,0:T(8,128)(2,1)S(1)}, u32[]{:S(2)}, u32[]{:S(2)}) %all-to-all-start.3) | async-done | bytes 524320 | tf_op jit(solution)/shard_map/all_to_all | solution.py:49
  117.2 4.6 %convolution_bitcast_fusion = f32[1024,1024]{1,0:T(8,128)} fusion(bf16[128,1024]{1,0:T(8,128)(2,1)S(1)} %copy-done.7, bf16[4,128,1024]{2,1,0:T(8,128)(2,1)} %gather_fusion.7, bf16[1,4,128,128]{3,2,1,0:T(8,128)(2,1)S(1)} %copy-done.5), kind=kOutput, calls=%fused_computation.9 | convolution fusion | flops 402784256 | bytes 5636096 | tf_op jit(solution)/shard_map/dot_general | solution.py:23
  121.8 5.2 %reshape.165 = f32[8,16,2,4,1024]{4,3,2,1,0:T(4,128)} reshape(f32[1024,1024]{1,0:T(8,128)} %convolution_bitcast_fusion) | data formatting | bytes 8388608 | tf_op jit(solution)/shard_map/reshape | solution.py:33
  127.1 7.3 %constant_dynamic-slice_fusion.1 = (f32[8,16,1,4,1024]{4,3,2,1,0:T(4,128)S(1)}, f32[8,16,1,4,1024]{4,3,2,1,0:T(4,128)}, f32[8,16,1,4,1024]{4,3,2,1,0:T(4,128)S(1)}, f32[8,16,1,4,1024]{4,3,2,1,0:T(4,128)S(1)}) fusion(f32[8,16,2,4,1024]{4,3,2,1,0:T(4,128)} %reshape.165, s32[]{:T(128)S(6)} %select_n.63, s32[]{:T(128)S(6)} %select_n.64, ...), kind=kLoop, calls=%fused_computation.49 | loop fusion | bytes 16777224 | tf_op jit(solution)/shard_map/jit(dynamic_index_in_dim)/dynamic_slice | solution.py:35
  135.6 3.5 %collective-permute-start = (f32[8,16,4,1024]{3,1,2,0:T(8,128)S(1)}, f32[8,16,4,1024]{3,1,2,0:T(8,128)S(1)}, u32[]{:S(2)}, u32[]{:S(2)}) collective-permute-start(f32[8,16,4,1024]{3,1,2,0:T(8,128)S(1)} %bitcast.91), channel_id=1, source_target_pairs={{0,1},{1,0},{2,3},{3,2},{4,5},{5,4},{6,7},{7,6},{8,9},{9,8},{10,11... | collective-permute-start | bytes 6291464 | tf_op jit(solution)/shard_map/ppermute | solution.py:37
  139.1 3.8 %collective-permute-done = f32[8,16,4,1024]{3,1,2,0:T(8,128)S(1)} collective-permute-done((f32[8,16,4,1024]{3,1,2,0:T(8,128)S(1)}, f32[8,16,4,1024]{3,1,2,0:T(8,128)S(1)}, u32[]{:S(2)}, u32[]{:S(2)}) %collective-permute-start) | collective-permute-done | bytes 2097184 | tf_op jit(solution)/shard_map/ppermute | solution.py:37
  142.9 2.7 bitcast_add_fusion.1
  145.7 2.8 %copy.84 = f32[8,16,1,4,1024]{4,1,3,0,2:T(8,128)S(1)} copy(f32[8,16,1,4,1024]{4,3,2,1,0:T(4,128)} %get-tuple-element.9) | data formatting | bytes 4194304 | tf_op jit(solution)/shard_map/jit(dynamic_index_in_dim)/dynamic_slice | solution.py:36
  149.1 3.8 %collective-permute-done.1 = f32[8,16,4,1024]{3,1,2,0:T(8,128)S(1)} collective-permute-done((f32[8,16,4,1024]{3,1,2,0:T(8,128)S(1)}, f32[8,16,4,1024]{3,1,2,0:T(8,128)S(1)}, u32[]{:S(2)}, u32[]{:S(2)}) %collective-permute-start.1) | collective-permute-done | bytes 2097184 | tf_op jit(solution)/shard_map/ppermute | solution.py:37
  152.9 2.7 %bitcast_add_fusion = f32[8,16,4,1024]{3,1,2,0:T(8,128)} fusion(f32[8,16,4,1024]{3,1,2,0:T(8,128)S(1)} %collective-permute-done.1, f32[8,16,1,4,1024]{4,3,2,1,0:T(4,128)S(1)} %get-tuple-element.8), kind=kLoop, calls=%fused_computation.11 | loop fusion | flops 524288 | bytes 6291456 | tf_op jit(solution)/shard_map/add | solution.py:37
  155.8 22.6 %reduce-scatter.6.cloned.1.call-done = f32[1,16,4,1024]{3,1,2,0:T(8,128)} async-done(((f32[8,16,4,1024]{3,1,2,0:T(8,128)}), f32[1,16,4,1024]{3,1,2,0:T(8,128)}) %reduce-scatter.6.cloned.1.call-update) | async-done | bytes 262160 | tf_op jit(solution)/shard_map/reduce_scatter | solution.py:38
  179.5 42.8 %reduce-scatter.8.cloned.1.call-done = f32[1,16,4,1024]{3,1,2,0:T(8,128)} async-done(((f32[8,16,4,1024]{3,1,2,0:T(8,128)}), f32[1,16,4,1024]{3,1,2,0:T(8,128)}) %reduce-scatter.8.cloned.1.call-update) | async-done | bytes 262160 | tf_op jit(solution)/shard_map/reduce_scatter | solution.py:38
  224.6 23.7 %all_to_all.25 = f32[32,4,1024]{2,1,0:T(4,128)} all-to-all(f32[32,4,1024]{2,1,0:T(4,128)S(1)} %get-tuple-element.14), channel_id=1, replica_groups=mesh['group'=8,'dom'=32] {'dom'}, dimensions={0} | all-to-all | bytes 1048576 | tf_op jit(solution)/shard_map/all_to_all | solution.py:42
  248.3 3.7 %all-to-all-start.2 = ((f32[32,4,1024]{2,1,0:T(4,128)}), f32[32,4,1024]{2,1,0:T(4,128)S(1)}, u32[]{:S(2)}, u32[]{:S(2)}) async-start(f32[32,4,1024]{2,1,0:T(4,128)} %get-tuple-element.15), calls=%async_computation.4 | async-start | bytes 1048576 | tf_op jit(solution)/shard_map/all_to_all | solution.py:42
  254.4 9.1 %all-to-all-done.2 = f32[32,4,1024]{2,1,0:T(4,128)S(1)} async-done(((f32[32,4,1024]{2,1,0:T(4,128)}), f32[32,4,1024]{2,1,0:T(4,128)S(1)}, u32[]{:S(2)}, u32[]{:S(2)}) %all-to-all-start.2) | async-done | bytes 524320 | tf_op jit(solution)/shard_map/all_to_all | solution.py:42
  (67 shorter events, 25.8 us)
Async XLA Ops:
  7.2 19.2 %copy-start = (bf16[1024,1024]{1,0:T(8,128)(2,1)S(1)}, bf16[1024,1024]{1,0:T(8,128)(2,1)}, u32[]{:S(2)}) copy-start(bf16[1024,1024]{1,0:T(8,128)(2,1)} %param.14) | copy-start | bytes 6291460
  8.2 3.8 %copy-start.2 = (bf16[128,1024]{1,0:T(8,128)(2,1)S(1)}, bf16[128,1024]{1,0:T(8,128)(2,1)}, u32[]{:S(2)}) copy-start(bf16[128,1024]{1,0:T(8,128)(2,1)} %param.10) | copy-start | bytes 786436
  17.6 8.8 %copy-start.5 = (bf16[1,4,128,128]{3,2,1,0:T(8,128)(2,1)S(1)}, bf16[1,4,128,128]{3,2,1,0:T(8,128)(2,1)}, u32[]{:S(2)}) copy-start(bf16[1,4,128,128]{3,2,1,0:T(8,128)(2,1)} %param.19) | copy-start | bytes 393220
  17.6 8.8 %copy-start.6 = (bf16[128,1024]{1,0:T(8,128)(2,1)S(1)}, bf16[128,1024]{1,0:T(8,128)(2,1)}, u32[]{:S(2)}) copy-start(bf16[128,1024]{1,0:T(8,128)(2,1)} %param.12) | copy-start | bytes 786436
  17.6 37.2 %all-to-all-start = ((bf16[32,2,16,1024]{3,2,1,0:T(8,128)(2,1)}), bf16[32,2,16,1024]{3,2,1,0:T(8,128)(2,1)}, u32[]{:S(2)}, u32[]{:S(2)}) async-start(bf16[32,2,16,1024]{3,2,1,0:T(8,128)(2,1)} %pad_maximum_fusion), calls=%async_computation.1 | async-start | bytes 4194304 | tf_op jit(solution)/shard_map/all_to_all | solution.py:90
  26.3 63.3 %reduce-scatter.4.cloned.1.call-start = ((), (), s32[]{:S(2)}) async-start(), calls=%async_computation.8 | async-start | bytes 1179648 | tf_op jit(solution)/shard_map/reduce_scatter | solution.py:87
  28.9 2.4 copy-start.9
  34.0 2.0 copy-start.3
  36.6 1.4 copy-start.10
  36.6 2.1 slice-start
  38.0 25.8 %copy-start.8 = (s32[512]{0:T(512)S(1)}, s32[512]{0:T(512)}, u32[]{:S(2)}) copy-start(s32[512]{0:T(512)} %param.16) | copy-start | bytes 6148
  55.6 26.6 %all-to-all-start.1 = ((bf16[8,32,1024]{2,1,0:T(8,128)(2,1)}), bf16[8,32,1024]{2,1,0:T(8,128)(2,1)S(1)}, u32[]{:S(2)}, u32[]{:S(2)}) async-start(bf16[8,32,1024]{2,1,0:T(8,128)(2,1)} %broadcast_in_dim.71), calls=%async_computation.2 | async-start | bytes 1048576 | tf_op jit(solution)/shard_map/all_to_all | solution.py:49
  89.6 24.6 %copy-start.4 = (bf16[128,1024]{1,0:T(8,128)(2,1)}, bf16[128,1024]{1,0:T(8,128)(2,1)S(1)}, u32[]{:S(2)}) copy-start(bf16[128,1024]{1,0:T(8,128)(2,1)S(1)} %get-tuple-element.2) | copy-start | bytes 786436
  95.3 18.9 %all-to-all-start.3 = ((bf16[8,32,1024]{2,1,0:T(8,128)(2,1)}), bf16[8,32,1024]{2,1,0:T(8,128)(2,1)S(1)}, u32[]{:S(2)}, u32[]{:S(2)}) async-start(bf16[8,32,1024]{2,1,0:T(8,128)(2,1)} %broadcast_in_dim.80), calls=%async_computation.5 | async-start | bytes 1048576 | tf_op jit(solution)/shard_map/all_to_all | solution.py:49
  99.2 79.2 %reduce-scatter.6.cloned.1.call-start = ((), (), s32[]{:S(2)}) async-start(), calls=%async_computation.9 | async-start | bytes 2359296 | tf_op jit(solution)/shard_map/reduce_scatter | solution.py:38
  114.2 3.0 %copy-start.7 = (bf16[128,1024]{1,0:T(8,128)(2,1)S(1)}, bf16[128,1024]{1,0:T(8,128)(2,1)}, u32[]{:S(2)}) copy-start(bf16[128,1024]{1,0:T(8,128)(2,1)} %param.12) | copy-start | bytes 786436
  135.6 7.3 %collective-permute-start = (f32[8,16,4,1024]{3,1,2,0:T(8,128)S(1)}, f32[8,16,4,1024]{3,1,2,0:T(8,128)S(1)}, u32[]{:S(2)}, u32[]{:S(2)}) collective-permute-start(f32[8,16,4,1024]{3,1,2,0:T(8,128)S(1)} %bitcast.91), channel_id=1, source_target_pairs={{0,1},{1,0},{2,3},{3,2},{4,5},{5,4},{6,7},{7,6},{8,9},{9,8},{10,11... | collective-permute-start | bytes 6291464 | tf_op jit(solution)/shard_map/ppermute | solution.py:37
  145.6 76.8 %reduce-scatter.8.cloned.1.call-start = ((), (), s32[]{:S(2)}) async-start(), calls=%async_computation.10 | async-start | bytes 2359296 | tf_op jit(solution)/shard_map/reduce_scatter | solution.py:38
  148.5 4.5 %collective-permute-start.1 = (f32[8,16,4,1024]{3,1,2,0:T(8,128)S(1)}, f32[8,16,4,1024]{3,1,2,0:T(8,128)S(1)}, u32[]{:S(2)}, u32[]{:S(2)}) collective-permute-start(f32[8,16,4,1024]{3,1,2,0:T(8,128)S(1)} %bitcast.92), channel_id=1, source_target_pairs={{0,1},{1,0},{2,3},{3,2},{4,5},{5,4},{6,7},{7,6},{8,9},{9,8},{10,11... | collective-permute-start | bytes 6291464 | tf_op jit(solution)/shard_map/ppermute | solution.py:37
  223.5 40.7 %copy-start.1 = (bf16[1024,1024]{1,0:T(8,128)(2,1)S(1)}, bf16[1024,1024]{1,0:T(8,128)(2,1)}, u32[]{:S(2)}) copy-start(bf16[1024,1024]{1,0:T(8,128)(2,1)} %param.14) | copy-start | bytes 6291460
  248.3 15.2 %all-to-all-start.2 = ((f32[32,4,1024]{2,1,0:T(4,128)}), f32[32,4,1024]{2,1,0:T(4,128)S(1)}, u32[]{:S(2)}, u32[]{:S(2)}) async-start(f32[32,4,1024]{2,1,0:T(4,128)} %get-tuple-element.15), calls=%async_computation.4 | async-start | bytes 1048576 | tf_op jit(solution)/shard_map/all_to_all | solution.py:42
Sparse Core Ops, SparseCore 0:
  38.1 41.3 reduce-scatter.3
  145.7 32.6 reduce-scatter.5
  181.0 41.3 reduce-scatter.7

commit v3 on v2

--- a/solution.py
+++ b/solution.py
@@ -25,17 +25,25 @@
     )
 
 
-def reduce_weight(product, rows_per_device):
+def pair_product(left_rows, right_rows):
+    n_group = lax.axis_size("group")
+    n_dom = lax.axis_size("dom")
+    core = lax.axis_index("dom") % 2
+    columns = left_rows.reshape(left_rows.shape[0], n_group, n_dom // 2, 2, -1)
+    keep = lax.dynamic_index_in_dim(columns, core, axis=3, keepdims=False)
+    give = lax.dynamic_index_in_dim(columns, 1 - core, axis=3, keepdims=False)
+    kept = weight_product(keep.reshape(left_rows.shape[0], -1), right_rows)
+    sent = weight_product(give.reshape(left_rows.shape[0], -1), right_rows)
+    return kept + lax.ppermute(sent, "dom", [(i, i ^ 1) for i in range(n_dom)])
+
+
+def reduce_weight(pair, rows_per_device):
     factor = 1.0 / math.sqrt(rows_per_device * lax.axis_size("group") * lax.axis_size("dom"))
     n_group = lax.axis_size("group")
     n_dom = lax.axis_size("dom")
-    width = product.shape[1]
-    blocks = product.reshape(n_group, n_dom // 2, 2, -1, width)
+    width = pair.shape[1]
     core = lax.axis_index("dom") % 2
-    keep = lax.dynamic_index_in_dim(blocks, core, axis=2, keepdims=False)
-    give = lax.dynamic_index_in_dim(blocks, 1 - core, axis=2, keepdims=False)
-    pair = keep + lax.ppermute(give, "dom", [(i, i ^ 1) for i in range(n_dom)])
-    in_group = lax.psum_scatter(pair, "group", scatter_dimension=0, tiled=True)
+    in_group = lax.psum_scatter(pair.reshape(n_group, -1, width), "group", scatter_dimension=0, tiled=True)
     chunks = in_group.reshape(n_dom // 2, 1, -1, width)
     slot = jnp.arange(2, dtype=jnp.int32)[None, :, None, None] == core
     outgoing = jnp.where(slot, chunks, 0.0).reshape(n_dom, -1, width)
@@ -101,14 +109,14 @@
     dz_first = (vertex_grad * gate_value * (1.0 + z_first * (1.0 - gate_value))).astype(
         jnp.bfloat16
     )
-    product_first = weight_product(dz_first, agg_first)
+    product_first = pair_product(dz_first, agg_first)
     product_first, new_history = lax.optimization_barrier((product_first, new_history))
     grad_first = reduce_weight(product_first, rows)
 
     hist_halo = hist_slots.reshape(-1, D)[halo_index]
     hub_second = gather_hubs(new_history[owned_hubs])
     agg_second = combine_tiles(new_history, hist_halo, hub_second, tile_cols, tile_vals)
-    grad_second = reduce_weight(weight_product(grad_out, agg_second), rows)
+    grad_second = reduce_weight(pair_product(grad_out, agg_second), rows)
     return (new_history, vertex_grad.astype(jnp.bfloat16), grad_first, grad_second)
 
 

time: 272 us -> 247 us (0.908)
  waiting for transfers between devices: 119 us -> 106 us
  local copies, waits for them, and re-layouts: 51.3 us -> 41.7 us
  other arithmetic: 18.8 us -> 14.7 us
  matrix products: 15.2 us -> 18.3 us
    reduce_scatter x2, waiting for transfers between devices: 65.5 us -> 41.9 us  [reduce_weight(): lax.psum_scatter(pair.reshape(n_group, -1, width), 'group', scatter_dimen...]
    all_to_all x2, waiting for transfers between devices: 20.5 us -> 33.9 us  [gather_hubs(): lax.all_to_all(copies, 'group', split_axis=0, concat_axis=0, tiled=True)]
    reshape x2 -> x0, local copies, waits for them, and re-layouts: 10.4 us -> none  [reduce_weight(): blocks = product.reshape(n_group, n_dom // 2, 2, -1, width)]
    dynamic_slice x3 -> x1, local copies, waits for them, and re-layouts: 11.3 us -> 2.04 us  [pair_product(): keep = lax.dynamic_index_in_dim(columns, core, axis=3, keepdims=False)]
    add x2 -> x0, other arithmetic: 5.37 us -> none  [reduce_weight(): pair = keep + lax.ppermute(give, 'dom', [(i, i ^ 1) for i in range(n_dom)])]
    all_to_all x1, waiting for transfers between devices: 15.9 us -> 12.1 us  [on_device(): lax.all_to_all(jnp.stack([feats[routes], history[routes]], axis=1), 'dom'...]
    dot_general x2 -> x4, matrix products: 7.38 us -> 5.35 us  [weight_product(): lax.dot_general(left_rows, right_rows, (((0,), (0,)), ((), ())), preferre...]
  transfers between devices with their start and end apart: 9 -> 9, of which waited for: 8 -> 7; matrix products, arithmetic and copies ran while one was open for 15% -> 19% of each run, Pallas kernels for 0% -> 0%
where the time goes in v3:
time: 247 us; the launch traced here: 246 us
  waiting for transfers between devices  106 us (43%)
  local copies, waits for them, and re-layouts  41.7 us (17%)
  starting transfers between devices  27.5 us (11%)
  blocking collectives  23.4 us (9%)
  matrix products  18.3 us (7%)
  other arithmetic  14.7 us (6%)
  between operations  14 us (6%)
    reduce_scatter x2, waiting for transfers between devices, reduce_weight(): lax.psum_scatter(pair.reshape(n_group, -1, width), 'group', scatter_dimen...  41.9 us
    all_to_all x2, waiting for transfers between devices, gather_hubs(): lax.all_to_all(copies, 'group', split_axis=0, concat_axis=0, tiled=True)  33.9 us
    all_to_all x1, blocking collectives, reduce_weight(): lax.all_to_all(outgoing, 'dom', split_axis=0, concat_axis=0, tiled=True)  23.4 us
    all_to_all x2, starting transfers between devices, gather_hubs(): lax.all_to_all(copies, 'group', split_axis=0, concat_axis=0, tiled=True)  12.3 us
    all_to_all x1, waiting for transfers between devices, on_device(): lax.all_to_all(jnp.stack([feats[routes], history[routes]], axis=1), 'dom'...  12.1 us
    all_to_all x1, waiting for transfers between devices, reduce_weight(): lax.all_to_all(outgoing, 'dom', split_axis=0, concat_axis=0, tiled=True)  10.8 us
    all_to_all x1, starting transfers between devices, on_device(): lax.all_to_all(jnp.stack([feats[routes], history[routes]], axis=1), 'dom'...  8.77 us
    ppermute x2, waiting for transfers between devices, pair_product(): return kept + lax.ppermute(sent, 'dom', [(i, i ^ 1) for i in range(n_dom)])  7.57 us
  transfers between devices with their start and end apart: 9, of which 7 were waited for; matrix products, arithmetic and copies ran while one was open for 19% of the time, Pallas kernels for 0%

profile of v3, /device:TPU:1, one launch (start us, length us, event | category | flops | bytes accessed | tf_op | source)
XLA Modules:
  0.0 246.0 jit_solution(3702211568157265237)
XLA Ops:
  8.2 3.8 %gather_fusion.1 = bf16[512,1024]{1,0:T(8,128)(2,1)S(1)} fusion(bf16[128,1024]{1,0:T(8,128)(2,1)} %param.11, s32[1024]{0:T(1024)S(1)} %pad_clamp_fusion.3), kind=kCustom, calls=%fused_computation.1 | custom fusion | bytes 2099200 | tf_op jit(solution)/shard_map/gather | solution.py:99
  12.0 2.8 %gather_fusion = bf16[512,1024]{1,0:T(8,128)(2,1)} fusion(bf16[128,1024]{1,0:T(8,128)(2,1)S(1)} %copy-done.1, s32[1024]{0:T(1024)S(1)} %pad_clamp_fusion.3), kind=kCustom, calls=%fused_computation | custom fusion | bytes 2099200 | tf_op jit(solution)/shard_map/gather | solution.py:99
  14.8 2.8 %pad_maximum_fusion = bf16[32,2,16,1024]{3,2,1,0:T(8,128)(2,1)} fusion(bf16[32,1,16,1024]{3,2,1,0:T(8,128)(2,1)S(1)} %bitcast.86, bf16[32,1,16,1024]{3,2,1,0:T(8,128)(2,1)} %bitcast.87), kind=kLoop, calls=%fused_computation.9 | loop fusion | flops 1048576 | bytes 4194304 | tf_op jit(solution)/shard_map/stack | solution.py:99
  17.6 8.8 %all-to-all-start = ((bf16[32,2,16,1024]{3,2,1,0:T(8,128)(2,1)}), bf16[32,2,16,1024]{3,2,1,0:T(8,128)(2,1)}, u32[]{:S(2)}, u32[]{:S(2)}) async-start(bf16[32,2,16,1024]{3,2,1,0:T(8,128)(2,1)} %pad_maximum_fusion), calls=%async_computation.1 | async-start | bytes 4194304 | tf_op jit(solution)/shard_map/all_to_all | solution.py:98
  26.4 2.5 %convolution_bitcast_fusion = f32[4,128,1024]{1,2,0:T(8,128)} fusion(bf16[128,1024]{1,0:T(8,128)(2,1)S(1)} %copy-done.6, bf16[1024,1024]{1,0:T(8,128)(2,1)S(1)} %copy-done, bf16[1,4,128,128]{3,2,1,0:T(8,128)(2,1)S(1)} %copy-done.5), kind=kOutput, calls=%fused_computation.14 | convolution fusion | flops 402784256 | bytes 4587520 | tf_op jit(solution)/shard_map/rtij,rid->rtjd/dot_general | solution.py:82
  28.9 3.1 %copy.43 = f32[4,128,1024]{2,0,1:T(4,128)} copy(f32[4,128,1024]{1,2,0:T(8,128)} %convolution_bitcast_fusion) | data formatting | bytes 4194304 | tf_op jit(solution)/shard_map/rtij,rid->rtjd/dot_general | solution.py:82
  32.0 4.2 %fusion.7 = f32[7,128,1024]{2,0,1:T(8,128)S(1)} fusion(f32[4,128,1024]{2,0,1:T(4,128)} %copy.43, s32[4]{0:T(128)S(1)} %bitcast.94), kind=kOutput, calls=%fused_computation.42 | convolution fusion | flops 44040220 | bytes 5767184 | tf_op jit(solution)/shard_map/rts,rtjd->sjd/dot_general | solution.py:91
  36.2 1.9 copy-done.2
  42.6 12.1 %all-to-all-done = bf16[32,2,16,1024]{3,2,1,0:T(8,128)(2,1)} async-done(((bf16[32,2,16,1024]{3,2,1,0:T(8,128)(2,1)}), bf16[32,2,16,1024]{3,2,1,0:T(8,128)(2,1)}, u32[]{:S(2)}, u32[]{:S(2)}) %all-to-all-start) | async-done | bytes 2097184 | tf_op jit(solution)/shard_map/all_to_all | solution.py:98
  55.6 8.2 %all-to-all-start.1 = ((bf16[8,32,1024]{2,1,0:T(8,128)(2,1)}), bf16[8,32,1024]{2,1,0:T(8,128)(2,1)}, u32[]{:S(2)}, u32[]{:S(2)}) async-start(bf16[8,32,1024]{2,1,0:T(8,128)(2,1)} %broadcast_in_dim.71), calls=%async_computation.2 | async-start | bytes 1048576 | tf_op jit(solution)/shard_map/all_to_all | solution.py:57
  63.9 2.8 %fusion.12 = (bf16[32,1,16,1024]{3,2,1,0:T(8,128)(2,1)S(1)}, bf16[32,1,16,1024]{3,2,1,0:T(8,128)(2,1)}) fusion(bf16[32,2,16,1024]{3,2,1,0:T(8,128)(2,1)} %all-to-all-done), kind=kLoop, calls=%fused_computation.51 | loop fusion | bytes 4194304 | tf_op jit(solution)/shard_map/slice | solution.py:102
  66.7 4.9 %gather_fusion.2 = bf16[512,1024]{1,0:T(8,128)(2,1)} fusion(bf16[512,1024]{1,0:T(8,128)(2,1)} %bitcast.79, s32[1024]{0:T(1024)S(1)} %pad_clamp_fusion.2), kind=kCustom, calls=%fused_computation.2 | custom fusion | bytes 2099200 | tf_op jit(solution)/shard_map/gather | solution.py:104
  71.5 13.0 %all-to-all-done.1 = bf16[8,32,1024]{2,1,0:T(8,128)(2,1)} async-done(((bf16[8,32,1024]{2,1,0:T(8,128)(2,1)}), bf16[8,32,1024]{2,1,0:T(8,128)(2,1)}, u32[]{:S(2)}, u32[]{:S(2)}) %all-to-all-start.1) | async-done | bytes 524320 | tf_op jit(solution)/shard_map/all_to_all | solution.py:57
  84.5 2.8 %pad_maximum_fusion.1 = bf16[896,1024]{1,0:T(8,128)(2,1)} fusion(bf16[256,1024]{1,0:T(8,128)(2,1)} %bitcast.14, bf16[512,1024]{1,0:T(8,128)(2,1)} %gather_fusion.2, bf16[128,1024]{1,0:T(8,128)(2,1)S(1)} %copy-done.1), kind=kLoop, calls=%fused_computation.10 | loop fusion | flops 5505024 | bytes 3670016 | tf_op jit(solution)/shard_map/concatenate | solution.py:15
  87.3 3.1 %gather_fusion.4 = bf16[4,128,1024]{2,1,0:T(8,128)(2,1)} fusion(bf16[7,128,1024]{2,1,0:T(8,128)(2,1)} %bitcast.84, s32[1024]{0:T(1024)S(1)} %pad_clamp_fusion), kind=kCustom, calls=%fused_computation.4 | custom fusion | bytes 2097168 | tf_op jit(solution)/shard_map/gather | solution.py:17
  90.4 2.4 fusion
  92.8 3.0 %scatter_fusion = f32[128,1024]{1,0:T(8,128)} fusion(f32[128,1024]{1,0:T(8,128)} %bitcast.82, s32[32]{0:T(128)S(1)} %fusion.10, f32[32,1024]{1,0:T(8,128)} %reduce-scatter.4.cloned.1.call-done), kind=kCustom, calls=%fused_computation.8 | custom fusion | flops 32768 | bytes 393344 | tf_op jit(solution)/shard_map/scatter-add | solution.py:96
  95.8 3.3 %fusion.13 = (bf16[128,1024]{1,0:T(8,128)(2,1)}, bf16[128,1024]{1,0:T(8,128)(2,1)}, bf16[128,1024]{1,0:T(8,128)(2,1)S(1)}) fusion(f32[128,1024]{1,0:T(8,128)} %scatter_fusion, bf16[1024,128]{1,0:T(8,128)(2,1)} %fusion, bf16[1024,1024]{1,0:T(8,128)(2,1)} %param.13), kind=kOutput, calls=%fused_computation.52 | convolution fusion | flops 270008320 | bytes 3670016 | tf_op jit(solution)/shard_map/dot_general | solution.py:106
  99.1 1.9 copy.49
  101.0 2.0 constant_dynamic-slice_fusion.1
  104.4 2.2 collective-permute-start
  106.6 3.8 %collective-permute-done = f32[512,1024]{1,0:T(8,128)S(1)} collective-permute-done((f32[512,1024]{1,0:T(8,128)S(1)}, f32[512,1024]{1,0:T(8,128)S(1)}, u32[]{:S(2)}, u32[]{:S(2)}) %collective-permute-start) | collective-permute-done | bytes 2097184 | tf_op jit(solution)/shard_map/ppermute | solution.py:37
  115.1 4.1 %all-to-all-start.3 = ((bf16[8,32,1024]{2,1,0:T(8,128)(2,1)}), bf16[8,32,1024]{2,1,0:T(8,128)(2,1)}, u32[]{:S(2)}, u32[]{:S(2)}) async-start(bf16[8,32,1024]{2,1,0:T(8,128)(2,1)} %broadcast_in_dim.80), calls=%async_computation.5 | async-start | bytes 1048576 | tf_op jit(solution)/shard_map/all_to_all | solution.py:57
  119.3 2.8 %gather_fusion.5 = bf16[512,1024]{1,0:T(8,128)(2,1)} fusion(bf16[512,1024]{1,0:T(8,128)(2,1)S(1)} %bitcast.78, s32[1024]{0:T(1024)S(1)} %pad_clamp_fusion.2), kind=kCustom, calls=%fused_computation.5 | custom fusion | bytes 2099200 | tf_op jit(solution)/shard_map/gather | solution.py:116
  122.1 20.9 %all-to-all-done.3 = bf16[8,32,1024]{2,1,0:T(8,128)(2,1)} async-done(((bf16[8,32,1024]{2,1,0:T(8,128)(2,1)}), bf16[8,32,1024]{2,1,0:T(8,128)(2,1)}, u32[]{:S(2)}, u32[]{:S(2)}) %all-to-all-start.3) | async-done | bytes 524320 | tf_op jit(solution)/shard_map/all_to_all | solution.py:57
  143.1 2.8 %pad_maximum_fusion.2 = bf16[896,1024]{1,0:T(8,128)(2,1)} fusion(bf16[256,1024]{1,0:T(8,128)(2,1)} %bitcast.26, bf16[512,1024]{1,0:T(8,128)(2,1)} %gather_fusion.5, bf16[128,1024]{1,0:T(8,128)(2,1)S(1)} %get-tuple-element.2), kind=kLoop, calls=%fused_computation.11 | loop fusion | flops 5505024 | bytes 3670016 | tf_op jit(solution)/shard_map/concatenate | solution.py:15
  145.8 2.2 gather_fusion.7
  149.4 3.8 %collective-permute-done.1 = f32[512,1024]{1,0:T(8,128)S(1)} collective-permute-done((f32[512,1024]{1,0:T(8,128)S(1)}, f32[512,1024]{1,0:T(8,128)S(1)}, u32[]{:S(2)}, u32[]{:S(2)}) %collective-permute-start.1) | collective-permute-done | bytes 2097184 | tf_op jit(solution)/shard_map/ppermute | solution.py:37
  156.2 41.9 %reduce-scatter.8.cloned.1.call-done = f32[1,64,1024]{2,1,0:T(8,128)} async-done(((f32[8,64,1024]{2,1,0:T(8,128)}), f32[1,64,1024]{2,1,0:T(8,128)}) %reduce-scatter.8.cloned.1.call-update) | async-done | bytes 262160 | tf_op jit(solution)/shard_map/reduce_scatter | solution.py:46
  200.1 23.4 %all_to_all.25 = f32[32,4,1024]{2,1,0:T(4,128)S(1)} all-to-all(f32[32,4,1024]{2,1,0:T(4,128)S(1)} %get-tuple-element.18), channel_id=1, replica_groups=mesh['group'=8,'dom'=32] {'dom'}, dimensions={0} | all-to-all | bytes 1048576 | tf_op jit(solution)/shard_map/all_to_all | solution.py:50
  223.6 3.7 %all-to-all-start.4 = ((f32[32,4,1024]{2,1,0:T(4,128)}), f32[32,4,1024]{2,1,0:T(4,128)S(1)}, u32[]{:S(2)}, u32[]{:S(2)}) async-start(f32[32,4,1024]{2,1,0:T(4,128)} %get-tuple-element.17), calls=%async_computation.7 | async-start | bytes 1048576 | tf_op jit(solution)/shard_map/all_to_all | solution.py:50
  228.0 10.8 %all-to-all-done.4 = f32[32,4,1024]{2,1,0:T(4,128)S(1)} async-done(((f32[32,4,1024]{2,1,0:T(4,128)}), f32[32,4,1024]{2,1,0:T(4,128)S(1)}, u32[]{:S(2)}, u32[]{:S(2)}) %all-to-all-start.4) | async-done | bytes 524320 | tf_op jit(solution)/shard_map/all_to_all | solution.py:50
  (67 shorter events, 20.4 us)
Async XLA Ops:
  7.2 19.2 %copy-start = (bf16[1024,1024]{1,0:T(8,128)(2,1)S(1)}, bf16[1024,1024]{1,0:T(8,128)(2,1)}, u32[]{:S(2)}) copy-start(bf16[1024,1024]{1,0:T(8,128)(2,1)} %param.14) | copy-start | bytes 6291460
  8.2 3.8 %copy-start.1 = (bf16[128,1024]{1,0:T(8,128)(2,1)S(1)}, bf16[128,1024]{1,0:T(8,128)(2,1)}, u32[]{:S(2)}) copy-start(bf16[128,1024]{1,0:T(8,128)(2,1)} %param.10) | copy-start | bytes 786436
  17.5 8.8 %copy-start.5 = (bf16[1,4,128,128]{3,2,1,0:T(8,128)(2,1)S(1)}, bf16[1,4,128,128]{3,2,1,0:T(8,128)(2,1)}, u32[]{:S(2)}) copy-start(bf16[1,4,128,128]{3,2,1,0:T(8,128)(2,1)} %param.19) | copy-start | bytes 393220
  17.6 8.8 %copy-start.6 = (bf16[128,1024]{1,0:T(8,128)(2,1)S(1)}, bf16[128,1024]{1,0:T(8,128)(2,1)}, u32[]{:S(2)}) copy-start(bf16[128,1024]{1,0:T(8,128)(2,1)} %param.12) | copy-start | bytes 786436
  17.6 37.2 %all-to-all-start = ((bf16[32,2,16,1024]{3,2,1,0:T(8,128)(2,1)}), bf16[32,2,16,1024]{3,2,1,0:T(8,128)(2,1)}, u32[]{:S(2)}, u32[]{:S(2)}) async-start(bf16[32,2,16,1024]{3,2,1,0:T(8,128)(2,1)} %pad_maximum_fusion), calls=%async_computation.1 | async-start | bytes 4194304 | tf_op jit(solution)/shard_map/all_to_all | solution.py:98
  26.3 66.5 %reduce-scatter.4.cloned.1.call-start = ((), (), s32[]{:S(2)}) async-start(), calls=%async_computation.8 | async-start | bytes 1179648 | tf_op jit(solution)/shard_map/reduce_scatter | solution.py:95
  28.9 3.1 %copy-start.10 = (s32[1,4]{1,0:T(1,128)S(1)}, s32[1,4]{1,0:T(1,128)}, u32[]{:S(2)}) copy-start(s32[1,4]{1,0:T(1,128)} %param.18) | copy-start | bytes 52
  36.2 2.0 copy-start.2
  38.8 2.3 slice-start
  40.2 1.8 copy-start.11
  41.0 22.8 %copy-start.9 = (s32[512]{0:T(512)S(1)}, s32[512]{0:T(512)}, u32[]{:S(2)}) copy-start(s32[512]{0:T(512)} %param.16) | copy-start | bytes 6148
  55.6 28.9 %all-to-all-start.1 = ((bf16[8,32,1024]{2,1,0:T(8,128)(2,1)}), bf16[8,32,1024]{2,1,0:T(8,128)(2,1)}, u32[]{:S(2)}, u32[]{:S(2)}) async-start(bf16[8,32,1024]{2,1,0:T(8,128)(2,1)} %broadcast_in_dim.71), calls=%async_computation.2 | async-start | bytes 1048576 | tf_op jit(solution)/shard_map/all_to_all | solution.py:57
  63.8 91.4 %reduce-scatter.6.cloned.1.call-start = ((), (), s32[]{:S(2)}) async-start(), calls=%async_computation.9 | async-start | bytes 2359296 | tf_op jit(solution)/shard_map/reduce_scatter | solution.py:46
  99.1 43.9 %copy-start.3 = (bf16[128,1024]{1,0:T(8,128)(2,1)}, bf16[128,1024]{1,0:T(8,128)(2,1)S(1)}, u32[]{:S(2)}) copy-start(bf16[128,1024]{1,0:T(8,128)(2,1)S(1)} %get-tuple-element.2) | copy-start | bytes 786436
  101.0 9.4 %copy-start.4 = (bf16[1024,128]{1,0:T(8,128)(2,1)S(1)}, bf16[1024,128]{1,0:T(8,128)(2,1)}, u32[]{:S(2)}) copy-start(bf16[1024,128]{1,0:T(8,128)(2,1)} %fusion) | copy-start | bytes 786436
  104.4 5.9 %collective-permute-start = (f32[512,1024]{1,0:T(8,128)S(1)}, f32[512,1024]{1,0:T(8,128)S(1)}, u32[]{:S(2)}, u32[]{:S(2)}) collective-permute-start(f32[512,1024]{1,0:T(8,128)S(1)} %fusion.14), channel_id=1, source_target_pairs={{0,1},{1,0},{2,3},{3,2},{4,5},{5,4},{6,7},{7,6},{8,9},{9,8},{10,11... | collective-permute-start | bytes 6291464 | tf_op jit(solution)/shard_map/ppermute | solution.py:37
  115.1 27.9 %all-to-all-start.3 = ((bf16[8,32,1024]{2,1,0:T(8,128)(2,1)}), bf16[8,32,1024]{2,1,0:T(8,128)(2,1)}, u32[]{:S(2)}, u32[]{:S(2)}) async-start(bf16[8,32,1024]{2,1,0:T(8,128)(2,1)} %broadcast_in_dim.80), calls=%async_computation.5 | async-start | bytes 1048576 | tf_op jit(solution)/shard_map/all_to_all | solution.py:57
  119.3 78.8 %reduce-scatter.8.cloned.1.call-start = ((), (), s32[]{:S(2)}) async-start(), calls=%async_computation.10 | async-start | bytes 2359296 | tf_op jit(solution)/shard_map/reduce_scatter | solution.py:46
  145.8 2.7 %copy-start.8 = (bf16[128,8,16,1,4]{0,4,3,2,1:T(4,128)(2,1)S(1)}, bf16[128,8,16,1,4]{0,4,3,2,1:T(4,128)(2,1)}, u32[]{:S(2)}) copy-start(bf16[128,8,16,1,4]{0,4,3,2,1:T(4,128)(2,1)} %get-tuple-element.14) | copy-start | bytes 393220
  148.0 5.2 %copy-start.7 = (bf16[128,8,16,1,4]{0,4,3,2,1:T(4,128)(2,1)S(1)}, bf16[128,8,16,1,4]{0,4,3,2,1:T(4,128)(2,1)}, u32[]{:S(2)}) copy-start(bf16[128,8,16,1,4]{0,4,3,2,1:T(4,128)(2,1)} %get-tuple-element.13) | copy-start | bytes 393220
  148.9 4.3 %collective-permute-start.1 = (f32[512,1024]{1,0:T(8,128)S(1)}, f32[512,1024]{1,0:T(8,128)S(1)}, u32[]{:S(2)}, u32[]{:S(2)}) collective-permute-start(f32[512,1024]{1,0:T(8,128)S(1)} %fusion.15), channel_id=1, source_target_pairs={{0,1},{1,0},{2,3},{3,2},{4,5},{5,4},{6,7},{7,6},{8,9},{9,8},{10,11... | collective-permute-start | bytes 6291464 | tf_op jit(solution)/shard_map/ppermute | solution.py:37
  223.6 15.2 %all-to-all-start.4 = ((f32[32,4,1024]{2,1,0:T(4,128)}), f32[32,4,1024]{2,1,0:T(4,128)S(1)}, u32[]{:S(2)}, u32[]{:S(2)}) async-start(f32[32,4,1024]{2,1,0:T(4,128)} %get-tuple-element.17), calls=%async_computation.7 | async-start | bytes 1048576 | tf_op jit(solution)/shard_map/all_to_all | solution.py:50
Sparse Core Ops, SparseCore 0:
  40.3 42.6 reduce-scatter.3
  112.3 40.6 reduce-scatter.5
  155.5 42.4 reduce-scatter.7

commit v4 on v3

--- a/solution.py
+++ b/solution.py
@@ -37,8 +37,7 @@
     return kept + lax.ppermute(sent, "dom", [(i, i ^ 1) for i in range(n_dom)])
 
 
-def reduce_weight(pair, rows_per_device):
-    factor = 1.0 / math.sqrt(rows_per_device * lax.axis_size("group") * lax.axis_size("dom"))
+def reduce_in_group(pair):
     n_group = lax.axis_size("group")
     n_dom = lax.axis_size("dom")
     width = pair.shape[1]
@@ -46,7 +45,11 @@
     in_group = lax.psum_scatter(pair.reshape(n_group, -1, width), "group", scatter_dimension=0, tiled=True)
     chunks = in_group.reshape(n_dom // 2, 1, -1, width)
     slot = jnp.arange(2, dtype=jnp.int32)[None, :, None, None] == core
-    outgoing = jnp.where(slot, chunks, 0.0).reshape(n_dom, -1, width)
+    return jnp.where(slot, chunks, 0.0).reshape(n_dom, -1, width)
+
+
+def reduce_over_dom(outgoing, rows_per_device):
+    factor = 1.0 / math.sqrt(rows_per_device * lax.axis_size("group") * lax.axis_size("dom"))
     pieces = lax.all_to_all(outgoing, "dom", split_axis=0, concat_axis=0, tiled=True)
     return pieces.sum(axis=0) * factor
 
@@ -111,12 +114,14 @@
     )
     product_first = pair_product(dz_first, agg_first)
     product_first, new_history = lax.optimization_barrier((product_first, new_history))
-    grad_first = reduce_weight(product_first, rows)
+    outgoing_first = reduce_in_group(product_first)
 
     hist_halo = hist_slots.reshape(-1, D)[halo_index]
     hub_second = gather_hubs(new_history[owned_hubs])
     agg_second = combine_tiles(new_history, hist_halo, hub_second, tile_cols, tile_vals)
-    grad_second = reduce_weight(pair_product(grad_out, agg_second), rows)
+    outgoing_second = reduce_in_group(pair_product(grad_out, agg_second))
+    both = reduce_over_dom(jnp.concatenate([outgoing_first, outgoing_second], axis=1), rows)
+    grad_first, grad_second = jnp.split(both, 2, axis=0)
     return (new_history, vertex_grad.astype(jnp.bfloat16), grad_first, grad_second)
 
 

time: 247 us -> 237 us (0.960)
  waiting for transfers between devices: 106 us -> 95.9 us
  blocking collectives: 23.4 us -> 28.6 us
  starting transfers between devices: 27.5 us -> 23.8 us
    all_to_all x1 -> x0, waiting for transfers between devices: 10.8 us -> none  [reduce_weight(): lax.all_to_all(outgoing, 'dom', split_axis=0, concat_axis=0, tiled=True)]
    all_to_all x1, blocking collectives: 23.4 us -> 28.6 us  [reduce_over_dom(): lax.all_to_all(outgoing, 'dom', split_axis=0, concat_axis=0, tiled=True)]
    all_to_all x1 -> x0, starting transfers between devices: 3.67 us -> none  [reduce_weight(): lax.all_to_all(outgoing, 'dom', split_axis=0, concat_axis=0, tiled=True)]
  transfers between devices with their start and end apart: 9 -> 8, of which waited for: 7 -> 6; matrix products, arithmetic and copies ran while one was open for 19% -> 19% of each run, Pallas kernels for 0% -> 0%
where the time goes in v4:
time: 237 us; the launch traced here: 236 us
  waiting for transfers between devices  95.9 us (40%)
  local copies, waits for them, and re-layouts  42.2 us (18%)
  blocking collectives  28.6 us (12%)
  starting transfers between devices  23.8 us (10%)
  matrix products  18.2 us (8%)
  between operations  14 us (6%)
  other arithmetic  12.8 us (5%)
    reduce_scatter x2, waiting for transfers between devices, reduce_in_group(): lax.psum_scatter(pair.reshape(n_group, -1, width), 'group', scatter_dimen...  42.1 us
    all_to_all x2, waiting for transfers between devices, gather_hubs(): lax.all_to_all(copies, 'group', split_axis=0, concat_axis=0, tiled=True)  34 us
    all_to_all x1, blocking collectives, reduce_over_dom(): lax.all_to_all(outgoing, 'dom', split_axis=0, concat_axis=0, tiled=True)  28.6 us
    all_to_all x2, starting transfers between devices, gather_hubs(): lax.all_to_all(copies, 'group', split_axis=0, concat_axis=0, tiled=True)  12.3 us
    all_to_all x1, waiting for transfers between devices, on_device(): lax.all_to_all(jnp.stack([feats[routes], history[routes]], axis=1), 'dom'...  12.2 us
    all_to_all x1, starting transfers between devices, on_device(): lax.all_to_all(jnp.stack([feats[routes], history[routes]], axis=1), 'dom'...  8.76 us
    ppermute x2, waiting for transfers between devices, pair_product(): return kept + lax.ppermute(sent, 'dom', [(i, i ^ 1) for i in range(n_dom)])  7.57 us
    concatenate x2, other arithmetic, combine_tiles(): source = jnp.concatenate([own_rows, halo_rows, hub_panel], axis=0)  5.57 us
  transfers between devices with their start and end apart: 8, of which 6 were waited for; matrix products, arithmetic and copies ran while one was open for 19% of the time, Pallas kernels for 0%

profile of v4, /device:TPU:1, one launch (start us, length us, event | category | flops | bytes accessed | tf_op | source)
XLA Modules:
  0.0 235.7 jit_solution(1544287607069158151)
XLA Ops:
  8.2 3.8 %gather_fusion.1 = bf16[512,1024]{1,0:T(8,128)(2,1)S(1)} fusion(bf16[128,1024]{1,0:T(8,128)(2,1)} %param.11, s32[1024]{0:T(1024)S(1)} %pad_clamp_fusion.3), kind=kCustom, calls=%fused_computation.1 | custom fusion | bytes 2099200 | tf_op jit(solution)/shard_map/gather | solution.py:102
  12.0 2.8 %gather_fusion = bf16[512,1024]{1,0:T(8,128)(2,1)} fusion(bf16[128,1024]{1,0:T(8,128)(2,1)S(1)} %copy-done.1, s32[1024]{0:T(1024)S(1)} %pad_clamp_fusion.3), kind=kCustom, calls=%fused_computation | custom fusion | bytes 2099200 | tf_op jit(solution)/shard_map/gather | solution.py:102
  14.8 2.8 %pad_maximum_fusion = bf16[32,2,16,1024]{3,2,1,0:T(8,128)(2,1)} fusion(bf16[32,1,16,1024]{3,2,1,0:T(8,128)(2,1)S(1)} %bitcast.86, bf16[32,1,16,1024]{3,2,1,0:T(8,128)(2,1)} %bitcast.87), kind=kLoop, calls=%fused_computation.9 | loop fusion | flops 1048576 | bytes 4194304 | tf_op jit(solution)/shard_map/stack | solution.py:102
  17.6 8.8 %all-to-all-start = ((bf16[32,2,16,1024]{3,2,1,0:T(8,128)(2,1)}), bf16[32,2,16,1024]{3,2,1,0:T(8,128)(2,1)}, u32[]{:S(2)}, u32[]{:S(2)}) async-start(bf16[32,2,16,1024]{3,2,1,0:T(8,128)(2,1)} %pad_maximum_fusion), calls=%async_computation.1 | async-start | bytes 4194304 | tf_op jit(solution)/shard_map/all_to_all | solution.py:101
  26.4 2.5 %convolution_bitcast_fusion = f32[4,128,1024]{1,2,0:T(8,128)} fusion(bf16[128,1024]{1,0:T(8,128)(2,1)S(1)} %copy-done.6, bf16[1024,1024]{1,0:T(8,128)(2,1)S(1)} %copy-done, bf16[1,4,128,128]{3,2,1,0:T(8,128)(2,1)S(1)} %copy-done.5), kind=kOutput, calls=%fused_computation.14 | convolution fusion | flops 402784256 | bytes 4587520 | tf_op jit(solution)/shard_map/rtij,rid->rtjd/dot_general | solution.py:85
  28.9 3.1 %copy.31 = f32[4,128,1024]{2,0,1:T(4,128)} copy(f32[4,128,1024]{1,2,0:T(8,128)} %convolution_bitcast_fusion) | data formatting | bytes 4194304 | tf_op jit(solution)/shard_map/rtij,rid->rtjd/dot_general | solution.py:85
  32.0 4.2 %fusion.7 = f32[7,128,1024]{2,0,1:T(8,128)S(1)} fusion(f32[4,128,1024]{2,0,1:T(4,128)} %copy.31, s32[4]{0:T(128)S(1)} %bitcast.94), kind=kOutput, calls=%fused_computation.42 | convolution fusion | flops 44040220 | bytes 5767184 | tf_op jit(solution)/shard_map/rts,rtjd->sjd/dot_general | solution.py:94
  36.2 1.9 copy-done.2
  42.5 12.2 %all-to-all-done = bf16[32,2,16,1024]{3,2,1,0:T(8,128)(2,1)} async-done(((bf16[32,2,16,1024]{3,2,1,0:T(8,128)(2,1)}), bf16[32,2,16,1024]{3,2,1,0:T(8,128)(2,1)}, u32[]{:S(2)}, u32[]{:S(2)}) %all-to-all-start) | async-done | bytes 2097184 | tf_op jit(solution)/shard_map/all_to_all | solution.py:101
  55.6 8.2 %all-to-all-start.1 = ((bf16[8,32,1024]{2,1,0:T(8,128)(2,1)}), bf16[8,32,1024]{2,1,0:T(8,128)(2,1)}, u32[]{:S(2)}, u32[]{:S(2)}) async-start(bf16[8,32,1024]{2,1,0:T(8,128)(2,1)} %broadcast_in_dim.71), calls=%async_computation.2 | async-start | bytes 1048576 | tf_op jit(solution)/shard_map/all_to_all | solution.py:60
  63.9 2.8 %fusion.12 = (bf16[32,1,16,1024]{3,2,1,0:T(8,128)(2,1)S(1)}, bf16[32,1,16,1024]{3,2,1,0:T(8,128)(2,1)}) fusion(bf16[32,2,16,1024]{3,2,1,0:T(8,128)(2,1)} %all-to-all-done), kind=kLoop, calls=%fused_computation.51 | loop fusion | bytes 4194304 | tf_op jit(solution)/shard_map/slice | solution.py:105
  66.7 4.8 %gather_fusion.2 = bf16[512,1024]{1,0:T(8,128)(2,1)} fusion(bf16[512,1024]{1,0:T(8,128)(2,1)} %bitcast.79, s32[1024]{0:T(1024)S(1)} %pad_clamp_fusion.2), kind=kCustom, calls=%fused_computation.2 | custom fusion | bytes 2099200 | tf_op jit(solution)/shard_map/gather | solution.py:107
  71.5 13.0 %all-to-all-done.1 = bf16[8,32,1024]{2,1,0:T(8,128)(2,1)} async-done(((bf16[8,32,1024]{2,1,0:T(8,128)(2,1)}), bf16[8,32,1024]{2,1,0:T(8,128)(2,1)}, u32[]{:S(2)}, u32[]{:S(2)}) %all-to-all-start.1) | async-done | bytes 524320 | tf_op jit(solution)/shard_map/all_to_all | solution.py:60
  84.6 2.8 %pad_maximum_fusion.1 = bf16[896,1024]{1,0:T(8,128)(2,1)} fusion(bf16[256,1024]{1,0:T(8,128)(2,1)} %bitcast.14, bf16[512,1024]{1,0:T(8,128)(2,1)} %gather_fusion.2, bf16[128,1024]{1,0:T(8,128)(2,1)S(1)} %copy-done.1), kind=kLoop, calls=%fused_computation.10 | loop fusion | flops 5505024 | bytes 3670016 | tf_op jit(solution)/shard_map/concatenate | solution.py:15
  87.4 3.1 %gather_fusion.4 = bf16[4,128,1024]{2,1,0:T(8,128)(2,1)} fusion(bf16[7,128,1024]{2,1,0:T(8,128)(2,1)} %bitcast.84, s32[1024]{0:T(1024)S(1)} %pad_clamp_fusion), kind=kCustom, calls=%fused_computation.4 | custom fusion | bytes 2097168 | tf_op jit(solution)/shard_map/gather | solution.py:17
  90.5 2.4 %fusion = bf16[1024,128]{1,0:T(8,128)(2,1)} fusion(bf16[4,128,1024]{2,1,0:T(8,128)(2,1)} %gather_fusion.4, bf16[1,4,128,128]{3,2,1,0:T(8,128)(2,1)S(1)} %copy-done.5), kind=kOutput, calls=%fused_computation.17 | convolution fusion | flops 134348800 | bytes 1441792 | tf_op jit(solution)/shard_map/rtij,rtjd->rid/dot_general | solution.py:18
  92.9 3.0 %scatter_fusion = f32[128,1024]{1,0:T(8,128)} fusion(f32[128,1024]{1,0:T(8,128)} %bitcast.82, s32[32]{0:T(128)S(1)} %fusion.10, f32[32,1024]{1,0:T(8,128)} %reduce-scatter.4.cloned.1.call-done), kind=kCustom, calls=%fused_computation.8 | custom fusion | flops 32768 | bytes 393344 | tf_op jit(solution)/shard_map/scatter-add | solution.py:99
  95.9 3.3 %fusion.13 = (bf16[128,1024]{1,0:T(8,128)(2,1)}, bf16[128,1024]{1,0:T(8,128)(2,1)}, bf16[128,1024]{1,0:T(8,128)(2,1)S(1)}) fusion(f32[128,1024]{1,0:T(8,128)} %scatter_fusion, bf16[1024,128]{1,0:T(8,128)(2,1)} %fusion, bf16[1024,1024]{1,0:T(8,128)(2,1)} %param.13), kind=kOutput, calls=%fused_computation.52 | convolution fusion | flops 270008320 | bytes 3670016 | tf_op jit(solution)/shard_map/dot_general | solution.py:109
  99.2 1.9 copy.37
  101.1 2.0 constant_dynamic-slice_fusion.1
  104.5 2.1 collective-permute-start
  106.6 3.8 %collective-permute-done = f32[512,1024]{1,0:T(8,128)S(1)} collective-permute-done((f32[512,1024]{1,0:T(8,128)S(1)}, f32[512,1024]{1,0:T(8,128)S(1)}, u32[]{:S(2)}, u32[]{:S(2)}) %collective-permute-start) | collective-permute-done | bytes 2097184 | tf_op jit(solution)/shard_map/ppermute | solution.py:37
  110.4 1.8 convolution_add_fusion.1
  115.1 4.1 %all-to-all-start.2 = ((bf16[8,32,1024]{2,1,0:T(8,128)(2,1)}), bf16[8,32,1024]{2,1,0:T(8,128)(2,1)}, u32[]{:S(2)}, u32[]{:S(2)}) async-start(bf16[8,32,1024]{2,1,0:T(8,128)(2,1)} %broadcast_in_dim.80), calls=%async_computation.4 | async-start | bytes 1048576 | tf_op jit(solution)/shard_map/all_to_all | solution.py:60
  119.3 2.8 %gather_fusion.5 = bf16[512,1024]{1,0:T(8,128)(2,1)} fusion(bf16[512,1024]{1,0:T(8,128)(2,1)S(1)} %bitcast.78, s32[1024]{0:T(1024)S(1)} %pad_clamp_fusion.2), kind=kCustom, calls=%fused_computation.5 | custom fusion | bytes 2099200 | tf_op jit(solution)/shard_map/gather | solution.py:119
  122.1 20.9 %all-to-all-done.2 = bf16[8,32,1024]{2,1,0:T(8,128)(2,1)} async-done(((bf16[8,32,1024]{2,1,0:T(8,128)(2,1)}), bf16[8,32,1024]{2,1,0:T(8,128)(2,1)}, u32[]{:S(2)}, u32[]{:S(2)}) %all-to-all-start.2) | async-done | bytes 524320 | tf_op jit(solution)/shard_map/all_to_all | solution.py:60
  143.0 2.8 %pad_maximum_fusion.2 = bf16[896,1024]{1,0:T(8,128)(2,1)} fusion(bf16[256,1024]{1,0:T(8,128)(2,1)} %bitcast.26, bf16[512,1024]{1,0:T(8,128)(2,1)} %gather_fusion.5, bf16[128,1024]{1,0:T(8,128)(2,1)S(1)} %get-tuple-element.2), kind=kLoop, calls=%fused_computation.11 | loop fusion | flops 5505024 | bytes 3670016 | tf_op jit(solution)/shard_map/concatenate | solution.py:15
  145.8 2.2 gather_fusion.7
  149.4 3.8 %collective-permute-done.1 = f32[512,1024]{1,0:T(8,128)S(1)} collective-permute-done((f32[512,1024]{1,0:T(8,128)S(1)}, f32[512,1024]{1,0:T(8,128)S(1)}, u32[]{:S(2)}, u32[]{:S(2)}) %collective-permute-start.1) | collective-permute-done | bytes 2097184 | tf_op jit(solution)/shard_map/ppermute | solution.py:37
  153.2 1.7 convolution_add_fusion
  156.1 42.1 %reduce-scatter.8.cloned.1.call-done = f32[1,64,1024]{2,1,0:T(8,128)} async-done(((f32[8,64,1024]{2,1,0:T(8,128)}), f32[1,64,1024]{2,1,0:T(8,128)}) %reduce-scatter.8.cloned.1.call-update) | async-done | bytes 262160 | tf_op jit(solution)/shard_map/reduce_scatter | solution.py:45
  199.8 28.6 %all_to_all.20 = f32[32,8,1024]{2,1,0:T(8,128)S(1)} all-to-all(f32[32,8,1024]{2,1,0:T(8,128)S(1)} %pad_maximum_fusion.3), channel_id=1, replica_groups=mesh['group'=8,'dom'=32] {'dom'}, dimensions={0} | all-to-all | bytes 2097152 | tf_op jit(solution)/shard_map/all_to_all | solution.py:53
  (65 shorter events, 15.5 us)
Async XLA Ops:
  7.2 19.2 %copy-start = (bf16[1024,1024]{1,0:T(8,128)(2,1)S(1)}, bf16[1024,1024]{1,0:T(8,128)(2,1)}, u32[]{:S(2)}) copy-start(bf16[1024,1024]{1,0:T(8,128)(2,1)} %param.14) | copy-start | bytes 6291460
  8.2 3.8 %copy-start.1 = (bf16[128,1024]{1,0:T(8,128)(2,1)S(1)}, bf16[128,1024]{1,0:T(8,128)(2,1)}, u32[]{:S(2)}) copy-start(bf16[128,1024]{1,0:T(8,128)(2,1)} %param.10) | copy-start | bytes 786436
  17.5 8.8 %copy-start.5 = (bf16[1,4,128,128]{3,2,1,0:T(8,128)(2,1)S(1)}, bf16[1,4,128,128]{3,2,1,0:T(8,128)(2,1)}, u32[]{:S(2)}) copy-start(bf16[1,4,128,128]{3,2,1,0:T(8,128)(2,1)} %param.19) | copy-start | bytes 393220
  17.5 8.8 %copy-start.6 = (bf16[128,1024]{1,0:T(8,128)(2,1)S(1)}, bf16[128,1024]{1,0:T(8,128)(2,1)}, u32[]{:S(2)}) copy-start(bf16[128,1024]{1,0:T(8,128)(2,1)} %param.12) | copy-start | bytes 786436
  17.6 37.2 %all-to-all-start = ((bf16[32,2,16,1024]{3,2,1,0:T(8,128)(2,1)}), bf16[32,2,16,1024]{3,2,1,0:T(8,128)(2,1)}, u32[]{:S(2)}, u32[]{:S(2)}) async-start(bf16[32,2,16,1024]{3,2,1,0:T(8,128)(2,1)} %pad_maximum_fusion), calls=%async_computation.1 | async-start | bytes 4194304 | tf_op jit(solution)/shard_map/all_to_all | solution.py:101
  26.3 66.5 %reduce-scatter.4.cloned.1.call-start = ((), (), s32[]{:S(2)}) async-start(), calls=%async_computation.7 | async-start | bytes 1179648 | tf_op jit(solution)/shard_map/reduce_scatter | solution.py:98
  28.9 3.1 %copy-start.10 = (s32[1,4]{1,0:T(1,128)S(1)}, s32[1,4]{1,0:T(1,128)}, u32[]{:S(2)}) copy-start(s32[1,4]{1,0:T(1,128)} %param.18) | copy-start | bytes 52
  36.2 1.9 copy-start.2
  38.7 2.3 slice-start
  40.1 1.7 copy-start.11
  41.0 22.8 %copy-start.9 = (s32[512]{0:T(512)S(1)}, s32[512]{0:T(512)}, u32[]{:S(2)}) copy-start(s32[512]{0:T(512)} %param.16) | copy-start | bytes 6148
  55.6 29.0 %all-to-all-start.1 = ((bf16[8,32,1024]{2,1,0:T(8,128)(2,1)}), bf16[8,32,1024]{2,1,0:T(8,128)(2,1)}, u32[]{:S(2)}, u32[]{:S(2)}) async-start(bf16[8,32,1024]{2,1,0:T(8,128)(2,1)} %broadcast_in_dim.71), calls=%async_computation.2 | async-start | bytes 1048576 | tf_op jit(solution)/shard_map/all_to_all | solution.py:60
  63.8 91.3 %reduce-scatter.6.cloned.1.call-start = ((), (), s32[]{:S(2)}) async-start(), calls=%async_computation.8 | async-start | bytes 2359296 | tf_op jit(solution)/shard_map/reduce_scatter | solution.py:45
  99.2 43.9 %copy-start.3 = (bf16[128,1024]{1,0:T(8,128)(2,1)}, bf16[128,1024]{1,0:T(8,128)(2,1)S(1)}, u32[]{:S(2)}) copy-start(bf16[128,1024]{1,0:T(8,128)(2,1)S(1)} %get-tuple-element.2) | copy-start | bytes 786436
  101.1 9.3 %copy-start.4 = (bf16[1024,128]{1,0:T(8,128)(2,1)S(1)}, bf16[1024,128]{1,0:T(8,128)(2,1)}, u32[]{:S(2)}) copy-start(bf16[1024,128]{1,0:T(8,128)(2,1)} %fusion) | copy-start | bytes 786436
  104.5 5.9 %collective-permute-start = (f32[512,1024]{1,0:T(8,128)S(1)}, f32[512,1024]{1,0:T(8,128)S(1)}, u32[]{:S(2)}, u32[]{:S(2)}) collective-permute-start(f32[512,1024]{1,0:T(8,128)S(1)} %fusion.15), channel_id=1, source_target_pairs={{0,1},{1,0},{2,3},{3,2},{4,5},{5,4},{6,7},{7,6},{8,9},{9,8},{10,11... | collective-permute-start | bytes 6291464 | tf_op jit(solution)/shard_map/ppermute | solution.py:37
  115.1 27.9 %all-to-all-start.2 = ((bf16[8,32,1024]{2,1,0:T(8,128)(2,1)}), bf16[8,32,1024]{2,1,0:T(8,128)(2,1)}, u32[]{:S(2)}, u32[]{:S(2)}) async-start(bf16[8,32,1024]{2,1,0:T(8,128)(2,1)} %broadcast_in_dim.80), calls=%async_computation.4 | async-start | bytes 1048576 | tf_op jit(solution)/shard_map/all_to_all | solution.py:60
  119.3 79.0 %reduce-scatter.8.cloned.1.call-start = ((), (), s32[]{:S(2)}) async-start(), calls=%async_computation.9 | async-start | bytes 2359296 | tf_op jit(solution)/shard_map/reduce_scatter | solution.py:45
  145.8 2.7 %copy-start.8 = (bf16[128,8,16,1,4]{0,4,3,2,1:T(4,128)(2,1)S(1)}, bf16[128,8,16,1,4]{0,4,3,2,1:T(4,128)(2,1)}, u32[]{:S(2)}) copy-start(bf16[128,8,16,1,4]{0,4,3,2,1:T(4,128)(2,1)} %get-tuple-element.14) | copy-start | bytes 393220
  148.0 5.2 %copy-start.7 = (bf16[128,8,16,1,4]{0,4,3,2,1:T(4,128)(2,1)S(1)}, bf16[128,8,16,1,4]{0,4,3,2,1:T(4,128)(2,1)}, u32[]{:S(2)}) copy-start(bf16[128,8,16,1,4]{0,4,3,2,1:T(4,128)(2,1)} %get-tuple-element.13) | copy-start | bytes 393220
  148.9 4.3 %collective-permute-start.1 = (f32[512,1024]{1,0:T(8,128)S(1)}, f32[512,1024]{1,0:T(8,128)S(1)}, u32[]{:S(2)}, u32[]{:S(2)}) collective-permute-start(f32[512,1024]{1,0:T(8,128)S(1)} %fusion.16), channel_id=1, source_target_pairs={{0,1},{1,0},{2,3},{3,2},{4,5},{5,4},{6,7},{7,6},{8,9},{9,8},{10,11... | collective-permute-start | bytes 6291464 | tf_op jit(solution)/shard_map/ppermute | solution.py:37
Sparse Core Ops, SparseCore 0:
  40.3 42.9 reduce-scatter.3
  112.3 40.8 reduce-scatter.5
  155.7 42.4 reduce-scatter.7

commit v5 on v4

--- a/solution.py
+++ b/solution.py
@@ -25,10 +25,10 @@
     )
 
 
-def pair_product(left_rows, right_rows):
+def pair_product(left_rows, right_rows, flip):
     n_group = lax.axis_size("group")
     n_dom = lax.axis_size("dom")
-    core = lax.axis_index("dom") % 2
+    core = (lax.axis_index("dom") + flip) % 2
     columns = left_rows.reshape(left_rows.shape[0], n_group, n_dom // 2, 2, -1)
     keep = lax.dynamic_index_in_dim(columns, core, axis=3, keepdims=False)
     give = lax.dynamic_index_in_dim(columns, 1 - core, axis=3, keepdims=False)
@@ -39,19 +39,23 @@
 
 def reduce_in_group(pair):
     n_group = lax.axis_size("group")
-    n_dom = lax.axis_size("dom")
     width = pair.shape[1]
-    core = lax.axis_index("dom") % 2
     in_group = lax.psum_scatter(pair.reshape(n_group, -1, width), "group", scatter_dimension=0, tiled=True)
-    chunks = in_group.reshape(n_dom // 2, 1, -1, width)
-    slot = jnp.arange(2, dtype=jnp.int32)[None, :, None, None] == core
-    return jnp.where(slot, chunks, 0.0).reshape(n_dom, -1, width)
+    return in_group.reshape(lax.axis_size("dom") // 2, -1, width)
 
 
-def reduce_over_dom(outgoing, rows_per_device):
+def reduce_over_dom(first, second, rows_per_device):
     factor = 1.0 / math.sqrt(rows_per_device * lax.axis_size("group") * lax.axis_size("dom"))
+    n_dom = lax.axis_size("dom")
+    width = first.shape[-1]
+    core = lax.axis_index("dom") % 2
+    slot = jnp.arange(2, dtype=jnp.int32)[None, :, None, None] == core
+    outgoing = jnp.where(slot, first[:, None], second[:, None]).reshape(n_dom, -1, width)
     pieces = lax.all_to_all(outgoing, "dom", split_axis=0, concat_axis=0, tiled=True)
-    return pieces.sum(axis=0) * factor
+    pieces = pieces.reshape(n_dom // 2, 2, -1, width)
+    own_core = lax.dynamic_index_in_dim(pieces, core, axis=1, keepdims=False)
+    other_core = lax.dynamic_index_in_dim(pieces, 1 - core, axis=1, keepdims=False)
+    return own_core.sum(axis=0) * factor, other_core.sum(axis=0) * factor
 
 
 def gather_hubs(hub_rows):
@@ -112,16 +116,15 @@
     dz_first = (vertex_grad * gate_value * (1.0 + z_first * (1.0 - gate_value))).astype(
         jnp.bfloat16
     )
-    product_first = pair_product(dz_first, agg_first)
+    product_first = pair_product(dz_first, agg_first, 0)
     product_first, new_history = lax.optimization_barrier((product_first, new_history))
     outgoing_first = reduce_in_group(product_first)
 
     hist_halo = hist_slots.reshape(-1, D)[halo_index]
     hub_second = gather_hubs(new_history[owned_hubs])
     agg_second = combine_tiles(new_history, hist_halo, hub_second, tile_cols, tile_vals)
-    outgoing_second = reduce_in_group(pair_product(grad_out, agg_second))
-    both = reduce_over_dom(jnp.concatenate([outgoing_first, outgoing_second], axis=1), rows)
-    grad_first, grad_second = jnp.split(both, 2, axis=0)
+    outgoing_second = reduce_in_group(pair_product(grad_out, agg_second, 1))
+    grad_first, grad_second = reduce_over_dom(outgoing_first, outgoing_second, rows)
     return (new_history, vertex_grad.astype(jnp.bfloat16), grad_first, grad_second)
 
 

time: 237 us -> 230 us (0.970)
  blocking collectives: 28.6 us -> 23.3 us
  waiting for transfers between devices: 95.9 us -> 93.2 us
    all_to_all x1, blocking collectives: 28.6 us -> 23.3 us  [reduce_over_dom(): lax.all_to_all(outgoing, 'dom', split_axis=0, concat_axis=0, tiled=True)]
    all_to_all x2, waiting for transfers between devices: 34 us -> 30.3 us  [gather_hubs(): lax.all_to_all(copies, 'group', split_axis=0, concat_axis=0, tiled=True)]
  transfers between devices with their start and end apart: 8 -> 8, of which waited for: 6 -> 6; matrix products, arithmetic and copies ran while one was open for 19% -> 21% of each run, Pallas kernels for 0% -> 0%
where the time goes in v5:
time: 230 us; the launch traced here: 229 us
  waiting for transfers between devices  93.2 us (41%)
  local copies, waits for them, and re-layouts  43.5 us (19%)
  starting transfers between devices  23.9 us (10%)
  blocking collectives  23.3 us (10%)
  matrix products  18.3 us (8%)
  between operations  14 us (6%)
  other arithmetic  13.1 us (6%)
    reduce_scatter x2, waiting for transfers between devices, reduce_in_group(): lax.psum_scatter(pair.reshape(n_group, -1, width), 'group', scatter_dimen...  42.3 us
    all_to_all x2, waiting for transfers between devices, gather_hubs(): lax.all_to_all(copies, 'group', split_axis=0, concat_axis=0, tiled=True)  30.3 us
    all_to_all x1, blocking collectives, reduce_over_dom(): lax.all_to_all(outgoing, 'dom', split_axis=0, concat_axis=0, tiled=True)  23.3 us
    all_to_all x1, waiting for transfers between devices, on_device(): lax.all_to_all(jnp.stack([feats[routes], history[routes]], axis=1), 'dom'...  13 us
    all_to_all x2, starting transfers between devices, gather_hubs(): lax.all_to_all(copies, 'group', split_axis=0, concat_axis=0, tiled=True)  12.3 us
    all_to_all x1, starting transfers between devices, on_device(): lax.all_to_all(jnp.stack([feats[routes], history[routes]], axis=1), 'dom'...  8.76 us
    ppermute x2, waiting for transfers between devices, pair_product(): return kept + lax.ppermute(sent, 'dom', [(i, i ^ 1) for i in range(n_dom)])  7.57 us
    concatenate x2, other arithmetic, combine_tiles(): source = jnp.concatenate([own_rows, halo_rows, hub_panel], axis=0)  5.56 us
  transfers between devices with their start and end apart: 8, of which 6 were waited for; matrix products, arithmetic and copies ran while one was open for 21% of the time, Pallas kernels for 0%

profile of v5, /device:TPU:1, one launch (start us, length us, event | category | flops | bytes accessed | tf_op | source)
XLA Modules:
  0.0 229.2 jit_solution(14280325380257228003)
XLA Ops:
  8.2 3.8 %gather_fusion.1 = bf16[512,1024]{1,0:T(8,128)(2,1)S(1)} fusion(bf16[128,1024]{1,0:T(8,128)(2,1)} %param.11, s32[1024]{0:T(1024)S(1)} %pad_clamp_fusion.3), kind=kCustom, calls=%fused_computation.1 | custom fusion | bytes 2099200 | tf_op jit(solution)/shard_map/gather | solution.py:106
  12.0 2.8 %gather_fusion = bf16[512,1024]{1,0:T(8,128)(2,1)} fusion(bf16[128,1024]{1,0:T(8,128)(2,1)S(1)} %copy-done.1, s32[1024]{0:T(1024)S(1)} %pad_clamp_fusion.3), kind=kCustom, calls=%fused_computation | custom fusion | bytes 2099200 | tf_op jit(solution)/shard_map/gather | solution.py:106
  14.8 2.8 %pad_maximum_fusion = bf16[32,2,16,1024]{3,2,1,0:T(8,128)(2,1)} fusion(bf16[32,1,16,1024]{3,2,1,0:T(8,128)(2,1)S(1)} %bitcast.87, bf16[32,1,16,1024]{3,2,1,0:T(8,128)(2,1)} %bitcast.88), kind=kLoop, calls=%fused_computation.9 | loop fusion | flops 1048576 | bytes 4194304 | tf_op jit(solution)/shard_map/stack | solution.py:106
  17.6 8.8 %all-to-all-start = ((bf16[32,2,16,1024]{3,2,1,0:T(8,128)(2,1)}), bf16[32,2,16,1024]{3,2,1,0:T(8,128)(2,1)}, u32[]{:S(2)}, u32[]{:S(2)}) async-start(bf16[32,2,16,1024]{3,2,1,0:T(8,128)(2,1)} %pad_maximum_fusion), calls=%async_computation.1 | async-start | bytes 4194304 | tf_op jit(solution)/shard_map/all_to_all | solution.py:105
  26.4 2.5 %convolution_bitcast_fusion = f32[4,128,1024]{1,2,0:T(8,128)} fusion(bf16[128,1024]{1,0:T(8,128)(2,1)S(1)} %copy-done.6, bf16[1024,1024]{1,0:T(8,128)(2,1)S(1)} %copy-done, bf16[1,4,128,128]{3,2,1,0:T(8,128)(2,1)S(1)} %copy-done.5), kind=kOutput, calls=%fused_computation.14 | convolution fusion | flops 402784256 | bytes 4587520 | tf_op jit(solution)/shard_map/rtij,rid->rtjd/dot_general | solution.py:89
  28.9 3.1 %copy.41 = f32[4,128,1024]{2,0,1:T(4,128)} copy(f32[4,128,1024]{1,2,0:T(8,128)} %convolution_bitcast_fusion) | data formatting | bytes 4194304 | tf_op jit(solution)/shard_map/rtij,rid->rtjd/dot_general | solution.py:89
  32.0 4.2 %fusion.7 = f32[7,128,1024]{2,0,1:T(8,128)S(1)} fusion(f32[4,128,1024]{2,0,1:T(4,128)} %copy.41, s32[4]{0:T(128)S(1)} %bitcast.96), kind=kOutput, calls=%fused_computation.43 | convolution fusion | flops 44040220 | bytes 5767184 | tf_op jit(solution)/shard_map/rts,rtjd->sjd/dot_general | solution.py:98
  36.2 1.9 copy-done.2
  41.8 13.0 %all-to-all-done = bf16[32,2,16,1024]{3,2,1,0:T(8,128)(2,1)} async-done(((bf16[32,2,16,1024]{3,2,1,0:T(8,128)(2,1)}), bf16[32,2,16,1024]{3,2,1,0:T(8,128)(2,1)}, u32[]{:S(2)}, u32[]{:S(2)}) %all-to-all-start) | async-done | bytes 2097184 | tf_op jit(solution)/shard_map/all_to_all | solution.py:105
  55.6 8.2 %all-to-all-start.1 = ((bf16[8,32,1024]{2,1,0:T(8,128)(2,1)}), bf16[8,32,1024]{2,1,0:T(8,128)(2,1)}, u32[]{:S(2)}, u32[]{:S(2)}) async-start(bf16[8,32,1024]{2,1,0:T(8,128)(2,1)} %broadcast_in_dim.65), calls=%async_computation.2 | async-start | bytes 1048576 | tf_op jit(solution)/shard_map/all_to_all | solution.py:64
  63.9 2.8 %fusion.12 = (bf16[32,1,16,1024]{3,2,1,0:T(8,128)(2,1)S(1)}, bf16[32,1,16,1024]{3,2,1,0:T(8,128)(2,1)}) fusion(bf16[32,2,16,1024]{3,2,1,0:T(8,128)(2,1)} %all-to-all-done), kind=kLoop, calls=%fused_computation.52 | loop fusion | bytes 4194304 | tf_op jit(solution)/shard_map/slice | solution.py:109
  66.7 4.9 %gather_fusion.2 = bf16[512,1024]{1,0:T(8,128)(2,1)} fusion(bf16[512,1024]{1,0:T(8,128)(2,1)} %bitcast.80, s32[1024]{0:T(1024)S(1)} %pad_clamp_fusion.2), kind=kCustom, calls=%fused_computation.2 | custom fusion | bytes 2099200 | tf_op jit(solution)/shard_map/gather | solution.py:111
  71.5 12.9 %all-to-all-done.1 = bf16[8,32,1024]{2,1,0:T(8,128)(2,1)} async-done(((bf16[8,32,1024]{2,1,0:T(8,128)(2,1)}), bf16[8,32,1024]{2,1,0:T(8,128)(2,1)}, u32[]{:S(2)}, u32[]{:S(2)}) %all-to-all-start.1) | async-done | bytes 524320 | tf_op jit(solution)/shard_map/all_to_all | solution.py:64
  84.5 2.8 %pad_maximum_fusion.1 = bf16[896,1024]{1,0:T(8,128)(2,1)} fusion(bf16[256,1024]{1,0:T(8,128)(2,1)} %bitcast.14, bf16[512,1024]{1,0:T(8,128)(2,1)} %gather_fusion.2, bf16[128,1024]{1,0:T(8,128)(2,1)S(1)} %copy-done.1), kind=kLoop, calls=%fused_computation.10 | loop fusion | flops 5505024 | bytes 3670016 | tf_op jit(solution)/shard_map/concatenate | solution.py:15
  87.3 3.1 %gather_fusion.4 = bf16[4,128,1024]{2,1,0:T(8,128)(2,1)} fusion(bf16[7,128,1024]{2,1,0:T(8,128)(2,1)} %bitcast.85, s32[1024]{0:T(1024)S(1)} %pad_clamp_fusion), kind=kCustom, calls=%fused_computation.4 | custom fusion | bytes 2097168 | tf_op jit(solution)/shard_map/gather | solution.py:17
  90.4 2.4 %fusion = bf16[1024,128]{1,0:T(8,128)(2,1)} fusion(bf16[4,128,1024]{2,1,0:T(8,128)(2,1)} %gather_fusion.4, bf16[1,4,128,128]{3,2,1,0:T(8,128)(2,1)S(1)} %copy-done.5), kind=kOutput, calls=%fused_computation.17 | convolution fusion | flops 134348800 | bytes 1441792 | tf_op jit(solution)/shard_map/rtij,rtjd->rid/dot_general | solution.py:18
  92.8 3.0 %scatter_fusion = f32[128,1024]{1,0:T(8,128)} fusion(f32[128,1024]{1,0:T(8,128)} %bitcast.83, s32[32]{0:T(128)S(1)} %fusion.10, f32[32,1024]{1,0:T(8,128)} %reduce-scatter.4.cloned.1.call-done), kind=kCustom, calls=%fused_computation.8 | custom fusion | flops 32768 | bytes 393344 | tf_op jit(solution)/shard_map/scatter-add | solution.py:103
  95.8 3.3 %fusion.13 = (bf16[128,1024]{1,0:T(8,128)(2,1)}, bf16[128,1024]{1,0:T(8,128)(2,1)}, bf16[128,1024]{1,0:T(8,128)(2,1)S(1)}) fusion(f32[128,1024]{1,0:T(8,128)} %scatter_fusion, bf16[1024,128]{1,0:T(8,128)(2,1)} %fusion, bf16[1024,1024]{1,0:T(8,128)(2,1)} %param.13), kind=kOutput, calls=%fused_computation.53 | convolution fusion | flops 270008320 | bytes 3670016 | tf_op jit(solution)/shard_map/dot_general | solution.py:113
  99.1 1.9 copy.47
  103.5 2.2 collective-permute-start
  105.7 3.8 %collective-permute-done = f32[512,1024]{1,0:T(8,128)S(1)} collective-permute-done((f32[512,1024]{1,0:T(8,128)S(1)}, f32[512,1024]{1,0:T(8,128)S(1)}, u32[]{:S(2)}, u32[]{:S(2)}) %collective-permute-start) | collective-permute-done | bytes 2097184 | tf_op jit(solution)/shard_map/ppermute | solution.py:37
  109.4 1.8 convolution_add_fusion.1
  114.2 4.1 %all-to-all-start.2 = ((bf16[8,32,1024]{2,1,0:T(8,128)(2,1)}), bf16[8,32,1024]{2,1,0:T(8,128)(2,1)}, u32[]{:S(2)}, u32[]{:S(2)}) async-start(bf16[8,32,1024]{2,1,0:T(8,128)(2,1)} %broadcast_in_dim.73), calls=%async_computation.4 | async-start | bytes 1048576 | tf_op jit(solution)/shard_map/all_to_all | solution.py:64
  118.4 1.8 copy.48
  120.2 1.8 constant_dynamic-slice_fusion.1
  122.0 2.8 %gather_fusion.5 = bf16[512,1024]{1,0:T(8,128)(2,1)} fusion(bf16[512,1024]{1,0:T(8,128)(2,1)S(1)} %bitcast.79, s32[1024]{0:T(1024)S(1)} %pad_clamp_fusion.2), kind=kCustom, calls=%fused_computation.5 | custom fusion | bytes 2099200 | tf_op jit(solution)/shard_map/gather | solution.py:123
  124.8 17.4 %all-to-all-done.2 = bf16[8,32,1024]{2,1,0:T(8,128)(2,1)} async-done(((bf16[8,32,1024]{2,1,0:T(8,128)(2,1)}), bf16[8,32,1024]{2,1,0:T(8,128)(2,1)}, u32[]{:S(2)}, u32[]{:S(2)}) %all-to-all-start.2) | async-done | bytes 524320 | tf_op jit(solution)/shard_map/all_to_all | solution.py:64
  142.1 2.8 %pad_maximum_fusion.2 = bf16[896,1024]{1,0:T(8,128)(2,1)} fusion(bf16[256,1024]{1,0:T(8,128)(2,1)} %bitcast.26, bf16[512,1024]{1,0:T(8,128)(2,1)} %gather_fusion.5, bf16[128,1024]{1,0:T(8,128)(2,1)S(1)} %get-tuple-element.2), kind=kLoop, calls=%fused_computation.11 | loop fusion | flops 5505024 | bytes 3670016 | tf_op jit(solution)/shard_map/concatenate | solution.py:15
  144.9 2.2 gather_fusion.7
  148.5 3.8 %collective-permute-done.1 = f32[512,1024]{1,0:T(8,128)S(1)} collective-permute-done((f32[512,1024]{1,0:T(8,128)S(1)}, f32[512,1024]{1,0:T(8,128)S(1)}, u32[]{:S(2)}, u32[]{:S(2)}) %collective-permute-start.1) | collective-permute-done | bytes 2097184 | tf_op jit(solution)/shard_map/ppermute | solution.py:37
  155.2 42.3 %reduce-scatter.8.cloned.1.call-done = f32[1,64,1024]{2,1,0:T(8,128)} async-done(((f32[8,64,1024]{2,1,0:T(8,128)}), f32[1,64,1024]{2,1,0:T(8,128)}) %reduce-scatter.8.cloned.1.call-update) | async-done | bytes 262160 | tf_op jit(solution)/shard_map/reduce_scatter | solution.py:43
  198.7 23.3 %all_to_all.20 = f32[32,4,1024]{2,1,0:T(4,128)S(1)} all-to-all(f32[32,4,1024]{2,1,0:T(4,128)S(1)} %bitcast_select_fusion), channel_id=1, replica_groups=mesh['group'=8,'dom'=32] {'dom'}, dimensions={0} | all-to-all | bytes 1048576 | tf_op jit(solution)/shard_map/all_to_all | solution.py:54
  (64 shorter events, 17.2 us)
Async XLA Ops:
  7.2 19.2 %copy-start = (bf16[1024,1024]{1,0:T(8,128)(2,1)S(1)}, bf16[1024,1024]{1,0:T(8,128)(2,1)}, u32[]{:S(2)}) copy-start(bf16[1024,1024]{1,0:T(8,128)(2,1)} %param.14) | copy-start | bytes 6291460
  8.2 3.8 %copy-start.1 = (bf16[128,1024]{1,0:T(8,128)(2,1)S(1)}, bf16[128,1024]{1,0:T(8,128)(2,1)}, u32[]{:S(2)}) copy-start(bf16[128,1024]{1,0:T(8,128)(2,1)} %param.10) | copy-start | bytes 786436
  17.5 8.8 %copy-start.5 = (bf16[1,4,128,128]{3,2,1,0:T(8,128)(2,1)S(1)}, bf16[1,4,128,128]{3,2,1,0:T(8,128)(2,1)}, u32[]{:S(2)}) copy-start(bf16[1,4,128,128]{3,2,1,0:T(8,128)(2,1)} %param.19) | copy-start | bytes 393220
  17.6 8.8 %copy-start.6 = (bf16[128,1024]{1,0:T(8,128)(2,1)S(1)}, bf16[128,1024]{1,0:T(8,128)(2,1)}, u32[]{:S(2)}) copy-start(bf16[128,1024]{1,0:T(8,128)(2,1)} %param.12) | copy-start | bytes 786436
  17.6 37.2 %all-to-all-start = ((bf16[32,2,16,1024]{3,2,1,0:T(8,128)(2,1)}), bf16[32,2,16,1024]{3,2,1,0:T(8,128)(2,1)}, u32[]{:S(2)}, u32[]{:S(2)}) async-start(bf16[32,2,16,1024]{3,2,1,0:T(8,128)(2,1)} %pad_maximum_fusion), calls=%async_computation.1 | async-start | bytes 4194304 | tf_op jit(solution)/shard_map/all_to_all | solution.py:105
  26.3 66.4 %reduce-scatter.4.cloned.1.call-start = ((), (), s32[]{:S(2)}) async-start(), calls=%async_computation.7 | async-start | bytes 1179648 | tf_op jit(solution)/shard_map/reduce_scatter | solution.py:102
  28.9 3.1 %copy-start.10 = (s32[1,4]{1,0:T(1,128)S(1)}, s32[1,4]{1,0:T(1,128)}, u32[]{:S(2)}) copy-start(s32[1,4]{1,0:T(1,128)} %param.18) | copy-start | bytes 52
  36.2 2.0 copy-start.2
  38.7 1.4 slice-start
  40.1 1.0 copy-start.11
  40.2 23.6 %copy-start.9 = (s32[512]{0:T(512)S(1)}, s32[512]{0:T(512)}, u32[]{:S(2)}) copy-start(s32[512]{0:T(512)} %param.16) | copy-start | bytes 6148
  55.6 28.9 %all-to-all-start.1 = ((bf16[8,32,1024]{2,1,0:T(8,128)(2,1)}), bf16[8,32,1024]{2,1,0:T(8,128)(2,1)}, u32[]{:S(2)}, u32[]{:S(2)}) async-start(bf16[8,32,1024]{2,1,0:T(8,128)(2,1)} %broadcast_in_dim.65), calls=%async_computation.2 | async-start | bytes 1048576 | tf_op jit(solution)/shard_map/all_to_all | solution.py:64
  63.8 90.4 %reduce-scatter.6.cloned.1.call-start = ((), (), s32[]{:S(2)}) async-start(), calls=%async_computation.8 | async-start | bytes 2359296 | tf_op jit(solution)/shard_map/reduce_scatter | solution.py:43
  99.1 43.0 %copy-start.3 = (bf16[128,1024]{1,0:T(8,128)(2,1)}, bf16[128,1024]{1,0:T(8,128)(2,1)S(1)}, u32[]{:S(2)}) copy-start(bf16[128,1024]{1,0:T(8,128)(2,1)S(1)} %get-tuple-element.2) | copy-start | bytes 786436
  101.0 8.5 %copy-start.4 = (bf16[1024,128]{1,0:T(8,128)(2,1)S(1)}, bf16[1024,128]{1,0:T(8,128)(2,1)}, u32[]{:S(2)}) copy-start(bf16[1024,128]{1,0:T(8,128)(2,1)} %fusion) | copy-start | bytes 786436
  103.5 6.0 %collective-permute-start = (f32[512,1024]{1,0:T(8,128)S(1)}, f32[512,1024]{1,0:T(8,128)S(1)}, u32[]{:S(2)}, u32[]{:S(2)}) collective-permute-start(f32[512,1024]{1,0:T(8,128)S(1)} %fusion.14), channel_id=1, source_target_pairs={{0,1},{1,0},{2,3},{3,2},{4,5},{5,4},{6,7},{7,6},{8,9},{9,8},{10,11... | collective-permute-start | bytes 6291464 | tf_op jit(solution)/shard_map/ppermute | solution.py:37
  114.2 27.9 %all-to-all-start.2 = ((bf16[8,32,1024]{2,1,0:T(8,128)(2,1)}), bf16[8,32,1024]{2,1,0:T(8,128)(2,1)}, u32[]{:S(2)}, u32[]{:S(2)}) async-start(bf16[8,32,1024]{2,1,0:T(8,128)(2,1)} %broadcast_in_dim.73), calls=%async_computation.4 | async-start | bytes 1048576 | tf_op jit(solution)/shard_map/all_to_all | solution.py:64
  118.3 79.2 %reduce-scatter.8.cloned.1.call-start = ((), (), s32[]{:S(2)}) async-start(), calls=%async_computation.9 | async-start | bytes 2359296 | tf_op jit(solution)/shard_map/reduce_scatter | solution.py:43
  144.9 2.7 %copy-start.8 = (bf16[128,8,16,1,4]{0,4,3,2,1:T(4,128)(2,1)S(1)}, bf16[128,8,16,1,4]{0,4,3,2,1:T(4,128)(2,1)}, u32[]{:S(2)}) copy-start(bf16[128,8,16,1,4]{0,4,3,2,1:T(4,128)(2,1)} %get-tuple-element.16) | copy-start | bytes 393220
  147.1 5.2 %copy-start.7 = (bf16[128,8,16,1,4]{0,4,3,2,1:T(4,128)(2,1)S(1)}, bf16[128,8,16,1,4]{0,4,3,2,1:T(4,128)(2,1)}, u32[]{:S(2)}) copy-start(bf16[128,8,16,1,4]{0,4,3,2,1:T(4,128)(2,1)} %get-tuple-element.15) | copy-start | bytes 393220
  148.0 4.3 %collective-permute-start.1 = (f32[512,1024]{1,0:T(8,128)S(1)}, f32[512,1024]{1,0:T(8,128)S(1)}, u32[]{:S(2)}, u32[]{:S(2)}) collective-permute-start(f32[512,1024]{1,0:T(8,128)S(1)} %fusion.15), channel_id=1, source_target_pairs={{0,1},{1,0},{2,3},{3,2},{4,5},{5,4},{6,7},{7,6},{8,9},{9,8},{10,11... | collective-permute-start | bytes 6291464 | tf_op jit(solution)/shard_map/ppermute | solution.py:37
Sparse Core Ops, SparseCore 0:
  40.3 42.7 reduce-scatter.3
  111.4 40.6 reduce-scatter.5
  154.6 42.8 reduce-scatter.7

commit v6 on v5

--- a/solution.py
+++ b/solution.py
@@ -89,7 +89,7 @@
     tile_terms = jnp.einsum(
         "rtij,rid->rtjd",
         tile_vals,
-        agg_grad.reshape(-1, TILE, D),
+        jnp.concatenate([agg_grad, grad_out], axis=1).reshape(-1, TILE, 2 * D),
         preferred_element_type=jnp.float32,
     )
     selector = (
@@ -97,18 +97,19 @@
     ).astype(jnp.float32)
     spread = jnp.einsum(
         "rts,rtjd->sjd", selector, tile_terms, precision=lax.Precision.HIGHEST
-    ).reshape(-1, D)
-    own_grad = spread[:V_DEV]
-    hub_grad = lax.psum_scatter(spread[V_DEV + HALO :], "group", scatter_dimension=0, tiled=True)
-    vertex_grad = own_grad.at[owned_hubs].add(hub_grad)
+    ).reshape(-1, 2 * D)
+    hub_sums = lax.psum_scatter(spread[V_DEV + HALO :], "group", scatter_dimension=0, tiled=True)
+    own_terms = spread[:V_DEV].at[owned_hubs].add(hub_sums)
+    vertex_grad = own_terms[:, :D]
+    own_weights = own_terms[:, D:]
+    halo_weights = spread[V_DEV : V_DEV + HALO, D:]
 
     both_slots = lax.all_to_all(
         jnp.stack([feats[routes], history[routes]], axis=1), "dom", split_axis=0, concat_axis=0, tiled=True
     )
-    feat_slots = both_slots[:, 0]
-    hist_slots = both_slots[:, 1]
+    feat_halo = both_slots[:, 0].reshape(-1, D)[halo_index]
+    hist_halo = both_slots[:, 1].reshape(-1, D)[halo_index]
     hub_first = gather_hubs(feats[owned_hubs])
-    feat_halo = feat_slots.reshape(-1, D)[halo_index]
     agg_first = combine_tiles(feats, feat_halo, hub_first, tile_cols, tile_vals)
     z_first = jnp.dot(agg_first, w_first, preferred_element_type=jnp.float32)
     new_history = jax.nn.silu(z_first).astype(jnp.bfloat16)
@@ -116,14 +117,19 @@
     dz_first = (vertex_grad * gate_value * (1.0 + z_first * (1.0 - gate_value))).astype(
         jnp.bfloat16
     )
-    product_first = pair_product(dz_first, agg_first, 0)
-    product_first, new_history = lax.optimization_barrier((product_first, new_history))
-    outgoing_first = reduce_in_group(product_first)
+    outgoing_first = reduce_in_group(pair_product(dz_first, agg_first, 0))
 
-    hist_halo = hist_slots.reshape(-1, D)[halo_index]
-    hub_second = gather_hubs(new_history[owned_hubs])
-    agg_second = combine_tiles(new_history, hist_halo, hub_second, tile_cols, tile_vals)
-    outgoing_second = reduce_in_group(pair_product(grad_out, agg_second, 1))
+    weights = jnp.concatenate([own_weights, halo_weights], axis=0)
+    weights_high = weights.astype(jnp.bfloat16)
+    weights_low = (weights - weights_high.astype(jnp.float32)).astype(jnp.bfloat16)
+    sources = jnp.concatenate([new_history, hist_halo], axis=0)
+    outgoing_second = reduce_in_group(
+        pair_product(
+            jnp.concatenate([weights_high, weights_low], axis=0),
+            jnp.concatenate([sources, sources], axis=0),
+            1,
+        )
+    )
     grad_first, grad_second = reduce_over_dom(outgoing_first, outgoing_second, rows)
     return (new_history, vertex_grad.astype(jnp.bfloat16), grad_first, grad_second)
 

time: 230 us -> 253 us (1.10)
  local copies, waits for them, and re-layouts: 43.5 us -> 70.1 us
  blocking collectives: 23.3 us -> 0 us
  matrix products: 18.3 us -> 28.1 us
  starting transfers between devices: 23.9 us -> 29.8 us
  other arithmetic: 13.1 us -> 16.7 us
    all_to_all x2 -> x1, waiting for transfers between devices: 30.3 us -> 5.28 us  [gather_hubs(): lax.all_to_all(copies, 'group', split_axis=0, concat_axis=0, tiled=True)]
    all_to_all x1 -> x0, blocking collectives: 23.3 us -> none  [reduce_over_dom(): lax.all_to_all(outgoing, 'dom', split_axis=0, concat_axis=0, tiled=True)]
    reduce_scatter x2, waiting for transfers between devices: 42.3 us -> 64.6 us  [reduce_in_group(): lax.psum_scatter(pair.reshape(n_group, -1, width), 'group', scatter_dimen...]
    dot_general x1 -> x2, local copies, waits for them, and re-layouts: 3.08 us -> 16.2 us  [the longest x1 10.7 us: on_device(): jnp.einsum('rts,rtjd->sjd', selector, tile_terms, precision=lax.Precision...]
    all_to_all x0 -> x1, starting transfers between devices: none -> 11.8 us  [reduce_over_dom(): lax.all_to_all(outgoing, 'dom', split_axis=0, concat_axis=0, tiled=True)]
    slice x3 -> x6, local copies, waits for them, and re-layouts: 2.81 us -> 13.9 us  [the longest x2 6.11 us: on_device(): halo_weights = spread[V_DEV:V_DEV + HALO, D:]]
    all_to_all x0 -> x1, waiting for transfers between devices: none -> 10.9 us  [reduce_over_dom(): lax.all_to_all(outgoing, 'dom', split_axis=0, concat_axis=0, tiled=True)]
    dot_general x4, matrix products: 5.36 us -> 12.8 us  [weight_product(): lax.dot_general(left_rows, right_rows, (((0,), (0,)), ((), ())), preferre...]
  transfers between devices with their start and end apart: 8 -> 8, of which waited for: 6 -> 7; matrix products, arithmetic and copies ran while one was open for 21% -> 24% of each run, Pallas kernels for 0% -> 0%
where the time goes in v6:
time: 253 us; the launch traced here: 252 us
  waiting for transfers between devices  93.4 us (37%)
  local copies, waits for them, and re-layouts  70.1 us (28%)
  starting transfers between devices  29.8 us (12%)
  matrix products  28.1 us (11%)
  other arithmetic  16.7 us (7%)
  between operations  14 us (6%)
    reduce_scatter x2, waiting for transfers between devices, reduce_in_group(): lax.psum_scatter(pair.reshape(n_group, -1, width), 'group', scatter_dimen...  64.6 us
    dot_general x4, matrix products, weight_product(): lax.dot_general(left_rows, right_rows, (((0,), (0,)), ((), ())), preferre...  12.8 us
    all_to_all x1, starting transfers between devices, reduce_over_dom(): lax.all_to_all(outgoing, 'dom', split_axis=0, concat_axis=0, tiled=True)  11.8 us
    all_to_all x1, waiting for transfers between devices, reduce_over_dom(): lax.all_to_all(outgoing, 'dom', split_axis=0, concat_axis=0, tiled=True)  10.9 us
    dot_general x1, local copies, waits for them, and re-layouts, on_device(): jnp.einsum('rts,rtjd->sjd', selector, tile_terms, precision=lax.Precision...  10.7 us
    all_to_all x1, starting transfers between devices, on_device(): lax.all_to_all(jnp.stack([feats[routes], history[routes]], axis=1), 'dom'...  8.65 us
    all_to_all x1, starting transfers between devices, gather_hubs(): lax.all_to_all(copies, 'group', split_axis=0, concat_axis=0, tiled=True)  8.18 us
    all_to_all x1, waiting for transfers between devices, on_device(): lax.all_to_all(jnp.stack([feats[routes], history[routes]], axis=1), 'dom'...  8.03 us
  transfers between devices with their start and end apart: 8, of which 7 were waited for; matrix products, arithmetic and copies ran while one was open for 24% of the time, Pallas kernels for 0%

profile of v6, /device:TPU:1, one launch (start us, length us, event | category | flops | bytes accessed | tf_op | source)
XLA Modules:
  0.0 252.1 jit_solution(16296429069402172194)
XLA Ops:
  7.2 2.6 %convolution_convert_fusion = bf16[128,1024]{1,0:T(8,128)(2,1)S(1)} fusion(bf16[128,1024]{1,0:T(8,128)(2,1)} %param.12, bf16[1024,1024]{1,0:T(8,128)(2,1)} %param.14), kind=kOutput, calls=%fused_computation.24 | convolution fusion | flops 268566528 | bytes 2621440 | tf_op jit(solution)/shard_map/dot_general | solution.py:84
  9.9 2.7 %convolution_bitcast_fusion = f32[4,128,2048]{1,2,0:T(8,128)} fusion(bf16[128,1024]{1,0:T(8,128)(2,1)S(1)} %copy-done.8, bf16[128,1024]{1,0:T(8,128)(2,1)S(1)} %convolution_convert_fusion, bf16[1,4,128,128]{3,2,1,0:T(8,128)(2,1)S(1)} %copy-done.9), kind=kOutput, calls=%fused_computation.7 | convolution fusion | flops 269484032 | bytes 4849664 | tf_op jit(solution)/shard_map/rtij,rid->rtjd/dot_general | solution.py:89
  12.6 5.5 %copy.53 = f32[4,128,2048]{2,0,1:T(4,128)} copy(f32[4,128,2048]{1,2,0:T(8,128)} %convolution_bitcast_fusion) | data formatting | bytes 8388608 | tf_op jit(solution)/shard_map/rtij,rid->rtjd/dot_general | solution.py:89
  18.1 6.7 %fusion.10 = f32[7,128,2048]{2,0,1:T(8,128)S(1)} fusion(f32[4,128,2048]{2,0,1:T(4,128)} %copy.53, s32[4]{0:T(128)S(1)} %bitcast.85), kind=kOutput, calls=%fused_computation.53 | convolution fusion | flops 88080416 | bytes 11534352 | tf_op jit(solution)/shard_map/rts,rtjd->sjd/dot_general | solution.py:98
  28.1 2.5 %copy.55 = f32[2,128,2048]{2,1,0:T(8,128)} copy(f32[2,128,2048]{2,0,1:T(2,128)S(1)} %slice.50) | data formatting | bytes 4194304 | tf_op jit(solution)/shard_map/slice | solution.py:101
  31.6 2.8 %gather_fusion.1 = bf16[512,1024]{1,0:T(8,128)(2,1)} fusion(bf16[128,1024]{1,0:T(8,128)(2,1)S(1)} %copy-done.2, s32[1024]{0:T(1024)S(1)} %pad_clamp_fusion.3), kind=kCustom, calls=%fused_computation.1 | custom fusion | bytes 2099200 | tf_op jit(solution)/shard_map/gather | solution.py:108
  34.4 2.8 %gather_fusion = bf16[512,1024]{1,0:T(8,128)(2,1)} fusion(bf16[128,1024]{1,0:T(8,128)(2,1)S(1)} %copy-done.1, s32[1024]{0:T(1024)S(1)} %pad_clamp_fusion.3), kind=kCustom, calls=%fused_computation | custom fusion | bytes 2099200 | tf_op jit(solution)/shard_map/gather | solution.py:108
  37.2 2.8 %pad_maximum_fusion.2 = bf16[32,2,16,1024]{3,2,1,0:T(8,128)(2,1)} fusion(bf16[32,1,16,1024]{3,2,1,0:T(8,128)(2,1)S(1)} %bitcast.79, bf16[32,1,16,1024]{3,2,1,0:T(8,128)(2,1)} %bitcast.80), kind=kLoop, calls=%fused_computation.15 | loop fusion | flops 1048576 | bytes 4194304 | tf_op jit(solution)/shard_map/stack | solution.py:108
  40.0 8.6 %all-to-all-start = ((bf16[32,2,16,1024]{3,2,1,0:T(8,128)(2,1)}), bf16[32,2,16,1024]{3,2,1,0:T(8,128)(2,1)}, u32[]{:S(2)}, u32[]{:S(2)}) async-start(bf16[32,2,16,1024]{3,2,1,0:T(8,128)(2,1)} %pad_maximum_fusion.2), calls=%async_computation | async-start | bytes 4194304 | tf_op jit(solution)/shard_map/all_to_all | solution.py:107
  48.7 10.7 %copy.54 = f32[7,128,2048]{2,1,0:T(8,128)} copy(f32[7,128,2048]{2,0,1:T(8,128)} %copy-done.3) | data formatting | bytes 14680064 | tf_op jit(solution)/shard_map/rts,rtjd->sjd/dot_general | solution.py:98
  60.0 3.2 %slice.53 = f32[512,1024]{1,0:T(8,128)} slice(f32[896,2048]{1,0:T(8,128)} %bitcast.73), slice={[128:640], [1024:2048]} | slice | bytes 4194304 | tf_op jit(solution)/shard_map/slice | solution.py:105
  63.2 2.9 %copy.59 = f32[512,1024]{0,1:T(8,128)} copy(f32[512,1024]{1,0:T(8,128)} %slice.53) | data formatting | bytes 4194304 | tf_op jit(solution)/shard_map/slice | solution.py:105
  66.1 2.9 %concatenate.27 = f32[512,8,16,2,4]{0,4,3,2,1:T(4,128)} reshape(f32[512,1024]{0,1:T(8,128)} %copy.59) | data formatting | bytes 4194304 | tf_op jit(solution)/shard_map/concatenate | solution.py:122
  69.0 8.0 %all-to-all-done = bf16[32,2,16,1024]{3,2,1,0:T(8,128)(2,1)} async-done(((bf16[32,2,16,1024]{3,2,1,0:T(8,128)(2,1)}), bf16[32,2,16,1024]{3,2,1,0:T(8,128)(2,1)}, u32[]{:S(2)}, u32[]{:S(2)}) %all-to-all-start) | async-done | bytes 2097184 | tf_op jit(solution)/shard_map/all_to_all | solution.py:107
  77.9 8.2 %all-to-all-start.1 = ((bf16[8,32,1024]{2,1,0:T(8,128)(2,1)}), bf16[8,32,1024]{2,1,0:T(8,128)(2,1)}, u32[]{:S(2)}, u32[]{:S(2)}) async-start(bf16[8,32,1024]{2,1,0:T(8,128)(2,1)} %broadcast_in_dim.57), calls=%async_computation.1 | async-start | bytes 1048576 | tf_op jit(solution)/shard_map/all_to_all | solution.py:64
  86.1 2.3 slice_bitcast_fusion
  88.4 2.8 %fusion.18 = (bf16[32,1,16,1024]{3,2,1,0:T(8,128)(2,1)S(1)}, bf16[32,1,16,1024]{3,2,1,0:T(8,128)(2,1)}) fusion(bf16[32,2,16,1024]{3,2,1,0:T(8,128)(2,1)} %all-to-all-done), kind=kLoop, calls=%fused_computation.61 | loop fusion | bytes 4194304 | tf_op jit(solution)/shard_map/slice | solution.py:111
  91.2 4.8 %gather_fusion.2 = bf16[512,1024]{1,0:T(8,128)(2,1)} fusion(bf16[512,1024]{1,0:T(8,128)(2,1)} %bitcast.72, s32[1024]{0:T(1024)S(1)} %pad_clamp_fusion.2), kind=kCustom, calls=%fused_computation.2 | custom fusion | bytes 2099200 | tf_op jit(solution)/shard_map/gather | solution.py:110
  96.0 2.8 %gather_fusion.5 = bf16[512,1024]{1,0:T(8,128)(2,1)} fusion(bf16[512,1024]{1,0:T(8,128)(2,1)S(1)} %bitcast.71, s32[1024]{0:T(1024)S(1)} %pad_clamp_fusion.2), kind=kCustom, calls=%fused_computation.5 | custom fusion | bytes 2099200 | tf_op jit(solution)/shard_map/gather | solution.py:111
  98.8 5.3 %all-to-all-done.1 = bf16[8,32,1024]{2,1,0:T(8,128)(2,1)} async-done(((bf16[8,32,1024]{2,1,0:T(8,128)(2,1)}), bf16[8,32,1024]{2,1,0:T(8,128)(2,1)}, u32[]{:S(2)}, u32[]{:S(2)}) %all-to-all-start.1) | async-done | bytes 524320 | tf_op jit(solution)/shard_map/all_to_all | solution.py:64
  104.1 2.8 %pad_maximum_fusion.3 = bf16[896,1024]{1,0:T(8,128)(2,1)} fusion(bf16[256,1024]{1,0:T(8,128)(2,1)} %bitcast.8, bf16[512,1024]{1,0:T(8,128)(2,1)} %gather_fusion.2, bf16[128,1024]{1,0:T(8,128)(2,1)S(1)} %copy-done.1), kind=kLoop, calls=%fused_computation.16 | loop fusion | flops 5505024 | bytes 3670016 | tf_op jit(solution)/shard_map/concatenate | solution.py:15
  106.8 3.2 %gather_fusion.4 = bf16[4,128,1024]{2,1,0:T(8,128)(2,1)} fusion(bf16[7,128,1024]{2,1,0:T(8,128)(2,1)} %bitcast.78, s32[1024]{0:T(1024)S(1)} %pad_clamp_fusion), kind=kCustom, calls=%fused_computation.4 | custom fusion | bytes 2097168 | tf_op jit(solution)/shard_map/gather | solution.py:17
  117.5 2.5 fusion
  123.0 3.4 %reshape.182 = bf16[1280,512]{0,1:T(8,128)(2,1)} reshape(bf16[1280,8,16,1,4]{0,4,3,2,1:T(4,128)(2,1)} %get-tuple-element.7) | data formatting | bytes 2621440 | tf_op jit(solution)/shard_map/reshape | solution.py:36
  126.3 4.9 %fusion.4 = f32[512,1024]{1,0:T(8,128)} fusion(bf16[1280,512]{0,1:T(8,128)(2,1)} %reshape.182, bf16[512,1024]{1,0:T(8,128)(2,1)} %gather_fusion.5, bf16[128,1024]{1,0:T(8,128)(2,1)} %get-tuple-element.12), kind=kOutput, calls=%fused_computation.25 | convolution fusion | flops 1352663040 | bytes 4718592 | tf_op jit(solution)/shard_map/dot_general | solution.py:23
  131.8 3.4 %reshape.181 = bf16[1280,512]{0,1:T(8,128)(2,1)} reshape(bf16[1280,8,16,1,4]{0,4,3,2,1:T(4,128)(2,1)} %get-tuple-element.6) | data formatting | bytes 2621440 | tf_op jit(solution)/shard_map/reshape | solution.py:35
  135.9 5.7 %convolution_add_fusion.1 = f32[512,1024]{1,0:T(8,128)} fusion(f32[512,1024]{1,0:T(8,128)} %collective-permute-done.1, bf16[1280,512]{0,1:T(8,128)(2,1)} %reshape.181, bf16[512,1024]{1,0:T(8,128)(2,1)} %gather_fusion.5, bf16[128,1024]{1,0:T(8,128)(2,1)} %get-tuple-element.12), kind=kOutput, calls=%fused_computation.19 | convolution fusion | flops 1353187328 | bytes 6815744 | tf_op jit(solution)/shard_map/dot_general | solution.py:23
  145.4 3.8 %collective-permute-done = f32[512,1024]{1,0:T(8,128)S(1)} collective-permute-done((f32[512,1024]{1,0:T(8,128)S(1)}, f32[512,1024]{1,0:T(8,128)S(1)}, u32[]{:S(2)}, u32[]{:S(2)}) %collective-permute-start) | collective-permute-done | bytes 2097184 | tf_op jit(solution)/shard_map/ppermute | solution.py:37
  151.1 21.7 %reduce-scatter.8.cloned.1.call-done = f32[1,64,1024]{2,1,0:T(8,128)} async-done(((f32[8,64,1024]{2,1,0:T(8,128)}), f32[1,64,1024]{2,1,0:T(8,128)}) %reduce-scatter.8.cloned.1.call-update) | async-done | bytes 262160 | tf_op jit(solution)/shard_map/reduce_scatter | solution.py:43
  173.9 42.9 %reduce-scatter.6.cloned.1.call-done = f32[1,64,1024]{2,1,0:T(8,128)} async-done(((f32[8,64,1024]{2,1,0:T(8,128)}), f32[1,64,1024]{2,1,0:T(8,128)}) %reduce-scatter.6.cloned.1.call-update) | async-done | bytes 262160 | tf_op jit(solution)/shard_map/reduce_scatter | solution.py:43
  220.4 11.8 %all-to-all-start.2 = ((f32[32,4,1024]{2,1,0:T(4,128)}), f32[32,4,1024]{2,1,0:T(4,128)}, u32[]{:S(2)}, u32[]{:S(2)}) async-start(f32[32,4,1024]{2,1,0:T(4,128)} %bitcast_select_fusion), calls=%async_computation.5 | async-start | bytes 1048576 | tf_op jit(solution)/shard_map/all_to_all | solution.py:54
  233.0 10.9 %all-to-all-done.2 = f32[32,4,1024]{2,1,0:T(4,128)} async-done(((f32[32,4,1024]{2,1,0:T(4,128)}), f32[32,4,1024]{2,1,0:T(4,128)}, u32[]{:S(2)}, u32[]{:S(2)}) %all-to-all-start.2) | async-done | bytes 524320 | tf_op jit(solution)/shard_map/all_to_all | solution.py:54
  (70 shorter events, 30.3 us)
Async XLA Ops:
  7.2 106.6 %copy-start = (bf16[1024,1024]{1,0:T(8,128)(2,1)S(1)}, bf16[1024,1024]{1,0:T(8,128)(2,1)}, u32[]{:S(2)}) copy-start(bf16[1024,1024]{1,0:T(8,128)(2,1)} %param.13) | copy-start | bytes 6291460
  7.2 2.7 %copy-start.8 = (bf16[128,1024]{1,0:T(8,128)(2,1)S(1)}, bf16[128,1024]{1,0:T(8,128)(2,1)}, u32[]{:S(2)}) copy-start(bf16[128,1024]{1,0:T(8,128)(2,1)} %param.12) | copy-start | bytes 786436
  7.2 2.7 %copy-start.9 = (bf16[1,4,128,128]{3,2,1,0:T(8,128)(2,1)S(1)}, bf16[1,4,128,128]{3,2,1,0:T(8,128)(2,1)}, u32[]{:S(2)}) copy-start(bf16[1,4,128,128]{3,2,1,0:T(8,128)(2,1)} %param.19) | copy-start | bytes 393220
  7.2 104.6 %reduce-scatter.4.cloned.1.call-start = ((), (), s32[]{:S(2)}) async-start(), calls=%async_computation.6 | async-start | bytes 2359296 | tf_op jit(solution)/shard_map/reduce_scatter | solution.py:101
  12.6 5.5 %copy-start.12 = (s32[1,4]{1,0:T(1,128)S(1)}, s32[1,4]{1,0:T(1,128)}, u32[]{:S(2)}) copy-start(s32[1,4]{1,0:T(1,128)} %param.18) | copy-start | bytes 52
  24.9 3.3 %copy-start.3 = (f32[7,128,2048]{2,0,1:T(8,128)}, f32[7,128,2048]{2,0,1:T(8,128)S(1)}, u32[]{:S(2)}) copy-start(f32[7,128,2048]{2,0,1:T(8,128)S(1)} %fusion.10) | copy-start | bytes 22020100
  30.6 0.7 copy-start.10
  30.6 1.0 copy-start.2
  31.6 2.8 %copy-start.1 = (bf16[128,1024]{1,0:T(8,128)(2,1)S(1)}, bf16[128,1024]{1,0:T(8,128)(2,1)}, u32[]{:S(2)}) copy-start(bf16[128,1024]{1,0:T(8,128)(2,1)} %param.10) | copy-start | bytes 786436
  34.4 2.8 %copy-start.7 = (bf16[512,1024]{1,0:T(8,128)(2,1)S(1)}, bf16[512,1024]{1,0:T(8,128)(2,1)}, u32[]{:S(2)}) copy-start(bf16[512,1024]{1,0:T(8,128)(2,1)} %gather_fusion.1) | copy-start | bytes 3145732
  40.0 37.0 %all-to-all-start = ((bf16[32,2,16,1024]{3,2,1,0:T(8,128)(2,1)}), bf16[32,2,16,1024]{3,2,1,0:T(8,128)(2,1)}, u32[]{:S(2)}, u32[]{:S(2)}) async-start(bf16[32,2,16,1024]{3,2,1,0:T(8,128)(2,1)} %pad_maximum_fusion.2), calls=%async_computation | async-start | bytes 4194304 | tf_op jit(solution)/shard_map/all_to_all | solution.py:107
  48.6 10.7 %copy-start.13 = (s32[1,32]{1,0:T(1,128)S(1)}, s32[1,32]{1,0:T(1,128)}, u32[]{:S(2)}) copy-start(s32[1,32]{1,0:T(1,128)} %param.17) | copy-start | bytes 388
  66.1 2.9 %copy-start.11 = (s32[512]{0:T(512)S(1)}, s32[512]{0:T(512)}, u32[]{:S(2)}) copy-start(s32[512]{0:T(512)} %param.16) | copy-start | bytes 6148
  77.9 26.2 %all-to-all-start.1 = ((bf16[8,32,1024]{2,1,0:T(8,128)(2,1)}), bf16[8,32,1024]{2,1,0:T(8,128)(2,1)}, u32[]{:S(2)}, u32[]{:S(2)}) async-start(bf16[8,32,1024]{2,1,0:T(8,128)(2,1)} %broadcast_in_dim.57), calls=%async_computation.1 | async-start | bytes 1048576 | tf_op jit(solution)/shard_map/all_to_all | solution.py:64
  86.1 86.8 %reduce-scatter.8.cloned.1.call-start = ((), (), s32[]{:S(2)}) async-start(), calls=%async_computation.8 | async-start | bytes 2359296 | tf_op jit(solution)/shard_map/reduce_scatter | solution.py:43
  106.8 4.9 %copy-start.5 = (f32[128,2048]{1,0:T(8,128)S(1)}, f32[128,2048]{1,0:T(8,128)}, u32[]{:S(2)}) copy-start(f32[128,2048]{1,0:T(8,128)} %slice_bitcast_fusion) | copy-start | bytes 3145732
  117.5 2.5 copy-start.4
  117.5 2.5 copy-start.6
  131.3 4.7 %collective-permute-start.1 = (f32[512,1024]{1,0:T(8,128)}, f32[512,1024]{1,0:T(8,128)}, u32[]{:S(2)}, u32[]{:S(2)}) collective-permute-start(f32[512,1024]{1,0:T(8,128)} %fusion.4), channel_id=1, source_target_pairs={{0,1},{1,0},{2,3},{3,2},{4,5},{5,4},{6,7},{7,6},{8,9},{9,8},{10,11... | collective-permute-start | bytes 6291464 | tf_op jit(solution)/shard_map/ppermute | solution.py:37
  141.6 75.2 %reduce-scatter.6.cloned.1.call-start = ((), (), s32[]{:S(2)}) async-start(), calls=%async_computation.7 | async-start | bytes 2359296 | tf_op jit(solution)/shard_map/reduce_scatter | solution.py:43
  145.0 4.2 %collective-permute-start = (f32[512,1024]{1,0:T(8,128)S(1)}, f32[512,1024]{1,0:T(8,128)S(1)}, u32[]{:S(2)}, u32[]{:S(2)}) collective-permute-start(f32[512,1024]{1,0:T(8,128)S(1)} %fusion.19), channel_id=1, source_target_pairs={{0,1},{1,0},{2,3},{3,2},{4,5},{5,4},{6,7},{7,6},{8,9},{9,8},{10,11... | collective-permute-start | bytes 6291464 | tf_op jit(solution)/shard_map/ppermute | solution.py:37
  220.4 23.5 %all-to-all-start.2 = ((f32[32,4,1024]{2,1,0:T(4,128)}), f32[32,4,1024]{2,1,0:T(4,128)}, u32[]{:S(2)}, u32[]{:S(2)}) async-start(f32[32,4,1024]{2,1,0:T(4,128)} %bitcast_select_fusion), calls=%async_computation.5 | async-start | bytes 1048576 | tf_op jit(solution)/shard_map/all_to_all | solution.py:54
Sparse Core Ops, SparseCore 0:
  30.8 42.2 reduce-scatter.3
  141.7 31.0 reduce-scatter.7
  175.4 41.3 reduce-scatter.5

commit v7 on v5

--- a/solution.py
+++ b/solution.py
@@ -37,10 +37,17 @@
     return kept + lax.ppermute(sent, "dom", [(i, i ^ 1) for i in range(n_dom)])
 
 
-def reduce_in_group(pair):
+def reduce_in_group(pair, split=False):
     n_group = lax.axis_size("group")
     width = pair.shape[1]
-    in_group = lax.psum_scatter(pair.reshape(n_group, -1, width), "group", scatter_dimension=0, tiled=True)
+    blocks = pair.reshape(n_group, -1, width)
+    if split:
+        half = width // 2
+        scattered = lax.psum_scatter(blocks[:, :, :half], "group", scatter_dimension=0, tiled=True)
+        exchanged = lax.all_to_all(blocks[:, :, half:], "group", split_axis=0, concat_axis=0, tiled=True)
+        in_group = jnp.concatenate([scattered[0], exchanged.sum(axis=0)], axis=1)
+    else:
+        in_group = lax.psum_scatter(blocks, "group", scatter_dimension=0, tiled=True)
     return in_group.reshape(lax.axis_size("dom") // 2, -1, width)
 
 
@@ -123,7 +130,7 @@
     hist_halo = hist_slots.reshape(-1, D)[halo_index]
     hub_second = gather_hubs(new_history[owned_hubs])
     agg_second = combine_tiles(new_history, hist_halo, hub_second, tile_cols, tile_vals)
-    outgoing_second = reduce_in_group(pair_product(grad_out, agg_second, 1))
+    outgoing_second = reduce_in_group(pair_product(grad_out, agg_second, 1), split=True)
     grad_first, grad_second = reduce_over_dom(outgoing_first, outgoing_second, rows)
     return (new_history, vertex_grad.astype(jnp.bfloat16), grad_first, grad_second)
 

time: 230 us -> 244 us (1.061)
  waiting for transfers between devices: 93.2 us -> 103 us
  starting transfers between devices: 23.9 us -> 27.8 us
    all_to_all x0 -> x1, waiting for transfers between devices: none -> 19.2 us  [reduce_in_group(): lax.all_to_all(blocks[:, :, half:], 'group', split_axis=0, concat_axis=0,...]
    all_to_all x2, waiting for transfers between devices: 30.3 us -> 23.8 us  [gather_hubs(): lax.all_to_all(copies, 'group', split_axis=0, concat_axis=0, tiled=True)]
    all_to_all x0 -> x1, starting transfers between devices: none -> 3.57 us  [reduce_in_group(): lax.all_to_all(blocks[:, :, half:], 'group', split_axis=0, concat_axis=0,...]
    reduce_scatter x2, waiting for transfers between devices: 42.3 us -> 38.9 us  [the longest x1 30.7 us: reduce_in_group(): lax.psum_scatter(blocks[:, :, :half], 'group', scatter_dimension=0, tiled...]
  transfers between devices with their start and end apart: 8 -> 9, of which waited for: 6 -> 8; matrix products, arithmetic and copies ran while one was open for 21% -> 19% of each run, Pallas kernels for 0% -> 0%
where the time goes in v7:
time: 244 us; the launch traced here: 243 us
  waiting for transfers between devices  103 us (42%)
  local copies, waits for them, and re-layouts  45 us (18%)
  starting transfers between devices  27.8 us (11%)
  blocking collectives  23.3 us (10%)
  matrix products  16.9 us (7%)
  between operations  14.1 us (6%)
  other arithmetic  13.2 us (5%)
    reduce_scatter x1, waiting for transfers between devices, reduce_in_group(): lax.psum_scatter(blocks[:, :, :half], 'group', scatter_dimension=0, tiled...  30.7 us
    all_to_all x2, waiting for transfers between devices, gather_hubs(): lax.all_to_all(copies, 'group', split_axis=0, concat_axis=0, tiled=True)  23.8 us
    all_to_all x1, blocking collectives, reduce_over_dom(): lax.all_to_all(outgoing, 'dom', split_axis=0, concat_axis=0, tiled=True)  23.3 us
    all_to_all x1, waiting for transfers between devices, reduce_in_group(): lax.all_to_all(blocks[:, :, half:], 'group', split_axis=0, concat_axis=0,...  19.2 us
    all_to_all x1, waiting for transfers between devices, on_device(): lax.all_to_all(jnp.stack([feats[routes], history[routes]], axis=1), 'dom'...  13 us
    all_to_all x2, starting transfers between devices, gather_hubs(): lax.all_to_all(copies, 'group', split_axis=0, concat_axis=0, tiled=True)  12.3 us
    all_to_all x1, starting transfers between devices, on_device(): lax.all_to_all(jnp.stack([feats[routes], history[routes]], axis=1), 'dom'...  8.76 us
    reduce_scatter x1, waiting for transfers between devices, reduce_in_group(): lax.psum_scatter(blocks, 'group', scatter_dimension=0, tiled=True)  8.19 us
  transfers between devices with their start and end apart: 9, of which 8 were waited for; matrix products, arithmetic and copies ran while one was open for 19% of the time, Pallas kernels for 0%

profile of v7, /device:TPU:1, one launch (start us, length us, event | category | flops | bytes accessed | tf_op | source)
XLA Modules:
  0.0 243.4 jit_solution(1805963370945560139)
XLA Ops:
  8.2 3.8 %gather_fusion.1 = bf16[512,1024]{1,0:T(8,128)(2,1)S(1)} fusion(bf16[128,1024]{1,0:T(8,128)(2,1)} %param.11, s32[1024]{0:T(1024)S(1)} %pad_clamp_fusion.3), kind=kCustom, calls=%fused_computation.1 | custom fusion | bytes 2099200 | tf_op jit(solution)/shard_map/gather | solution.py:113
  12.0 2.8 %gather_fusion = bf16[512,1024]{1,0:T(8,128)(2,1)} fusion(bf16[128,1024]{1,0:T(8,128)(2,1)S(1)} %copy-done.1, s32[1024]{0:T(1024)S(1)} %pad_clamp_fusion.3), kind=kCustom, calls=%fused_computation | custom fusion | bytes 2099200 | tf_op jit(solution)/shard_map/gather | solution.py:113
  14.8 2.8 %pad_maximum_fusion = bf16[32,2,16,1024]{3,2,1,0:T(8,128)(2,1)} fusion(bf16[32,1,16,1024]{3,2,1,0:T(8,128)(2,1)S(1)} %bitcast.89, bf16[32,1,16,1024]{3,2,1,0:T(8,128)(2,1)} %bitcast.90), kind=kLoop, calls=%fused_computation.9 | loop fusion | flops 1048576 | bytes 4194304 | tf_op jit(solution)/shard_map/stack | solution.py:113
  17.6 8.8 %all-to-all-start = ((bf16[32,2,16,1024]{3,2,1,0:T(8,128)(2,1)}), bf16[32,2,16,1024]{3,2,1,0:T(8,128)(2,1)}, u32[]{:S(2)}, u32[]{:S(2)}) async-start(bf16[32,2,16,1024]{3,2,1,0:T(8,128)(2,1)} %pad_maximum_fusion), calls=%async_computation.1 | async-start | bytes 4194304 | tf_op jit(solution)/shard_map/all_to_all | solution.py:112
  26.4 2.5 %convolution_bitcast_fusion = f32[4,128,1024]{1,2,0:T(8,128)} fusion(bf16[128,1024]{1,0:T(8,128)(2,1)S(1)} %copy-done.6, bf16[1024,1024]{1,0:T(8,128)(2,1)S(1)} %copy-done, bf16[1,4,128,128]{3,2,1,0:T(8,128)(2,1)S(1)} %copy-done.5), kind=kOutput, calls=%fused_computation.14 | convolution fusion | flops 402784256 | bytes 4587520 | tf_op jit(solution)/shard_map/rtij,rid->rtjd/dot_general | solution.py:96
  28.9 3.1 %copy.41 = f32[4,128,1024]{2,0,1:T(4,128)} copy(f32[4,128,1024]{1,2,0:T(8,128)} %convolution_bitcast_fusion) | data formatting | bytes 4194304 | tf_op jit(solution)/shard_map/rtij,rid->rtjd/dot_general | solution.py:96
  32.0 4.2 %fusion.7 = f32[7,128,1024]{2,0,1:T(8,128)S(1)} fusion(f32[4,128,1024]{2,0,1:T(4,128)} %copy.41, s32[4]{0:T(128)S(1)} %bitcast.98), kind=kOutput, calls=%fused_computation.44 | convolution fusion | flops 44040220 | bytes 5767184 | tf_op jit(solution)/shard_map/rts,rtjd->sjd/dot_general | solution.py:105
  36.2 1.9 copy-done.2
  41.8 13.0 %all-to-all-done = bf16[32,2,16,1024]{3,2,1,0:T(8,128)(2,1)} async-done(((bf16[32,2,16,1024]{3,2,1,0:T(8,128)(2,1)}), bf16[32,2,16,1024]{3,2,1,0:T(8,128)(2,1)}, u32[]{:S(2)}, u32[]{:S(2)}) %all-to-all-start) | async-done | bytes 2097184 | tf_op jit(solution)/shard_map/all_to_all | solution.py:112
  55.6 8.2 %all-to-all-start.1 = ((bf16[8,32,1024]{2,1,0:T(8,128)(2,1)}), bf16[8,32,1024]{2,1,0:T(8,128)(2,1)}, u32[]{:S(2)}, u32[]{:S(2)}) async-start(bf16[8,32,1024]{2,1,0:T(8,128)(2,1)} %broadcast_in_dim.65), calls=%async_computation.2 | async-start | bytes 1048576 | tf_op jit(solution)/shard_map/all_to_all | solution.py:71
  63.8 2.8 %fusion.13 = (bf16[32,1,16,1024]{3,2,1,0:T(8,128)(2,1)S(1)}, bf16[32,1,16,1024]{3,2,1,0:T(8,128)(2,1)}) fusion(bf16[32,2,16,1024]{3,2,1,0:T(8,128)(2,1)} %all-to-all-done), kind=kLoop, calls=%fused_computation.54 | loop fusion | bytes 4194304 | tf_op jit(solution)/shard_map/slice | solution.py:116
  66.6 4.8 %gather_fusion.2 = bf16[512,1024]{1,0:T(8,128)(2,1)} fusion(bf16[512,1024]{1,0:T(8,128)(2,1)} %bitcast.82, s32[1024]{0:T(1024)S(1)} %pad_clamp_fusion.2), kind=kCustom, calls=%fused_computation.2 | custom fusion | bytes 2099200 | tf_op jit(solution)/shard_map/gather | solution.py:118
  71.5 13.0 %all-to-all-done.1 = bf16[8,32,1024]{2,1,0:T(8,128)(2,1)} async-done(((bf16[8,32,1024]{2,1,0:T(8,128)(2,1)}), bf16[8,32,1024]{2,1,0:T(8,128)(2,1)}, u32[]{:S(2)}, u32[]{:S(2)}) %all-to-all-start.1) | async-done | bytes 524320 | tf_op jit(solution)/shard_map/all_to_all | solution.py:71
  84.5 2.8 %pad_maximum_fusion.1 = bf16[896,1024]{1,0:T(8,128)(2,1)} fusion(bf16[256,1024]{1,0:T(8,128)(2,1)} %bitcast.14, bf16[512,1024]{1,0:T(8,128)(2,1)} %gather_fusion.2, bf16[128,1024]{1,0:T(8,128)(2,1)S(1)} %copy-done.1), kind=kLoop, calls=%fused_computation.10 | loop fusion | flops 5505024 | bytes 3670016 | tf_op jit(solution)/shard_map/concatenate | solution.py:15
  87.3 3.1 %gather_fusion.4 = bf16[4,128,1024]{2,1,0:T(8,128)(2,1)} fusion(bf16[7,128,1024]{2,1,0:T(8,128)(2,1)} %bitcast.87, s32[1024]{0:T(1024)S(1)} %pad_clamp_fusion), kind=kCustom, calls=%fused_computation.4 | custom fusion | bytes 2097168 | tf_op jit(solution)/shard_map/gather | solution.py:17
  90.4 2.4 fusion
  92.8 3.0 %scatter_fusion = f32[128,1024]{1,0:T(8,128)} fusion(f32[128,1024]{1,0:T(8,128)} %bitcast.85, s32[32]{0:T(128)S(1)} %fusion.10, f32[32,1024]{1,0:T(8,128)} %reduce-scatter.4.cloned.1.call-done), kind=kCustom, calls=%fused_computation.8 | custom fusion | flops 32768 | bytes 393344 | tf_op jit(solution)/shard_map/scatter-add | solution.py:110
  95.8 3.3 %fusion.14 = (bf16[128,1024]{1,0:T(8,128)(2,1)}, bf16[128,1024]{1,0:T(8,128)(2,1)}, bf16[128,1024]{1,0:T(8,128)(2,1)S(1)}) fusion(f32[128,1024]{1,0:T(8,128)} %scatter_fusion, bf16[1024,128]{1,0:T(8,128)(2,1)} %fusion, bf16[1024,1024]{1,0:T(8,128)(2,1)} %param.13), kind=kOutput, calls=%fused_computation.55 | convolution fusion | flops 270008320 | bytes 3670016 | tf_op jit(solution)/shard_map/dot_general | solution.py:120
  99.1 1.9 copy.47
  103.5 2.4 collective-permute-start
  105.8 3.8 %collective-permute-done = f32[512,1024]{1,0:T(8,128)S(1)} collective-permute-done((f32[512,1024]{1,0:T(8,128)S(1)}, f32[512,1024]{1,0:T(8,128)S(1)}, u32[]{:S(2)}, u32[]{:S(2)}) %collective-permute-start) | collective-permute-done | bytes 2097184 | tf_op jit(solution)/shard_map/ppermute | solution.py:37
  114.3 4.1 %all-to-all-start.2 = ((bf16[8,32,1024]{2,1,0:T(8,128)(2,1)}), bf16[8,32,1024]{2,1,0:T(8,128)(2,1)}, u32[]{:S(2)}, u32[]{:S(2)}) async-start(bf16[8,32,1024]{2,1,0:T(8,128)(2,1)} %broadcast_in_dim.73), calls=%async_computation.4 | async-start | bytes 1048576 | tf_op jit(solution)/shard_map/all_to_all | solution.py:71
  122.9 2.8 %gather_fusion.5 = bf16[512,1024]{1,0:T(8,128)(2,1)} fusion(bf16[512,1024]{1,0:T(8,128)(2,1)S(1)} %bitcast.81, s32[1024]{0:T(1024)S(1)} %pad_clamp_fusion.2), kind=kCustom, calls=%fused_computation.5 | custom fusion | bytes 2099200 | tf_op jit(solution)/shard_map/gather | solution.py:130
  125.7 10.8 %all-to-all-done.2 = bf16[8,32,1024]{2,1,0:T(8,128)(2,1)} async-done(((bf16[8,32,1024]{2,1,0:T(8,128)(2,1)}), bf16[8,32,1024]{2,1,0:T(8,128)(2,1)}, u32[]{:S(2)}, u32[]{:S(2)}) %all-to-all-start.2) | async-done | bytes 524320 | tf_op jit(solution)/shard_map/all_to_all | solution.py:71
  136.5 2.8 %pad_maximum_fusion.2 = bf16[896,1024]{1,0:T(8,128)(2,1)} fusion(bf16[256,1024]{1,0:T(8,128)(2,1)} %bitcast.26, bf16[512,1024]{1,0:T(8,128)(2,1)} %gather_fusion.5, bf16[128,1024]{1,0:T(8,128)(2,1)S(1)} %get-tuple-element.2), kind=kLoop, calls=%fused_computation.11 | loop fusion | flops 5505024 | bytes 3670016 | tf_op jit(solution)/shard_map/concatenate | solution.py:15
  139.2 2.2 gather_fusion.7
  143.0 3.8 %collective-permute-done.1 = f32[512,1024]{1,0:T(8,128)S(1)} collective-permute-done((f32[512,1024]{1,0:T(8,128)S(1)}, f32[512,1024]{1,0:T(8,128)S(1)}, u32[]{:S(2)}, u32[]{:S(2)}) %collective-permute-start.1) | collective-permute-done | bytes 2097184 | tf_op jit(solution)/shard_map/ppermute | solution.py:37
  148.8 3.6 %all-to-all-start.3 = ((f32[8,64,512]{2,1,0:T(8,128)}), f32[8,64,512]{2,1,0:T(8,128)S(1)}, u32[]{:S(2)}, u32[]{:S(2)}) async-start(f32[8,64,512]{2,1,0:T(8,128)} %get-tuple-element.11), calls=%async_computation.6 | async-start | bytes 2097152 | tf_op jit(solution)/shard_map/all_to_all | solution.py:47
  152.5 8.2 %reduce-scatter.6.cloned.1.call-done = f32[1,64,1024]{2,1,0:T(8,128)} async-done(((f32[8,64,1024]{2,1,0:T(8,128)}), f32[1,64,1024]{2,1,0:T(8,128)}) %reduce-scatter.6.cloned.1.call-update) | async-done | bytes 262160 | tf_op jit(solution)/shard_map/reduce_scatter | solution.py:50
  161.7 19.2 %all-to-all-done.3 = f32[8,64,512]{2,1,0:T(8,128)S(1)} async-done(((f32[8,64,512]{2,1,0:T(8,128)}), f32[8,64,512]{2,1,0:T(8,128)S(1)}, u32[]{:S(2)}, u32[]{:S(2)}) %all-to-all-start.3) | async-done | bytes 1048608 | tf_op jit(solution)/shard_map/all_to_all | solution.py:47
  181.0 30.7 %reduce-scatter.8.cloned.1.call-done = f32[1,64,512]{2,1,0:T(8,128)} async-done(((f32[8,64,512]{2,1,0:T(8,128)}), f32[1,64,512]{2,1,0:T(8,128)}) %reduce-scatter.8.cloned.1.call-update) | async-done | bytes 131088 | tf_op jit(solution)/shard_map/reduce_scatter | solution.py:46
  212.9 23.3 %all_to_all.25 = f32[32,4,1024]{2,1,0:T(4,128)S(1)} all-to-all(f32[32,4,1024]{2,1,0:T(4,128)S(1)} %bitcast_select_fusion), channel_id=1, replica_groups=mesh['group'=8,'dom'=32] {'dom'}, dimensions={0} | all-to-all | bytes 1048576 | tf_op jit(solution)/shard_map/all_to_all | solution.py:61
  (70 shorter events, 23.7 us)
Async XLA Ops:
  7.2 19.2 %copy-start = (bf16[1024,1024]{1,0:T(8,128)(2,1)S(1)}, bf16[1024,1024]{1,0:T(8,128)(2,1)}, u32[]{:S(2)}) copy-start(bf16[1024,1024]{1,0:T(8,128)(2,1)} %param.14) | copy-start | bytes 6291460
  8.2 3.8 %copy-start.1 = (bf16[128,1024]{1,0:T(8,128)(2,1)S(1)}, bf16[128,1024]{1,0:T(8,128)(2,1)}, u32[]{:S(2)}) copy-start(bf16[128,1024]{1,0:T(8,128)(2,1)} %param.10) | copy-start | bytes 786436
  17.5 8.8 %copy-start.5 = (bf16[1,4,128,128]{3,2,1,0:T(8,128)(2,1)S(1)}, bf16[1,4,128,128]{3,2,1,0:T(8,128)(2,1)}, u32[]{:S(2)}) copy-start(bf16[1,4,128,128]{3,2,1,0:T(8,128)(2,1)} %param.19) | copy-start | bytes 393220
  17.6 8.8 %copy-start.6 = (bf16[128,1024]{1,0:T(8,128)(2,1)S(1)}, bf16[128,1024]{1,0:T(8,128)(2,1)}, u32[]{:S(2)}) copy-start(bf16[128,1024]{1,0:T(8,128)(2,1)} %param.12) | copy-start | bytes 786436
  17.6 37.2 %all-to-all-start = ((bf16[32,2,16,1024]{3,2,1,0:T(8,128)(2,1)}), bf16[32,2,16,1024]{3,2,1,0:T(8,128)(2,1)}, u32[]{:S(2)}, u32[]{:S(2)}) async-start(bf16[32,2,16,1024]{3,2,1,0:T(8,128)(2,1)} %pad_maximum_fusion), calls=%async_computation.1 | async-start | bytes 4194304 | tf_op jit(solution)/shard_map/all_to_all | solution.py:112
  26.3 66.4 %reduce-scatter.4.cloned.1.call-start = ((), (), s32[]{:S(2)}) async-start(), calls=%async_computation.8 | async-start | bytes 1179648 | tf_op jit(solution)/shard_map/reduce_scatter | solution.py:109
  28.9 3.1 %copy-start.10 = (s32[1,4]{1,0:T(1,128)S(1)}, s32[1,4]{1,0:T(1,128)}, u32[]{:S(2)}) copy-start(s32[1,4]{1,0:T(1,128)} %param.18) | copy-start | bytes 52
  36.2 2.0 copy-start.2
  38.7 1.4 slice-start
  40.1 1.0 copy-start.11
  40.2 23.6 %copy-start.9 = (s32[512]{0:T(512)S(1)}, s32[512]{0:T(512)}, u32[]{:S(2)}) copy-start(s32[512]{0:T(512)} %param.16) | copy-start | bytes 6148
  55.6 28.9 %all-to-all-start.1 = ((bf16[8,32,1024]{2,1,0:T(8,128)(2,1)}), bf16[8,32,1024]{2,1,0:T(8,128)(2,1)}, u32[]{:S(2)}, u32[]{:S(2)}) async-start(bf16[8,32,1024]{2,1,0:T(8,128)(2,1)} %broadcast_in_dim.65), calls=%async_computation.2 | async-start | bytes 1048576 | tf_op jit(solution)/shard_map/all_to_all | solution.py:71
  99.1 37.4 %copy-start.3 = (bf16[128,1024]{1,0:T(8,128)(2,1)}, bf16[128,1024]{1,0:T(8,128)(2,1)S(1)}, u32[]{:S(2)}) copy-start(bf16[128,1024]{1,0:T(8,128)(2,1)S(1)} %get-tuple-element.2) | copy-start | bytes 786436
  101.0 8.7 %copy-start.4 = (bf16[1024,128]{1,0:T(8,128)(2,1)S(1)}, bf16[1024,128]{1,0:T(8,128)(2,1)}, u32[]{:S(2)}) copy-start(bf16[1024,128]{1,0:T(8,128)(2,1)} %fusion) | copy-start | bytes 786436
  103.5 6.2 %collective-permute-start = (f32[512,1024]{1,0:T(8,128)S(1)}, f32[512,1024]{1,0:T(8,128)S(1)}, u32[]{:S(2)}, u32[]{:S(2)}) collective-permute-start(f32[512,1024]{1,0:T(8,128)S(1)} %fusion.15), channel_id=1, source_target_pairs={{0,1},{1,0},{2,3},{3,2},{4,5},{5,4},{6,7},{7,6},{8,9},{9,8},{10,11... | collective-permute-start | bytes 6291464 | tf_op jit(solution)/shard_map/ppermute | solution.py:37
  114.3 22.1 %all-to-all-start.2 = ((bf16[8,32,1024]{2,1,0:T(8,128)(2,1)}), bf16[8,32,1024]{2,1,0:T(8,128)(2,1)}, u32[]{:S(2)}, u32[]{:S(2)}) async-start(bf16[8,32,1024]{2,1,0:T(8,128)(2,1)} %broadcast_in_dim.73), calls=%async_computation.4 | async-start | bytes 1048576 | tf_op jit(solution)/shard_map/all_to_all | solution.py:71
  118.5 42.2 %reduce-scatter.6.cloned.1.call-start = ((), (), s32[]{:S(2)}) async-start(), calls=%async_computation.9 | async-start | bytes 2359296 | tf_op jit(solution)/shard_map/reduce_scatter | solution.py:50
  119.2 92.4 %reduce-scatter.8.cloned.1.call-start = ((), (), s32[]{:S(2)}) async-start(), calls=%async_computation.10 | async-start | bytes 1179648 | tf_op jit(solution)/shard_map/reduce_scatter | solution.py:46
  139.2 2.7 %copy-start.8 = (bf16[128,8,16,1,4]{0,4,3,2,1:T(4,128)(2,1)S(1)}, bf16[128,8,16,1,4]{0,4,3,2,1:T(4,128)(2,1)}, u32[]{:S(2)}) copy-start(bf16[128,8,16,1,4]{0,4,3,2,1:T(4,128)(2,1)} %get-tuple-element.18) | copy-start | bytes 393220
  141.4 5.4 %copy-start.7 = (bf16[128,8,16,1,4]{0,4,3,2,1:T(4,128)(2,1)S(1)}, bf16[128,8,16,1,4]{0,4,3,2,1:T(4,128)(2,1)}, u32[]{:S(2)}) copy-start(bf16[128,8,16,1,4]{0,4,3,2,1:T(4,128)(2,1)} %get-tuple-element.17) | copy-start | bytes 393220
  142.3 4.4 %collective-permute-start.1 = (f32[512,1024]{1,0:T(8,128)S(1)}, f32[512,1024]{1,0:T(8,128)S(1)}, u32[]{:S(2)}, u32[]{:S(2)}) collective-permute-start(f32[512,1024]{1,0:T(8,128)S(1)} %fusion.16), channel_id=1, source_target_pairs={{0,1},{1,0},{2,3},{3,2},{4,5},{5,4},{6,7},{7,6},{8,9},{9,8},{10,11... | collective-permute-start | bytes 6291464 | tf_op jit(solution)/shard_map/ppermute | solution.py:37
  148.8 32.1 %all-to-all-start.3 = ((f32[8,64,512]{2,1,0:T(8,128)}), f32[8,64,512]{2,1,0:T(8,128)S(1)}, u32[]{:S(2)}, u32[]{:S(2)}) async-start(f32[8,64,512]{2,1,0:T(8,128)} %get-tuple-element.11), calls=%async_computation.6 | async-start | bytes 2097152 | tf_op jit(solution)/shard_map/all_to_all | solution.py:47
Sparse Core Ops, SparseCore 0:
  40.3 42.7 reduce-scatter.3
  121.9 38.7 reduce-scatter.5
  163.2 48.4 reduce-scatter.7

commit v8 on v5

--- a/solution.py
+++ b/solution.py
@@ -60,9 +60,13 @@
 
 def gather_hubs(hub_rows):
     n_group = lax.axis_size("group")
-    copies = jnp.broadcast_to(hub_rows[None], (n_group,) + hub_rows.shape)
-    spread = lax.all_to_all(copies, "group", split_axis=0, concat_axis=0, tiled=True)
-    return spread.reshape(-1, hub_rows.shape[1])
+    shifted = [hub_rows] + [
+        lax.ppermute(hub_rows, "group", [(i, (i + s) % n_group) for i in range(n_group)])
+        for s in range(1, n_group)
+    ]
+    by_shift = jnp.stack(shifted, axis=0)
+    shift_of_source = (lax.axis_index("group") - jnp.arange(n_group, dtype=jnp.int32)) % n_group
+    return jnp.take(by_shift, shift_of_source, axis=0).reshape(-1, hub_rows.shape[1])
 
 
 def on_device(

time: 230 us -> 249 us (1.083)
  waiting for transfers between devices: 93.2 us -> 70 us
  starting transfers between devices: 23.9 us -> 42.4 us
  local copies, waits for them, and re-layouts: 43.5 us -> 58 us
  other arithmetic: 13.1 us -> 17.8 us
  matrix products: 18.3 us -> 22.5 us
    all_to_all x2 -> x0, waiting for transfers between devices: 30.3 us -> none  [gather_hubs(): lax.all_to_all(copies, 'group', split_axis=0, concat_axis=0, tiled=True)]
    ppermute x0 -> x14, starting transfers between devices: none -> 29.5 us  [gather_hubs(): lax.ppermute(hub_rows, 'group', [(i, (i + s) % n_group) for i in range(n_...]
    unnamed x26 -> x46, local copies, waits for them, and re-layouts: 4.71 us -> 17.5 us
    all_to_all x2 -> x0, starting transfers between devices: 12.3 us -> none  [gather_hubs(): lax.all_to_all(copies, 'group', split_axis=0, concat_axis=0, tiled=True)]
    ppermute x0 -> x14, waiting for transfers between devices: none -> 4.75 us  [gather_hubs(): lax.ppermute(hub_rows, 'group', [(i, (i + s) % n_group) for i in range(n_...]
    reduce_scatter x2, waiting for transfers between devices: 42.3 us -> 46.9 us  [reduce_in_group(): lax.psum_scatter(pair.reshape(n_group, -1, width), 'group', scatter_dimen...]
    ppermute x2, waiting for transfers between devices: 7.57 us -> 3.79 us  [pair_product(): return kept + lax.ppermute(sent, 'dom', [(i, i ^ 1) for i in range(n_dom)])]
    dot_general x4, matrix products: 5.36 us -> 8.49 us  [weight_product(): lax.dot_general(left_rows, right_rows, (((0,), (0,)), ((), ())), preferre...]
  transfers between devices with their start and end apart: 8 -> 20, of which waited for: 6 -> 8; matrix products, arithmetic and copies ran while one was open for 21% -> 29% of each run, Pallas kernels for 0% -> 0%
where the time goes in v8:
time: 249 us; the launch traced here: 248 us
  waiting for transfers between devices  70 us (28%)
  local copies, waits for them, and re-layouts  58 us (23%)
  starting transfers between devices  42.4 us (17%)
  blocking collectives  23 us (9%)
  matrix products  22.5 us (9%)
  other arithmetic  17.8 us (7%)
  between operations  14 us (6%)
    reduce_scatter x2, waiting for transfers between devices, reduce_in_group(): lax.psum_scatter(pair.reshape(n_group, -1, width), 'group', scatter_dimen...  46.9 us
    ppermute x14, starting transfers between devices, gather_hubs(): lax.ppermute(hub_rows, 'group', [(i, (i + s) % n_group) for i in range(n_...  29.5 us
    all_to_all x1, blocking collectives, reduce_over_dom(): lax.all_to_all(outgoing, 'dom', split_axis=0, concat_axis=0, tiled=True)  23 us
    unnamed x46, local copies, waits for them, and re-layouts  17.5 us
    all_to_all x1, waiting for transfers between devices, on_device(): lax.all_to_all(jnp.stack([feats[routes], history[routes]], axis=1), 'dom'...  14.6 us
    all_to_all x1, starting transfers between devices, on_device(): lax.all_to_all(jnp.stack([feats[routes], history[routes]], axis=1), 'dom'...  9.33 us
    dot_general x4, matrix products, weight_product(): lax.dot_general(left_rows, right_rows, (((0,), (0,)), ((), ())), preferre...  8.49 us
    gather x2, local copies, waits for them, and re-layouts, combine_tiles(): picked = source.reshape(-1, tile_vals.shape[2], feature_width)[tile_cols]  5.25 us
  transfers between devices with their start and end apart: 20, of which 8 were waited for; matrix products, arithmetic and copies ran while one was open for 29% of the time, Pallas kernels for 0%

profile of v8, /device:TPU:1, one launch (start us, length us, event | category | flops | bytes accessed | tf_op | source)
XLA Modules:
  0.0 247.7 jit_solution(11604752850928510716)
XLA Ops:
  10.6 2.5 %collective-permute-start = (bf16[32,1024]{1,0:T(8,128)(2,1)S(1)}, bf16[32,1024]{1,0:T(8,128)(2,1)}, u32[]{:S(2)}, u32[]{:S(2)}) collective-permute-start(bf16[32,1024]{1,0:T(8,128)(2,1)S(1)} %gather_fusion.3), channel_id=1, source_target_pairs={{0,32},{32,64},{64,96},{96,128},{128,160},{160,192},{192,224},{224... | collective-permute-start | bytes 196616 | tf_op jit(solution)/shard_map/ppermute | solution.py:64
  13.1 3.0 %collective-permute-start.1 = (bf16[32,1024]{1,0:T(8,128)(2,1)S(1)}, bf16[32,1024]{1,0:T(8,128)(2,1)}, u32[]{:S(2)}, u32[]{:S(2)}) collective-permute-start(bf16[32,1024]{1,0:T(8,128)(2,1)S(1)} %gather_fusion.3), channel_id=1, source_target_pairs={{0,64},{32,96},{64,128},{96,160},{128,192},{160,224},{192,0},{224,... | collective-permute-start | bytes 196616 | tf_op jit(solution)/shard_map/ppermute | solution.py:64
  16.1 3.8 %collective-permute-start.2 = (bf16[32,1024]{1,0:T(8,128)(2,1)S(1)}, bf16[32,1024]{1,0:T(8,128)(2,1)}, u32[]{:S(2)}, u32[]{:S(2)}) collective-permute-start(bf16[32,1024]{1,0:T(8,128)(2,1)S(1)} %gather_fusion.3), channel_id=1, source_target_pairs={{0,96},{32,128},{64,160},{96,192},{128,224},{160,0},{192,32},{224,... | collective-permute-start | bytes 196616 | tf_op jit(solution)/shard_map/ppermute | solution.py:64
  20.3 4.5 %collective-permute-start.4 = (bf16[32,1024]{1,0:T(8,128)(2,1)S(1)}, bf16[32,1024]{1,0:T(8,128)(2,1)S(1)}, u32[]{:S(2)}, u32[]{:S(2)}) collective-permute-start(bf16[32,1024]{1,0:T(8,128)(2,1)S(1)} %gather_fusion.3), channel_id=1, source_target_pairs={{0,160},{32,192},{64,224},{96,0},{128,32},{160,64},{192,96},{224,1... | collective-permute-start | bytes 196616 | tf_op jit(solution)/shard_map/ppermute | solution.py:64
  24.8 3.5 %convolution_bitcast_fusion = f32[4,128,1024]{1,2,0:T(8,128)} fusion(bf16[128,1024]{1,0:T(8,128)(2,1)} %param.14, bf16[1024,1024]{1,0:T(8,128)(2,1)S(1)} %copy-done, bf16[1,4,128,128]{3,2,1,0:T(8,128)(2,1)} %param.21), kind=kOutput, calls=%fused_computation.16 | convolution fusion | flops 402784256 | bytes 4587520 | tf_op jit(solution)/shard_map/rtij,rid->rtjd/dot_general | solution.py:93
  28.3 3.1 %copy.41 = f32[4,128,1024]{2,0,1:T(4,128)} copy(f32[4,128,1024]{1,2,0:T(8,128)} %convolution_bitcast_fusion) | data formatting | bytes 4194304 | tf_op jit(solution)/shard_map/rtij,rid->rtjd/dot_general | solution.py:93
  31.4 4.2 %fusion.7 = f32[7,128,1024]{2,0,1:T(8,128)S(1)} fusion(f32[4,128,1024]{2,0,1:T(4,128)} %copy.41, s32[4]{0:T(128)S(1)} %bitcast.130), kind=kOutput, calls=%fused_computation.67 | convolution fusion | flops 44040220 | bytes 5767184 | tf_op jit(solution)/shard_map/rts,rtjd->sjd/dot_general | solution.py:102
  39.5 2.8 %gather_fusion = bf16[512,1024]{1,0:T(8,128)(2,1)} fusion(bf16[128,1024]{1,0:T(8,128)(2,1)S(1)} %copy-done.1, s32[1024]{0:T(1024)S(1)} %get-tuple-element.23), kind=kCustom, calls=%fused_computation.2 | custom fusion | bytes 2099200 | tf_op jit(solution)/shard_map/gather | solution.py:110
  42.4 2.8 %gather_fusion.1 = bf16[512,1024]{1,0:T(8,128)(2,1)} fusion(bf16[128,1024]{1,0:T(8,128)(2,1)S(1)} %copy-done.2, s32[1024]{0:T(1024)S(1)} %get-tuple-element.23), kind=kCustom, calls=%fused_computation.3 | custom fusion | bytes 2099200 | tf_op jit(solution)/shard_map/gather | solution.py:110
  45.1 3.1 %pad_maximum_fusion = bf16[32,2,16,1024]{3,2,1,0:T(8,128)(2,1)} fusion(bf16[32,1,16,1024]{3,2,1,0:T(8,128)(2,1)} %bitcast.120, bf16[32,1,16,1024]{3,2,1,0:T(8,128)(2,1)} %bitcast.119), kind=kLoop, calls=%fused_computation.11 | loop fusion | flops 1048576 | bytes 4194304 | tf_op jit(solution)/shard_map/stack | solution.py:110
  48.3 9.3 %all-to-all-start = ((bf16[32,2,16,1024]{3,2,1,0:T(8,128)(2,1)}), bf16[32,2,16,1024]{3,2,1,0:T(8,128)(2,1)}, u32[]{:S(2)}, u32[]{:S(2)}) async-start(bf16[32,2,16,1024]{3,2,1,0:T(8,128)(2,1)} %pad_maximum_fusion), calls=%async_computation.1 | async-start | bytes 4194304 | tf_op jit(solution)/shard_map/all_to_all | solution.py:109
  60.3 2.4 collective-permute-start.5
  71.4 14.6 %all-to-all-done = bf16[32,2,16,1024]{3,2,1,0:T(8,128)(2,1)} async-done(((bf16[32,2,16,1024]{3,2,1,0:T(8,128)(2,1)}), bf16[32,2,16,1024]{3,2,1,0:T(8,128)(2,1)}, u32[]{:S(2)}, u32[]{:S(2)}) %all-to-all-start) | async-done | bytes 2097184 | tf_op jit(solution)/shard_map/all_to_all | solution.py:109
  86.0 2.8 %fusion.13 = (bf16[32,1,16,1024]{3,2,1,0:T(8,128)(2,1)S(1)}, bf16[32,1,16,1024]{3,2,1,0:T(8,128)(2,1)}) fusion(bf16[32,2,16,1024]{3,2,1,0:T(8,128)(2,1)} %all-to-all-done), kind=kLoop, calls=%fused_computation.79 | loop fusion | bytes 4194304 | tf_op jit(solution)/shard_map/slice | solution.py:113
  88.8 4.8 %gather_fusion.2 = bf16[512,1024]{1,0:T(8,128)(2,1)} fusion(bf16[512,1024]{1,0:T(8,128)(2,1)} %bitcast.112, s32[1024]{0:T(1024)S(1)} %pad_clamp_fusion.3), kind=kCustom, calls=%fused_computation.4 | custom fusion | bytes 2099200 | tf_op jit(solution)/shard_map/gather | solution.py:115
  93.6 2.8 %pad_maximum_fusion.1 = bf16[896,1024]{1,0:T(8,128)(2,1)} fusion(bf16[256,1024]{1,0:T(8,128)(2,1)} %bitcast.121, bf16[512,1024]{1,0:T(8,128)(2,1)} %gather_fusion.2, bf16[128,1024]{1,0:T(8,128)(2,1)S(1)} %copy-done.1), kind=kLoop, calls=%fused_computation.12 | loop fusion | flops 5505024 | bytes 3670016 | tf_op jit(solution)/shard_map/concatenate | solution.py:15
  96.4 3.1 %gather_fusion.4 = bf16[4,128,1024]{2,1,0:T(8,128)(2,1)} fusion(bf16[7,128,1024]{2,1,0:T(8,128)(2,1)} %bitcast.116, s32[1024]{0:T(1024)S(1)} %get-tuple-element.20), kind=kCustom, calls=%fused_computation.6 | custom fusion | bytes 2097168 | tf_op jit(solution)/shard_map/gather | solution.py:17
  99.5 2.4 fusion
  102.0 3.0 %scatter_fusion = f32[128,1024]{1,0:T(8,128)} fusion(f32[128,1024]{1,0:T(8,128)} %bitcast.115, s32[32]{0:T(128)S(1)} %copy-done.12, f32[32,1024]{1,0:T(8,128)} %reduce-scatter.4.cloned.1.call-done), kind=kCustom, calls=%fused_computation.10 | custom fusion | flops 32768 | bytes 393344 | tf_op jit(solution)/shard_map/scatter-add | solution.py:107
  105.0 3.4 %fusion.14 = (bf16[128,1024]{1,0:T(8,128)(2,1)}, bf16[128,1024]{1,0:T(8,128)(2,1)}, bf16[128,1024]{1,0:T(8,128)(2,1)S(1)}) fusion(f32[128,1024]{1,0:T(8,128)} %scatter_fusion, bf16[1024,128]{1,0:T(8,128)(2,1)} %fusion, bf16[1024,1024]{1,0:T(8,128)(2,1)} %param.15), kind=kOutput, calls=%fused_computation.80 | convolution fusion | flops 270008320 | bytes 3670016 | tf_op jit(solution)/shard_map/dot_general | solution.py:117
  111.9 2.7 %fusion.15 = f32[512,1024]{1,0:T(8,128)} fusion(bf16[128,512]{0,1:T(8,128)(2,1)S(1)} %bitcast.129, bf16[1024,128]{1,0:T(8,128)(2,1)} %fusion), kind=kOutput, calls=%fused_computation.81 | convolution fusion | flops 134217728 | bytes 2490368 | tf_op jit(solution)/shard_map/dot_general | solution.py:23
  119.1 2.8 %gather_fusion.5 = bf16[512,1024]{1,0:T(8,128)(2,1)} fusion(bf16[512,1024]{1,0:T(8,128)(2,1)S(1)} %bitcast.111, s32[1024]{0:T(1024)S(1)} %pad_clamp_fusion.3), kind=kCustom, calls=%fused_computation.7 | custom fusion | bytes 2099200 | tf_op jit(solution)/shard_map/gather | solution.py:127
  121.9 3.6 %convolution_add_fusion.1 = f32[512,1024]{1,0:T(8,128)} fusion(f32[512,1024]{1,0:T(8,128)} %collective-permute-done.7, bf16[128,512]{0,1:T(8,128)(2,1)} %bitcast.128, bf16[1024,128]{1,0:T(8,128)(2,1)} %fusion), kind=kOutput, calls=%fused_computation.15 | convolution fusion | flops 134742016 | bytes 4587520 | tf_op jit(solution)/shard_map/dot_general | solution.py:23
  128.2 4.7 %collective-permute-start.10 = (bf16[32,1024]{1,0:T(8,128)(2,1)}, bf16[32,1024]{1,0:T(8,128)(2,1)}, u32[]{:S(2)}, u32[]{:S(2)}) collective-permute-start(bf16[32,1024]{1,0:T(8,128)(2,1)} %gather_fusion.6), channel_id=1, source_target_pairs={{0,96},{32,128},{64,160},{96,192},{128,224},{160,0},{192,32},{224,... | collective-permute-start | bytes 196616 | tf_op jit(solution)/shard_map/ppermute | solution.py:64
  133.8 3.3 %collective-permute-start.12 = (bf16[32,1024]{1,0:T(8,128)(2,1)}, bf16[32,1024]{1,0:T(8,128)(2,1)}, u32[]{:S(2)}, u32[]{:S(2)}) collective-permute-start(bf16[32,1024]{1,0:T(8,128)(2,1)} %gather_fusion.6), channel_id=1, source_target_pairs={{0,160},{32,192},{64,224},{96,0},{128,32},{160,64},{192,96},{224,1... | collective-permute-start | bytes 196616 | tf_op jit(solution)/shard_map/ppermute | solution.py:64
  137.2 3.2 %collective-permute-start.13 = (bf16[32,1024]{1,0:T(8,128)(2,1)}, bf16[32,1024]{1,0:T(8,128)(2,1)S(1)}, u32[]{:S(2)}, u32[]{:S(2)}) collective-permute-start(bf16[32,1024]{1,0:T(8,128)(2,1)} %gather_fusion.6), channel_id=1, source_target_pairs={{0,192},{32,224},{64,0},{96,32},{128,64},{160,96},{192,128},{224,1... | collective-permute-start | bytes 196616 | tf_op jit(solution)/shard_map/ppermute | solution.py:64
  151.3 2.4 gather_fusion.9
  159.4 2.7 %collective-permute-start.15 = (f32[512,1024]{1,0:T(8,128)S(1)}, f32[512,1024]{1,0:T(8,128)S(1)}, u32[]{:S(2)}, u32[]{:S(2)}) collective-permute-start(f32[512,1024]{1,0:T(8,128)S(1)} %fusion.16), channel_id=1, source_target_pairs={{0,1},{1,0},{2,3},{3,2},{4,5},{5,4},{6,7},{7,6},{8,9},{9,8},{10,11... | collective-permute-start | bytes 6291464 | tf_op jit(solution)/shard_map/ppermute | solution.py:37
  162.1 3.8 %collective-permute-done.15 = f32[512,1024]{1,0:T(8,128)S(1)} collective-permute-done((f32[512,1024]{1,0:T(8,128)S(1)}, f32[512,1024]{1,0:T(8,128)S(1)}, u32[]{:S(2)}, u32[]{:S(2)}) %collective-permute-start.15) | collective-permute-done | bytes 2097184 | tf_op jit(solution)/shard_map/ppermute | solution.py:37
  167.8 5.6 %reduce-scatter.6.cloned.1.call-done = f32[1,64,1024]{2,1,0:T(8,128)} async-done(((f32[8,64,1024]{2,1,0:T(8,128)}), f32[1,64,1024]{2,1,0:T(8,128)}) %reduce-scatter.6.cloned.1.call-update) | async-done | bytes 262160 | tf_op jit(solution)/shard_map/reduce_scatter | solution.py:43
  174.5 41.2 %reduce-scatter.8.cloned.1.call-done = f32[1,64,1024]{2,1,0:T(8,128)} async-done(((f32[8,64,1024]{2,1,0:T(8,128)}), f32[1,64,1024]{2,1,0:T(8,128)}) %reduce-scatter.8.cloned.1.call-update) | async-done | bytes 262160 | tf_op jit(solution)/shard_map/reduce_scatter | solution.py:43
  216.9 23.0 %all_to_all.10 = f32[32,4,1024]{2,1,0:T(4,128)S(1)} all-to-all(f32[32,4,1024]{2,1,0:T(4,128)S(1)} %bitcast_select_fusion), channel_id=1, replica_groups=mesh['group'=8,'dom'=32] {'dom'}, dimensions={0} | all-to-all | bytes 1048576 | tf_op jit(solution)/shard_map/all_to_all | solution.py:54
  (114 shorter events, 52.8 us)
Async XLA Ops:
  7.2 17.6 %copy-start = (bf16[1024,1024]{1,0:T(8,128)(2,1)S(1)}, bf16[1024,1024]{1,0:T(8,128)(2,1)}, u32[]{:S(2)}) copy-start(bf16[1024,1024]{1,0:T(8,128)(2,1)} %param.16) | copy-start | bytes 6291460
  7.2 94.8 %reduce-scatter.4.cloned.1.call-start = ((), (), s32[]{:S(2)}) async-start(), calls=%async_computation.5 | async-start | bytes 1179648 | tf_op jit(solution)/shard_map/reduce_scatter | solution.py:106
  8.0 20.2 %copy-start.11 = (s32[32]{0:T(128)}, s32[32]{0:T(128)S(1)}, u32[]{:S(2)}) copy-start(s32[32]{0:T(128)S(1)} %fusion.11) | copy-start | bytes 388
  10.6 49.8 %collective-permute-start = (bf16[32,1024]{1,0:T(8,128)(2,1)S(1)}, bf16[32,1024]{1,0:T(8,128)(2,1)}, u32[]{:S(2)}, u32[]{:S(2)}) collective-permute-start(bf16[32,1024]{1,0:T(8,128)(2,1)S(1)} %gather_fusion.3), channel_id=1, source_target_pairs={{0,32},{32,64},{64,96},{96,128},{128,160},{160,192},{192,224},{224... | collective-permute-start | bytes 196616 | tf_op jit(solution)/shard_map/ppermute | solution.py:64
  13.1 50.5 %collective-permute-start.1 = (bf16[32,1024]{1,0:T(8,128)(2,1)S(1)}, bf16[32,1024]{1,0:T(8,128)(2,1)}, u32[]{:S(2)}, u32[]{:S(2)}) collective-permute-start(bf16[32,1024]{1,0:T(8,128)(2,1)S(1)} %gather_fusion.3), channel_id=1, source_target_pairs={{0,64},{32,96},{64,128},{96,160},{128,192},{160,224},{192,0},{224,... | collective-permute-start | bytes 196616 | tf_op jit(solution)/shard_map/ppermute | solution.py:64
  16.1 49.0 %collective-permute-start.2 = (bf16[32,1024]{1,0:T(8,128)(2,1)S(1)}, bf16[32,1024]{1,0:T(8,128)(2,1)}, u32[]{:S(2)}, u32[]{:S(2)}) collective-permute-start(bf16[32,1024]{1,0:T(8,128)(2,1)S(1)} %gather_fusion.3), channel_id=1, source_target_pairs={{0,96},{32,128},{64,160},{96,192},{128,224},{160,0},{192,32},{224,... | collective-permute-start | bytes 196616 | tf_op jit(solution)/shard_map/ppermute | solution.py:64
  19.8 46.1 %collective-permute-start.3 = (bf16[32,1024]{1,0:T(8,128)(2,1)S(1)}, bf16[32,1024]{1,0:T(8,128)(2,1)}, u32[]{:S(2)}, u32[]{:S(2)}) collective-permute-start(bf16[32,1024]{1,0:T(8,128)(2,1)S(1)} %gather_fusion.3), channel_id=1, source_target_pairs={{0,128},{32,160},{64,192},{96,224},{128,0},{160,32},{192,64},{224,... | collective-permute-start | bytes 196616 | tf_op jit(solution)/shard_map/ppermute | solution.py:64
  20.3 46.5 %collective-permute-start.4 = (bf16[32,1024]{1,0:T(8,128)(2,1)S(1)}, bf16[32,1024]{1,0:T(8,128)(2,1)S(1)}, u32[]{:S(2)}, u32[]{:S(2)}) collective-permute-start(bf16[32,1024]{1,0:T(8,128)(2,1)S(1)} %gather_fusion.3), channel_id=1, source_target_pairs={{0,160},{32,192},{64,224},{96,0},{128,32},{160,64},{192,96},{224,1... | collective-permute-start | bytes 196616 | tf_op jit(solution)/shard_map/ppermute | solution.py:64
  28.3 3.1 %copy-start.14 = (s32[1,4]{1,0:T(1,128)S(1)}, s32[1,4]{1,0:T(1,128)}, u32[]{:S(2)}) copy-start(s32[1,4]{1,0:T(1,128)} %param.20) | copy-start | bytes 52
  39.5 2.8 %copy-start.2 = (bf16[128,1024]{1,0:T(8,128)(2,1)S(1)}, bf16[128,1024]{1,0:T(8,128)(2,1)}, u32[]{:S(2)}) copy-start(bf16[128,1024]{1,0:T(8,128)(2,1)} %param.13) | copy-start | bytes 786436
  48.3 9.9 %slice-start = ((f32[7,128,1024]{2,0,1:T(8,128)}), f32[1,128,1024]{2,0,1:T(1,128)S(1)}, s32[]{:S(2)}) async-start(f32[7,128,1024]{2,0,1:T(8,128)} %copy-done.3), calls=%async_computation.8 | async-start | bytes 1048576 | tf_op jit(solution)/shard_map/slice | solution.py:105
  48.3 37.7 %all-to-all-start = ((bf16[32,2,16,1024]{3,2,1,0:T(8,128)(2,1)}), bf16[32,2,16,1024]{3,2,1,0:T(8,128)(2,1)}, u32[]{:S(2)}, u32[]{:S(2)}) async-start(bf16[32,2,16,1024]{3,2,1,0:T(8,128)(2,1)} %pad_maximum_fusion), calls=%async_computation.1 | async-start | bytes 4194304 | tf_op jit(solution)/shard_map/all_to_all | solution.py:109
  57.6 115.8 %reduce-scatter.6.cloned.1.call-start = ((), (), s32[]{:S(2)}) async-start(), calls=%async_computation.6 | async-start | bytes 2359296 | tf_op jit(solution)/shard_map/reduce_scatter | solution.py:43
  60.3 7.1 %collective-permute-start.5 = (bf16[32,1024]{1,0:T(8,128)(2,1)S(1)}, bf16[32,1024]{1,0:T(8,128)(2,1)S(1)}, u32[]{:S(2)}, u32[]{:S(2)}) collective-permute-start(bf16[32,1024]{1,0:T(8,128)(2,1)S(1)} %gather_fusion.3), channel_id=1, source_target_pairs={{0,192},{32,224},{64,0},{96,32},{128,64},{160,96},{192,128},{224,1... | collective-permute-start | bytes 196616 | tf_op jit(solution)/shard_map/ppermute | solution.py:64
  63.6 5.7 %collective-permute-start.6 = (bf16[32,1024]{1,0:T(8,128)(2,1)S(1)}, bf16[32,1024]{1,0:T(8,128)(2,1)S(1)}, u32[]{:S(2)}, u32[]{:S(2)}) collective-permute-start(bf16[32,1024]{1,0:T(8,128)(2,1)S(1)} %gather_fusion.3), channel_id=1, source_target_pairs={{0,224},{32,0},{64,32},{96,64},{128,96},{160,128},{192,160},{224,1... | collective-permute-start | bytes 196616 | tf_op jit(solution)/shard_map/ppermute | solution.py:64
  93.6 5.9 %copy-start.7 = (bf16[1,4,128,128]{3,2,1,0:T(8,128)(2,1)S(1)}, bf16[1,4,128,128]{3,2,1,0:T(8,128)(2,1)}, u32[]{:S(2)}) copy-start(bf16[1,4,128,128]{3,2,1,0:T(8,128)(2,1)} %param.21) | copy-start | bytes 393220
  96.4 5.5 %copy-start.12 = (s32[32]{0:T(128)S(1)}, s32[32]{0:T(128)}, u32[]{:S(2)}) copy-start(s32[32]{0:T(128)} %copy-done.11) | copy-start | bytes 388
  108.4 17.1 %copy-start.5 = (bf16[128,1024]{1,0:T(8,128)(2,1)}, bf16[128,1024]{1,0:T(8,128)(2,1)S(1)}, u32[]{:S(2)}) copy-start(bf16[128,1024]{1,0:T(8,128)(2,1)S(1)} %get-tuple-element.3) | copy-start | bytes 786436
  114.7 7.2 %collective-permute-start.7 = (f32[512,1024]{1,0:T(8,128)}, f32[512,1024]{1,0:T(8,128)}, u32[]{:S(2)}, u32[]{:S(2)}) collective-permute-start(f32[512,1024]{1,0:T(8,128)} %fusion.15), channel_id=1, source_target_pairs={{0,1},{1,0},{2,3},{3,2},{4,5},{5,4},{6,7},{7,6},{8,9},{9,8},{10,11... | collective-permute-start | bytes 6291464 | tf_op jit(solution)/shard_map/ppermute | solution.py:37
  126.7 27.0 %copy-start.10 = (pred[8]{0:T(512)(128)(4,1)S(1)}, pred[8]{0:T(512)(128)(4,1)}, u32[]{:S(2)}) copy-start(pred[8]{0:T(512)(128)(4,1)} %compare_and_fusion) | copy-start | bytes 28
  126.7 10.5 %collective-permute-start.8 = (bf16[32,1024]{1,0:T(8,128)(2,1)}, bf16[32,1024]{1,0:T(8,128)(2,1)}, u32[]{:S(2)}, u32[]{:S(2)}) collective-permute-start(bf16[32,1024]{1,0:T(8,128)(2,1)} %gather_fusion.6), channel_id=1, source_target_pairs={{0,32},{32,64},{64,96},{96,128},{128,160},{160,192},{192,224},{224... | collective-permute-start | bytes 196616 | tf_op jit(solution)/shard_map/ppermute | solution.py:64
  128.2 13.7 %collective-permute-start.9 = (bf16[32,1024]{1,0:T(8,128)(2,1)}, bf16[32,1024]{1,0:T(8,128)(2,1)}, u32[]{:S(2)}, u32[]{:S(2)}) collective-permute-start(bf16[32,1024]{1,0:T(8,128)(2,1)} %gather_fusion.6), channel_id=1, source_target_pairs={{0,64},{32,96},{64,128},{96,160},{128,192},{160,224},{192,0},{224,... | collective-permute-start | bytes 196616 | tf_op jit(solution)/shard_map/ppermute | solution.py:64
  128.2 15.2 %collective-permute-start.10 = (bf16[32,1024]{1,0:T(8,128)(2,1)}, bf16[32,1024]{1,0:T(8,128)(2,1)}, u32[]{:S(2)}, u32[]{:S(2)}) collective-permute-start(bf16[32,1024]{1,0:T(8,128)(2,1)} %gather_fusion.6), channel_id=1, source_target_pairs={{0,96},{32,128},{64,160},{96,192},{128,224},{160,0},{192,32},{224,... | collective-permute-start | bytes 196616 | tf_op jit(solution)/shard_map/ppermute | solution.py:64
  132.9 11.9 %collective-permute-start.11 = (bf16[32,1024]{1,0:T(8,128)(2,1)}, bf16[32,1024]{1,0:T(8,128)(2,1)}, u32[]{:S(2)}, u32[]{:S(2)}) collective-permute-start(bf16[32,1024]{1,0:T(8,128)(2,1)} %gather_fusion.6), channel_id=1, source_target_pairs={{0,128},{32,160},{64,192},{96,224},{128,0},{160,32},{192,64},{224,... | collective-permute-start | bytes 196616 | tf_op jit(solution)/shard_map/ppermute | solution.py:64
  133.8 12.4 %collective-permute-start.12 = (bf16[32,1024]{1,0:T(8,128)(2,1)}, bf16[32,1024]{1,0:T(8,128)(2,1)}, u32[]{:S(2)}, u32[]{:S(2)}) collective-permute-start(bf16[32,1024]{1,0:T(8,128)(2,1)} %gather_fusion.6), channel_id=1, source_target_pairs={{0,160},{32,192},{64,224},{96,0},{128,32},{160,64},{192,96},{224,1... | collective-permute-start | bytes 196616 | tf_op jit(solution)/shard_map/ppermute | solution.py:64
  137.1 17.7 %copy-start.4 = (bf16[512,1024]{1,0:T(8,128)(2,1)S(1)}, bf16[512,1024]{1,0:T(8,128)(2,1)}, u32[]{:S(2)}) copy-start(bf16[512,1024]{1,0:T(8,128)(2,1)} %gather_fusion.5) | copy-start | bytes 3145732
  137.1 17.8 %copy-start.6 = (bf16[128,1024]{1,0:T(8,128)(2,1)S(1)}, bf16[128,1024]{1,0:T(8,128)(2,1)}, u32[]{:S(2)}) copy-start(bf16[128,1024]{1,0:T(8,128)(2,1)} %copy-done.5) | copy-start | bytes 786436
  137.1 78.6 %reduce-scatter.8.cloned.1.call-start = ((), (), s32[]{:S(2)}) async-start(), calls=%async_computation.7 | async-start | bytes 2359296 | tf_op jit(solution)/shard_map/reduce_scatter | solution.py:43
  137.2 12.7 %collective-permute-start.13 = (bf16[32,1024]{1,0:T(8,128)(2,1)}, bf16[32,1024]{1,0:T(8,128)(2,1)S(1)}, u32[]{:S(2)}, u32[]{:S(2)}) collective-permute-start(bf16[32,1024]{1,0:T(8,128)(2,1)} %gather_fusion.6), channel_id=1, source_target_pairs={{0,192},{32,224},{64,0},{96,32},{128,64},{160,96},{192,128},{224,1... | collective-permute-start | bytes 196616 | tf_op jit(solution)/shard_map/ppermute | solution.py:64
  141.9 8.8 %collective-permute-start.14 = (bf16[32,1024]{1,0:T(8,128)(2,1)}, bf16[32,1024]{1,0:T(8,128)(2,1)S(1)}, u32[]{:S(2)}, u32[]{:S(2)}) collective-permute-start(bf16[32,1024]{1,0:T(8,128)(2,1)} %gather_fusion.6), channel_id=1, source_target_pairs={{0,224},{32,0},{64,32},{96,64},{128,96},{160,128},{192,160},{224,1... | collective-permute-start | bytes 196616 | tf_op jit(solution)/shard_map/ppermute | solution.py:64
  158.5 7.4 %copy-start.8 = (bf16[128,8,16,1,4]{0,4,3,2,1:T(4,128)(2,1)S(1)}, bf16[128,8,16,1,4]{0,4,3,2,1:T(4,128)(2,1)}, u32[]{:S(2)}) copy-start(bf16[128,8,16,1,4]{0,4,3,2,1:T(4,128)(2,1)} %get-tuple-element.16) | copy-start | bytes 393220
  159.4 6.5 %collective-permute-start.15 = (f32[512,1024]{1,0:T(8,128)S(1)}, f32[512,1024]{1,0:T(8,128)S(1)}, u32[]{:S(2)}, u32[]{:S(2)}) collective-permute-start(f32[512,1024]{1,0:T(8,128)S(1)} %fusion.16), channel_id=1, source_target_pairs={{0,1},{1,0},{2,3},{3,2},{4,5},{5,4},{6,7},{7,6},{8,9},{9,8},{10,11... | collective-permute-start | bytes 6291464 | tf_op jit(solution)/shard_map/ppermute | solution.py:37
  (4 other events, 7.5 us)
Sparse Core Ops, SparseCore 0:
  39.6 36.1 reduce-scatter.3
  137.3 36.1 reduce-scatter.5
  176.0 39.6 reduce-scatter.7

commit v9 on v5

--- a/solution.py
+++ b/solution.py
@@ -117,14 +117,17 @@
         jnp.bfloat16
     )
     product_first = pair_product(dz_first, agg_first, 0)
-    product_first, new_history = lax.optimization_barrier((product_first, new_history))
-    outgoing_first = reduce_in_group(product_first)
 
     hist_halo = hist_slots.reshape(-1, D)[halo_index]
     hub_second = gather_hubs(new_history[owned_hubs])
     agg_second = combine_tiles(new_history, hist_halo, hub_second, tile_cols, tile_vals)
-    outgoing_second = reduce_in_group(pair_product(grad_out, agg_second, 1))
-    grad_first, grad_second = reduce_over_dom(outgoing_first, outgoing_second, rows)
+    product_second = pair_product(grad_out, agg_second, 1)
+    n_group = lax.axis_size("group")
+    both = jnp.concatenate(
+        [product_first.reshape(n_group, -1, D), product_second.reshape(n_group, -1, D)], axis=1
+    )
+    outgoing = reduce_in_group(both.reshape(-1, D)).reshape(2, lax.axis_size("dom") // 2, -1, D)
+    grad_first, grad_second = reduce_over_dom(outgoing[0], outgoing[1], rows)
     return (new_history, vertex_grad.astype(jnp.bfloat16), grad_first, grad_second)
 
 

time: 230 us -> 215 us (0.935)
  waiting for transfers between devices: 93.2 us -> 78.2 us
  blocking collectives: 23.3 us -> 19 us
    all_to_all x2, waiting for transfers between devices: 30.3 us -> 14.2 us  [gather_hubs(): lax.all_to_all(copies, 'group', split_axis=0, concat_axis=0, tiled=True)]
    reduce_scatter x2 -> x1, waiting for transfers between devices: 42.3 us -> 49.2 us  [reduce_in_group(): lax.psum_scatter(pair.reshape(n_group, -1, width), 'group', scatter_dimen...]
    ppermute x2, waiting for transfers between devices: 7.57 us -> 1.7 us  [pair_product(): return kept + lax.ppermute(sent, 'dom', [(i, i ^ 1) for i in range(n_dom)])]
    all_to_all x1, blocking collectives: 23.3 us -> 19 us  [reduce_over_dom(): lax.all_to_all(outgoing, 'dom', split_axis=0, concat_axis=0, tiled=True)]
    concatenate x0 -> x1, other arithmetic: none -> 2.47 us  [on_device(): jnp.concatenate([product_first.reshape(n_group, -1, D), product_second.re...]
    unnamed x26 -> x30, local copies, waits for them, and re-layouts: 4.71 us -> 4.68 us
  transfers between devices with their start and end apart: 8 -> 7, of which waited for: 6 -> 5; matrix products, arithmetic and copies ran while one was open for 21% -> 24% of each run, Pallas kernels for 0% -> 0%
where the time goes in v9:
time: 215 us; the launch traced here: 214 us
  waiting for transfers between devices  78.2 us (36%)
  local copies, waits for them, and re-layouts  43.2 us (20%)
  starting transfers between devices  25.9 us (12%)
  blocking collectives  19 us (9%)
  matrix products  18.5 us (9%)
  other arithmetic  15.2 us (7%)
  between operations  14.4 us (7%)
    reduce_scatter x1, waiting for transfers between devices, reduce_in_group(): lax.psum_scatter(pair.reshape(n_group, -1, width), 'group', scatter_dimen...  49.2 us
    all_to_all x1, blocking collectives, reduce_over_dom(): lax.all_to_all(outgoing, 'dom', split_axis=0, concat_axis=0, tiled=True)  19 us
    all_to_all x2, waiting for transfers between devices, gather_hubs(): lax.all_to_all(copies, 'group', split_axis=0, concat_axis=0, tiled=True)  14.2 us
    all_to_all x1, waiting for transfers between devices, on_device(): lax.all_to_all(jnp.stack([feats[routes], history[routes]], axis=1), 'dom'...  13 us
    all_to_all x2, starting transfers between devices, gather_hubs(): lax.all_to_all(copies, 'group', split_axis=0, concat_axis=0, tiled=True)  12.3 us
    all_to_all x1, starting transfers between devices, on_device(): lax.all_to_all(jnp.stack([feats[routes], history[routes]], axis=1), 'dom'...  8.77 us
    dot_general x4, matrix products, weight_product(): lax.dot_general(left_rows, right_rows, (((0,), (0,)), ((), ())), preferre...  5.61 us
    gather x2, local copies, waits for them, and re-layouts, combine_tiles(): picked = source.reshape(-1, tile_vals.shape[2], feature_width)[tile_cols]  5.26 us
  transfers between devices with their start and end apart: 7, of which 5 were waited for; matrix products, arithmetic and copies ran while one was open for 24% of the time, Pallas kernels for 0%

profile of v9, /device:TPU:1, one launch (start us, length us, event | category | flops | bytes accessed | tf_op | source)
XLA Modules:
  0.0 214.4 jit_solution(7443454966539164773)
XLA Ops:
  8.2 3.8 %gather_fusion.1 = bf16[512,1024]{1,0:T(8,128)(2,1)S(1)} fusion(bf16[128,1024]{1,0:T(8,128)(2,1)} %param.11, s32[1024]{0:T(1024)S(1)} %pad_clamp_fusion.3), kind=kCustom, calls=%fused_computation.1 | custom fusion | bytes 2099200 | tf_op jit(solution)/shard_map/gather | solution.py:106
  12.0 2.8 %gather_fusion = bf16[512,1024]{1,0:T(8,128)(2,1)} fusion(bf16[128,1024]{1,0:T(8,128)(2,1)S(1)} %copy-done.1, s32[1024]{0:T(1024)S(1)} %pad_clamp_fusion.3), kind=kCustom, calls=%fused_computation | custom fusion | bytes 2099200 | tf_op jit(solution)/shard_map/gather | solution.py:106
  14.8 2.8 %pad_maximum_fusion.1 = bf16[32,2,16,1024]{3,2,1,0:T(8,128)(2,1)} fusion(bf16[32,1,16,1024]{3,2,1,0:T(8,128)(2,1)S(1)} %bitcast.87, bf16[32,1,16,1024]{3,2,1,0:T(8,128)(2,1)} %bitcast.88), kind=kLoop, calls=%fused_computation.10 | loop fusion | flops 1048576 | bytes 4194304 | tf_op jit(solution)/shard_map/stack | solution.py:106
  17.6 8.8 %all-to-all-start = ((bf16[32,2,16,1024]{3,2,1,0:T(8,128)(2,1)}), bf16[32,2,16,1024]{3,2,1,0:T(8,128)(2,1)}, u32[]{:S(2)}, u32[]{:S(2)}) async-start(bf16[32,2,16,1024]{3,2,1,0:T(8,128)(2,1)} %pad_maximum_fusion.1), calls=%async_computation | async-start | bytes 4194304 | tf_op jit(solution)/shard_map/all_to_all | solution.py:105
  26.4 2.5 %convolution_bitcast_fusion = f32[4,128,1024]{1,2,0:T(8,128)} fusion(bf16[128,1024]{1,0:T(8,128)(2,1)S(1)} %copy-done.7, bf16[1024,1024]{1,0:T(8,128)(2,1)S(1)} %copy-done, bf16[1,4,128,128]{3,2,1,0:T(8,128)(2,1)S(1)} %copy-done.6), kind=kOutput, calls=%fused_computation.15 | convolution fusion | flops 402784256 | bytes 4587520 | tf_op jit(solution)/shard_map/rtij,rid->rtjd/dot_general | solution.py:89
  28.9 3.1 %copy.50 = f32[4,128,1024]{2,0,1:T(4,128)} copy(f32[4,128,1024]{1,2,0:T(8,128)} %convolution_bitcast_fusion) | data formatting | bytes 4194304 | tf_op jit(solution)/shard_map/rtij,rid->rtjd/dot_general | solution.py:89
  32.0 4.2 %fusion.7 = f32[7,128,1024]{2,0,1:T(8,128)S(1)} fusion(f32[4,128,1024]{2,0,1:T(4,128)} %copy.50, s32[4]{0:T(128)S(1)} %bitcast.96), kind=kOutput, calls=%fused_computation.44 | convolution fusion | flops 44040220 | bytes 5767184 | tf_op jit(solution)/shard_map/rts,rtjd->sjd/dot_general | solution.py:98
  36.2 1.9 copy-done.2
  41.7 13.0 %all-to-all-done = bf16[32,2,16,1024]{3,2,1,0:T(8,128)(2,1)} async-done(((bf16[32,2,16,1024]{3,2,1,0:T(8,128)(2,1)}), bf16[32,2,16,1024]{3,2,1,0:T(8,128)(2,1)}, u32[]{:S(2)}, u32[]{:S(2)}) %all-to-all-start) | async-done | bytes 2097184 | tf_op jit(solution)/shard_map/all_to_all | solution.py:105
  55.6 8.2 %all-to-all-start.1 = ((bf16[8,32,1024]{2,1,0:T(8,128)(2,1)}), bf16[8,32,1024]{2,1,0:T(8,128)(2,1)}, u32[]{:S(2)}, u32[]{:S(2)}) async-start(bf16[8,32,1024]{2,1,0:T(8,128)(2,1)} %broadcast_in_dim.65), calls=%async_computation.1 | async-start | bytes 1048576 | tf_op jit(solution)/shard_map/all_to_all | solution.py:64
  63.8 2.8 %fusion.12 = (bf16[32,1,16,1024]{3,2,1,0:T(8,128)(2,1)S(1)}, bf16[32,1,16,1024]{3,2,1,0:T(8,128)(2,1)}) fusion(bf16[32,2,16,1024]{3,2,1,0:T(8,128)(2,1)} %all-to-all-done), kind=kLoop, calls=%fused_computation.53 | loop fusion | bytes 4194304 | tf_op jit(solution)/shard_map/slice | solution.py:109
  66.6 4.8 %gather_fusion.2 = bf16[512,1024]{1,0:T(8,128)(2,1)} fusion(bf16[512,1024]{1,0:T(8,128)(2,1)} %bitcast.80, s32[1024]{0:T(1024)S(1)} %pad_clamp_fusion.2), kind=kCustom, calls=%fused_computation.2 | custom fusion | bytes 2099200 | tf_op jit(solution)/shard_map/gather | solution.py:111
  71.5 13.1 %all-to-all-done.1 = bf16[8,32,1024]{2,1,0:T(8,128)(2,1)} async-done(((bf16[8,32,1024]{2,1,0:T(8,128)(2,1)}), bf16[8,32,1024]{2,1,0:T(8,128)(2,1)}, u32[]{:S(2)}, u32[]{:S(2)}) %all-to-all-start.1) | async-done | bytes 524320 | tf_op jit(solution)/shard_map/all_to_all | solution.py:64
  84.6 2.8 %pad_maximum_fusion.2 = bf16[896,1024]{1,0:T(8,128)(2,1)} fusion(bf16[256,1024]{1,0:T(8,128)(2,1)} %bitcast.8, bf16[512,1024]{1,0:T(8,128)(2,1)} %gather_fusion.2, bf16[128,1024]{1,0:T(8,128)(2,1)S(1)} %copy-done.1), kind=kLoop, calls=%fused_computation.11 | loop fusion | flops 5505024 | bytes 3670016 | tf_op jit(solution)/shard_map/concatenate | solution.py:15
  87.4 3.1 %gather_fusion.4 = bf16[4,128,1024]{2,1,0:T(8,128)(2,1)} fusion(bf16[7,128,1024]{2,1,0:T(8,128)(2,1)} %bitcast.85, s32[1024]{0:T(1024)S(1)} %pad_clamp_fusion), kind=kCustom, calls=%fused_computation.4 | custom fusion | bytes 2097168 | tf_op jit(solution)/shard_map/gather | solution.py:17
  90.5 2.4 %fusion = bf16[1024,128]{1,0:T(8,128)(2,1)} fusion(bf16[4,128,1024]{2,1,0:T(8,128)(2,1)} %gather_fusion.4, bf16[1,4,128,128]{3,2,1,0:T(8,128)(2,1)S(1)} %copy-done.6), kind=kOutput, calls=%fused_computation.18 | convolution fusion | flops 134348800 | bytes 1441792 | tf_op jit(solution)/shard_map/rtij,rtjd->rid/dot_general | solution.py:18
  92.9 3.0 %scatter_fusion = f32[128,1024]{1,0:T(8,128)} fusion(f32[128,1024]{1,0:T(8,128)} %bitcast.83, s32[32]{0:T(128)S(1)} %fusion.10, f32[32,1024]{1,0:T(8,128)} %reduce-scatter.3.cloned.1.call-done), kind=kCustom, calls=%fused_computation.8 | custom fusion | flops 32768 | bytes 393344 | tf_op jit(solution)/shard_map/scatter-add | solution.py:103
  95.9 3.3 %multiply_convert_fusion = (bf16[128,1024]{1,0:T(8,128)(2,1)}, bf16[128,1024]{1,0:T(8,128)(2,1)}, bf16[128,1024]{1,0:T(8,128)(2,1)S(1)}) fusion(f32[128,1024]{1,0:T(8,128)} %scatter_fusion, bf16[1024,128]{1,0:T(8,128)(2,1)} %fusion, bf16[1024,1024]{1,0:T(8,128)(2,1)} %param.13), kind=kOutput, calls=%fused_computation.24 | convolution fusion | flops 270008320 | bytes 3670016 | tf_op jit(solution)/shard_map/dot_general | solution.py:113
  102.2 4.1 %all-to-all-start.2 = ((bf16[8,32,1024]{2,1,0:T(8,128)(2,1)}), bf16[8,32,1024]{2,1,0:T(8,128)(2,1)}, u32[]{:S(2)}, u32[]{:S(2)}) async-start(bf16[8,32,1024]{2,1,0:T(8,128)(2,1)} %broadcast_in_dim.70), calls=%async_computation.3 | async-start | bytes 1048576 | tf_op jit(solution)/shard_map/all_to_all | solution.py:64
  106.6 1.8 copy.54
  108.4 1.8 constant_dynamic-slice_fusion.1
  110.2 2.8 %gather_fusion.5 = bf16[512,1024]{1,0:T(8,128)(2,1)} fusion(bf16[512,1024]{1,0:T(8,128)(2,1)S(1)} %bitcast.79, s32[1024]{0:T(1024)S(1)} %pad_clamp_fusion.2), kind=kCustom, calls=%fused_computation.5 | custom fusion | bytes 2099200 | tf_op jit(solution)/shard_map/gather | solution.py:121
  113.0 1.9 copy.53
  116.5 2.7 %fusion.14 = f32[512,1024]{1,0:T(8,128)} fusion(bf16[128,512]{0,1:T(8,128)(2,1)S(1)} %bitcast.95, bf16[1024,128]{1,0:T(8,128)(2,1)} %fusion), kind=kOutput, calls=%fused_computation.55 | convolution fusion | flops 134217728 | bytes 2490368 | tf_op jit(solution)/shard_map/dot_general | solution.py:23
  119.2 1.9 collective-permute-start
  122.3 2.4 %pad_maximum_fusion.3 = bf16[896,1024]{1,0:T(8,128)(2,1)} fusion(bf16[256,1024]{1,0:T(8,128)(2,1)} %bitcast.26, bf16[512,1024]{1,0:T(8,128)(2,1)S(1)} %copy-done.3, bf16[128,1024]{1,0:T(8,128)(2,1)S(1)} %get-tuple-element.12), kind=kLoop, calls=%fused_computation.12 | loop fusion | flops 5505024 | bytes 3670016 | tf_op jit(solution)/shard_map/concatenate | solution.py:15
  124.7 2.1 %gather_fusion.7 = bf16[4,128,1024]{2,1,0:T(8,128)(2,1)S(1)} fusion(bf16[7,128,1024]{2,1,0:T(8,128)(2,1)} %bitcast.84, s32[1024]{0:T(1024)S(1)} %pad_clamp_fusion), kind=kCustom, calls=%fused_computation.7 | custom fusion | bytes 2097168 | tf_op jit(solution)/shard_map/gather | solution.py:17
  127.8 2.6 %collective-permute-start.1 = (f32[512,1024]{1,0:T(8,128)S(1)}, f32[512,1024]{1,0:T(8,128)S(1)}, u32[]{:S(2)}, u32[]{:S(2)}) collective-permute-start(f32[512,1024]{1,0:T(8,128)S(1)} %fusion.15), channel_id=1, source_target_pairs={{0,1},{1,0},{2,3},{3,2},{4,5},{5,4},{6,7},{7,6},{8,9},{9,8},{10,11... | collective-permute-start | bytes 6291464 | tf_op jit(solution)/shard_map/ppermute | solution.py:37
  130.5 2.1 convolution_add_fusion.1
  134.7 2.5 %pad_maximum_fusion = f32[8,128,1024]{2,1,0:T(8,128)} fusion(f32[8,64,1024]{2,1,0:T(8,128)S(1)} %bitcast.82, f32[8,64,1024]{2,1,0:T(8,128)S(1)} %bitcast.81), kind=kLoop, calls=%fused_computation.9 | loop fusion | flops 1048576 | bytes 8388608 | tf_op jit(solution)/shard_map/concatenate | solution.py:126
  137.3 49.2 %reduce-scatter.5.cloned.1.call-done = f32[1,128,1024]{2,1,0:T(8,128)} async-done(((f32[8,128,1024]{2,1,0:T(8,128)}), f32[1,128,1024]{2,1,0:T(8,128)}) %reduce-scatter.5.cloned.1.call-update) | async-done | bytes 524304 | tf_op jit(solution)/shard_map/reduce_scatter | solution.py:43
  187.9 19.0 %all_to_all.20 = f32[32,4,1024]{2,1,0:T(4,128)S(1)} all-to-all(f32[32,4,1024]{2,1,0:T(4,128)S(1)} %bitcast_select_fusion), channel_id=1, replica_groups=mesh['group'=8,'dom'=32] {'dom'}, dimensions={0} | all-to-all | bytes 1048576 | tf_op jit(solution)/shard_map/all_to_all | solution.py:54
  (67 shorter events, 16.7 us)
Async XLA Ops:
  7.2 19.2 %copy-start = (bf16[1024,1024]{1,0:T(8,128)(2,1)S(1)}, bf16[1024,1024]{1,0:T(8,128)(2,1)}, u32[]{:S(2)}) copy-start(bf16[1024,1024]{1,0:T(8,128)(2,1)} %param.14) | copy-start | bytes 6291460
  8.2 3.8 %copy-start.1 = (bf16[128,1024]{1,0:T(8,128)(2,1)S(1)}, bf16[128,1024]{1,0:T(8,128)(2,1)}, u32[]{:S(2)}) copy-start(bf16[128,1024]{1,0:T(8,128)(2,1)} %param.10) | copy-start | bytes 786436
  17.6 8.8 %copy-start.6 = (bf16[1,4,128,128]{3,2,1,0:T(8,128)(2,1)S(1)}, bf16[1,4,128,128]{3,2,1,0:T(8,128)(2,1)}, u32[]{:S(2)}) copy-start(bf16[1,4,128,128]{3,2,1,0:T(8,128)(2,1)} %param.19) | copy-start | bytes 393220
  17.6 8.8 %copy-start.7 = (bf16[128,1024]{1,0:T(8,128)(2,1)S(1)}, bf16[128,1024]{1,0:T(8,128)(2,1)}, u32[]{:S(2)}) copy-start(bf16[128,1024]{1,0:T(8,128)(2,1)} %param.12) | copy-start | bytes 786436
  17.6 37.2 %all-to-all-start = ((bf16[32,2,16,1024]{3,2,1,0:T(8,128)(2,1)}), bf16[32,2,16,1024]{3,2,1,0:T(8,128)(2,1)}, u32[]{:S(2)}, u32[]{:S(2)}) async-start(bf16[32,2,16,1024]{3,2,1,0:T(8,128)(2,1)} %pad_maximum_fusion.1), calls=%async_computation | async-start | bytes 4194304 | tf_op jit(solution)/shard_map/all_to_all | solution.py:105
  26.3 66.6 %reduce-scatter.3.cloned.1.call-start = ((), (), s32[]{:S(2)}) async-start(), calls=%async_computation.6 | async-start | bytes 1179648 | tf_op jit(solution)/shard_map/reduce_scatter | solution.py:102
  28.9 3.1 %copy-start.12 = (s32[1,4]{1,0:T(1,128)S(1)}, s32[1,4]{1,0:T(1,128)}, u32[]{:S(2)}) copy-start(s32[1,4]{1,0:T(1,128)} %param.18) | copy-start | bytes 52
  36.2 1.9 copy-start.2
  38.7 1.4 copy-start.13
  38.7 2.1 slice-start
  40.1 23.6 %copy-start.11 = (s32[512]{0:T(512)S(1)}, s32[512]{0:T(512)}, u32[]{:S(2)}) copy-start(s32[512]{0:T(512)} %param.16) | copy-start | bytes 6148
  55.6 29.0 %all-to-all-start.1 = ((bf16[8,32,1024]{2,1,0:T(8,128)(2,1)}), bf16[8,32,1024]{2,1,0:T(8,128)(2,1)}, u32[]{:S(2)}, u32[]{:S(2)}) async-start(bf16[8,32,1024]{2,1,0:T(8,128)(2,1)} %broadcast_in_dim.65), calls=%async_computation.1 | async-start | bytes 1048576 | tf_op jit(solution)/shard_map/all_to_all | solution.py:64
  99.3 23.0 %copy-start.4 = (bf16[128,1024]{1,0:T(8,128)(2,1)}, bf16[128,1024]{1,0:T(8,128)(2,1)S(1)}, u32[]{:S(2)}) copy-start(bf16[128,1024]{1,0:T(8,128)(2,1)S(1)} %get-tuple-element.12) | copy-start | bytes 786436
  102.2 20.1 %all-to-all-start.2 = ((bf16[8,32,1024]{2,1,0:T(8,128)(2,1)}), bf16[8,32,1024]{2,1,0:T(8,128)(2,1)}, u32[]{:S(2)}, u32[]{:S(2)}) async-start(bf16[8,32,1024]{2,1,0:T(8,128)(2,1)} %broadcast_in_dim.70), calls=%async_computation.3 | async-start | bytes 1048576 | tf_op jit(solution)/shard_map/all_to_all | solution.py:64
  106.4 80.1 %reduce-scatter.5.cloned.1.call-start = ((), (), s32[]{:S(2)}) async-start(), calls=%async_computation.7 | async-start | bytes 4718592 | tf_op jit(solution)/shard_map/reduce_scatter | solution.py:43
  113.0 9.3 %copy-start.3 = (bf16[512,1024]{1,0:T(8,128)(2,1)S(1)}, bf16[512,1024]{1,0:T(8,128)(2,1)}, u32[]{:S(2)}) copy-start(bf16[512,1024]{1,0:T(8,128)(2,1)} %gather_fusion.5) | copy-start | bytes 3145732
  119.2 11.2 %collective-permute-start = (f32[512,1024]{1,0:T(8,128)}, f32[512,1024]{1,0:T(8,128)}, u32[]{:S(2)}, u32[]{:S(2)}) collective-permute-start(f32[512,1024]{1,0:T(8,128)} %fusion.14), channel_id=1, source_target_pairs={{0,1},{1,0},{2,3},{3,2},{4,5},{5,4},{6,7},{7,6},{8,9},{9,8},{10,11... | collective-permute-start | bytes 6291464 | tf_op jit(solution)/shard_map/ppermute | solution.py:37
  124.7 2.7 %copy-start.9 = (bf16[128,8,16,1,4]{0,4,3,2,1:T(4,128)(2,1)S(1)}, bf16[128,8,16,1,4]{0,4,3,2,1:T(4,128)(2,1)}, u32[]{:S(2)}) copy-start(bf16[128,8,16,1,4]{0,4,3,2,1:T(4,128)(2,1)} %get-tuple-element.16) | copy-start | bytes 393220
  126.9 3.6 %copy-start.5 = (bf16[1024,128]{1,0:T(8,128)(2,1)S(1)}, bf16[1024,128]{1,0:T(8,128)(2,1)}, u32[]{:S(2)}) copy-start(bf16[1024,128]{1,0:T(8,128)(2,1)} %fusion) | copy-start | bytes 786436
  126.9 3.6 %copy-start.10 = (bf16[128,8,16,1,4]{0,4,3,2,1:T(4,128)(2,1)S(1)}, bf16[128,8,16,1,4]{0,4,3,2,1:T(4,128)(2,1)}, u32[]{:S(2)}) copy-start(bf16[128,8,16,1,4]{0,4,3,2,1:T(4,128)(2,1)} %get-tuple-element.13) | copy-start | bytes 393220
  127.8 6.4 %collective-permute-start.1 = (f32[512,1024]{1,0:T(8,128)S(1)}, f32[512,1024]{1,0:T(8,128)S(1)}, u32[]{:S(2)}, u32[]{:S(2)}) collective-permute-start(f32[512,1024]{1,0:T(8,128)S(1)} %fusion.15), channel_id=1, source_target_pairs={{0,1},{1,0},{2,3},{3,2},{4,5},{5,4},{6,7},{7,6},{8,9},{9,8},{10,11... | collective-permute-start | bytes 6291464 | tf_op jit(solution)/shard_map/ppermute | solution.py:37
  130.4 3.8 %copy-start.8 = (bf16[128,8,16,1,4]{0,4,3,2,1:T(4,128)(2,1)S(1)}, bf16[128,8,16,1,4]{0,4,3,2,1:T(4,128)(2,1)}, u32[]{:S(2)}) copy-start(bf16[128,8,16,1,4]{0,4,3,2,1:T(4,128)(2,1)} %get-tuple-element.15) | copy-start | bytes 393220
Sparse Core Ops, SparseCore 0:
  40.3 42.9 reduce-scatter.2
  137.3 49.1 reduce-scatter.4

commit v10 on v9

--- a/solution.py
+++ b/solution.py
@@ -102,11 +102,8 @@
     hub_grad = lax.psum_scatter(spread[V_DEV + HALO :], "group", scatter_dimension=0, tiled=True)
     vertex_grad = own_grad.at[owned_hubs].add(hub_grad)
 
-    both_slots = lax.all_to_all(
-        jnp.stack([feats[routes], history[routes]], axis=1), "dom", split_axis=0, concat_axis=0, tiled=True
-    )
-    feat_slots = both_slots[:, 0]
-    hist_slots = both_slots[:, 1]
+    feat_slots = lax.all_to_all(feats[routes], "dom", split_axis=0, concat_axis=0, tiled=True)
+    hist_slots = lax.all_to_all(history[routes], "dom", split_axis=0, concat_axis=0, tiled=True)
     hub_first = gather_hubs(feats[owned_hubs])
     feat_halo = feat_slots.reshape(-1, D)[halo_index]
     agg_first = combine_tiles(feats, feat_halo, hub_first, tile_cols, tile_vals)

time: 215 us -> 210 us (0.977)
  waiting for transfers between devices: 78.2 us -> 73.2 us
  other arithmetic: 15.2 us -> 12.4 us
  starting transfers between devices: 25.9 us -> 28.2 us
    all_to_all x2, waiting for transfers between devices: 14.2 us -> 5.82 us  [gather_hubs(): lax.all_to_all(copies, 'group', split_axis=0, concat_axis=0, tiled=True)]
    ppermute x2, starting transfers between devices: 4.55 us -> 1.06 us  [pair_product(): return kept + lax.ppermute(sent, 'dom', [(i, i ^ 1) for i in range(n_dom)])]
    all_to_all x2, starting transfers between devices: 12.3 us -> 15.3 us  [gather_hubs(): lax.all_to_all(copies, 'group', split_axis=0, concat_axis=0, tiled=True)]
    slice x1 -> x0, local copies, waits for them, and re-layouts: 2.81 us -> none  [on_device(): hist_slots = both_slots[:, 1]]
    all_to_all x1 -> x2, starting transfers between devices: 8.77 us -> 11.6 us  [the longest x1 7.63 us: on_device(): lax.all_to_all(feats[routes], 'dom', split_axis=0, concat_axis=0, tiled=T...]
    another operation x1 -> x0, other arithmetic: 2.79 us -> none  [on_device(): jnp.stack([feats[routes], history[routes]], axis=1)]
    slice x2 -> x1, local copies, waits for them, and re-layouts: 0.01 us -> 2.67 us  [on_device(): own_grad = spread[:V_DEV]]
    reduce_scatter x1, waiting for transfers between devices: 49.2 us -> 51.5 us  [reduce_in_group(): lax.psum_scatter(pair.reshape(n_group, -1, width), 'group', scatter_dimen...]
  transfers between devices with their start and end apart: 7 -> 8, of which waited for: 5 -> 5; matrix products, arithmetic and copies ran while one was open for 24% -> 30% of each run, Pallas kernels for 0% -> 0%
where the time goes in v10:
time: 210 us; the launch traced here: 209 us
  waiting for transfers between devices  73.2 us (35%)
  local copies, waits for them, and re-layouts  43.2 us (21%)
  starting transfers between devices  28.2 us (13%)
  blocking collectives  19 us (9%)
  matrix products  18.5 us (9%)
  between operations  14.4 us (7%)
  other arithmetic  12.4 us (6%)
    reduce_scatter x1, waiting for transfers between devices, reduce_in_group(): lax.psum_scatter(pair.reshape(n_group, -1, width), 'group', scatter_dimen...  51.5 us
    all_to_all x1, blocking collectives, reduce_over_dom(): lax.all_to_all(outgoing, 'dom', split_axis=0, concat_axis=0, tiled=True)  19 us
    all_to_all x2, starting transfers between devices, gather_hubs(): lax.all_to_all(copies, 'group', split_axis=0, concat_axis=0, tiled=True)  15.3 us
    all_to_all x1, waiting for transfers between devices, on_device(): lax.all_to_all(feats[routes], 'dom', split_axis=0, concat_axis=0, tiled=T...  14.1 us
    all_to_all x1, starting transfers between devices, on_device(): lax.all_to_all(feats[routes], 'dom', split_axis=0, concat_axis=0, tiled=T...  7.63 us
    all_to_all x2, waiting for transfers between devices, gather_hubs(): lax.all_to_all(copies, 'group', split_axis=0, concat_axis=0, tiled=True)  5.82 us
    dot_general x4, matrix products, weight_product(): lax.dot_general(left_rows, right_rows, (((0,), (0,)), ((), ())), preferre...  5.62 us
    gather x2, local copies, waits for them, and re-layouts, combine_tiles(): picked = source.reshape(-1, tile_vals.shape[2], feature_width)[tile_cols]  5.24 us
  transfers between devices with their start and end apart: 8, of which 5 were waited for; matrix products, arithmetic and copies ran while one was open for 30% of the time, Pallas kernels for 0%

profile of v10, /device:TPU:1, one launch (start us, length us, event | category | flops | bytes accessed | tf_op | source)
XLA Modules:
  0.0 208.9 jit_solution(15349469711690297101)
XLA Ops:
  10.5 9.0 %all-to-all-start.1 = ((bf16[8,32,1024]{2,1,0:T(8,128)(2,1)}), bf16[8,32,1024]{2,1,0:T(8,128)(2,1)S(1)}, u32[]{:S(2)}, u32[]{:S(2)}) async-start(bf16[8,32,1024]{2,1,0:T(8,128)(2,1)} %broadcast_in_dim.65), calls=%async_computation.1 | async-start | bytes 1048576 | tf_op jit(solution)/shard_map/all_to_all | solution.py:64
  19.6 2.5 %convolution_bitcast_fusion = f32[4,128,1024]{1,2,0:T(8,128)} fusion(bf16[128,1024]{1,0:T(8,128)(2,1)S(1)} %copy-done.9, bf16[1024,1024]{1,0:T(8,128)(2,1)S(1)} %copy-done, bf16[1,4,128,128]{3,2,1,0:T(8,128)(2,1)S(1)} %copy-done.8), kind=kOutput, calls=%fused_computation.14 | convolution fusion | flops 402784256 | bytes 4587520 | tf_op jit(solution)/shard_map/rtij,rid->rtjd/dot_general | solution.py:89
  22.1 3.1 %copy.35 = f32[4,128,1024]{2,0,1:T(4,128)} copy(f32[4,128,1024]{1,2,0:T(8,128)} %convolution_bitcast_fusion) | data formatting | bytes 4194304 | tf_op jit(solution)/shard_map/rtij,rid->rtjd/dot_general | solution.py:89
  25.2 4.2 %fusion.7 = f32[7,128,1024]{2,0,1:T(8,128)S(1)} fusion(f32[4,128,1024]{2,0,1:T(4,128)} %copy.35, s32[4]{0:T(128)S(1)} %bitcast.92), kind=kOutput, calls=%fused_computation.43 | convolution fusion | flops 44040220 | bytes 5767184 | tf_op jit(solution)/shard_map/rts,rtjd->sjd/dot_general | solution.py:98
  29.4 1.9 copy-done.3
  33.5 2.8 %gather_fusion = bf16[512,1024]{1,0:T(8,128)(2,1)} fusion(bf16[128,1024]{1,0:T(8,128)(2,1)S(1)} %copy-done.1, s32[1024]{0:T(1024)S(1)} %pad_clamp_fusion.3), kind=kCustom, calls=%fused_computation | custom fusion | bytes 2099200 | tf_op jit(solution)/shard_map/gather | solution.py:105
  37.5 7.6 %all-to-all-start = ((bf16[32,16,1024]{2,1,0:T(8,128)(2,1)}), bf16[32,16,1024]{2,1,0:T(8,128)(2,1)}, u32[]{:S(2)}, u32[]{:S(2)}) async-start(bf16[32,16,1024]{2,1,0:T(8,128)(2,1)} %bitcast.82), calls=%async_computation | async-start | bytes 2097152 | tf_op jit(solution)/shard_map/all_to_all | solution.py:105
  45.2 2.8 %gather_fusion.4 = bf16[512,1024]{1,0:T(8,128)(2,1)} fusion(bf16[128,1024]{1,0:T(8,128)(2,1)S(1)} %copy-done.2, s32[1024]{0:T(1024)S(1)} %pad_clamp_fusion.3), kind=kCustom, calls=%fused_computation.4 | custom fusion | bytes 2099200 | tf_op jit(solution)/shard_map/gather | solution.py:106
  48.0 14.1 %all-to-all-done = bf16[32,16,1024]{2,1,0:T(8,128)(2,1)} async-done(((bf16[32,16,1024]{2,1,0:T(8,128)(2,1)}), bf16[32,16,1024]{2,1,0:T(8,128)(2,1)}, u32[]{:S(2)}, u32[]{:S(2)}) %all-to-all-start) | async-done | bytes 1048608 | tf_op jit(solution)/shard_map/all_to_all | solution.py:105
  62.1 3.9 %all-to-all-start.2 = ((bf16[32,16,1024]{2,1,0:T(8,128)(2,1)}), bf16[32,16,1024]{2,1,0:T(8,128)(2,1)S(1)}, u32[]{:S(2)}, u32[]{:S(2)}) async-start(bf16[32,16,1024]{2,1,0:T(8,128)(2,1)} %bitcast.81), calls=%async_computation.3 | async-start | bytes 2097152 | tf_op jit(solution)/shard_map/all_to_all | solution.py:106
  66.1 2.7 %slice.42 = f32[1,128,1024]{2,0,1:T(1,128)S(1)} slice(f32[7,128,1024]{2,0,1:T(8,128)} %copy-done.3), slice={[0:1], [0:128], [0:1024]} | slice | bytes 1048576 | tf_op jit(solution)/shard_map/slice | solution.py:101
  69.6 4.9 %gather_fusion.1 = bf16[512,1024]{1,0:T(8,128)(2,1)} fusion(bf16[512,1024]{1,0:T(8,128)(2,1)} %bitcast.2, s32[1024]{0:T(1024)S(1)} %pad_clamp_fusion.2), kind=kCustom, calls=%fused_computation.1 | custom fusion | bytes 2099200 | tf_op jit(solution)/shard_map/gather | solution.py:108
  74.5 2.8 %pad_maximum_fusion.1 = bf16[896,1024]{1,0:T(8,128)(2,1)} fusion(bf16[256,1024]{1,0:T(8,128)(2,1)} %bitcast.84, bf16[512,1024]{1,0:T(8,128)(2,1)} %gather_fusion.1, bf16[128,1024]{1,0:T(8,128)(2,1)S(1)} %copy-done.1), kind=kLoop, calls=%fused_computation.10 | loop fusion | flops 5505024 | bytes 3670016 | tf_op jit(solution)/shard_map/concatenate | solution.py:15
  77.3 3.1 %gather_fusion.3 = bf16[4,128,1024]{2,1,0:T(8,128)(2,1)} fusion(bf16[7,128,1024]{2,1,0:T(8,128)(2,1)} %bitcast.80, s32[1024]{0:T(1024)S(1)} %pad_clamp_fusion), kind=kCustom, calls=%fused_computation.3 | custom fusion | bytes 2097168 | tf_op jit(solution)/shard_map/gather | solution.py:17
  80.4 2.4 %fusion = bf16[1024,128]{1,0:T(8,128)(2,1)} fusion(bf16[4,128,1024]{2,1,0:T(8,128)(2,1)} %gather_fusion.3, bf16[1,4,128,128]{3,2,1,0:T(8,128)(2,1)S(1)} %copy-done.8), kind=kOutput, calls=%fused_computation.17 | convolution fusion | flops 134348800 | bytes 1441792 | tf_op jit(solution)/shard_map/rtij,rtjd->rid/dot_general | solution.py:18
  82.8 3.0 %scatter_fusion = f32[128,1024]{1,0:T(8,128)} fusion(f32[128,1024]{1,0:T(8,128)} %bitcast.78, s32[32]{0:T(128)S(1)} %fusion.10, f32[32,1024]{1,0:T(8,128)} %reduce-scatter.3.cloned.1.call-done), kind=kCustom, calls=%fused_computation.8 | custom fusion | flops 32768 | bytes 393344 | tf_op jit(solution)/shard_map/scatter-add | solution.py:103
  85.8 3.3 %multiply_convert_fusion = (bf16[128,1024]{1,0:T(8,128)(2,1)}, bf16[128,1024]{1,0:T(8,128)(2,1)}, bf16[128,1024]{1,0:T(8,128)(2,1)S(1)}) fusion(f32[128,1024]{1,0:T(8,128)} %scatter_fusion, bf16[1024,128]{1,0:T(8,128)(2,1)} %fusion, bf16[1024,1024]{1,0:T(8,128)(2,1)} %param.13), kind=kOutput, calls=%fused_computation.23 | convolution fusion | flops 270008320 | bytes 3670016 | tf_op jit(solution)/shard_map/dot_general | solution.py:110
  92.1 6.3 %all-to-all-start.3 = ((bf16[8,32,1024]{2,1,0:T(8,128)(2,1)}), bf16[8,32,1024]{2,1,0:T(8,128)(2,1)}, u32[]{:S(2)}, u32[]{:S(2)}) async-start(bf16[8,32,1024]{2,1,0:T(8,128)(2,1)} %broadcast_in_dim.70), calls=%async_computation.4 | async-start | bytes 1048576 | tf_op jit(solution)/shard_map/all_to_all | solution.py:64
  98.6 1.8 copy.39
  100.4 1.8 constant_dynamic-slice_fusion.1
  102.2 2.8 %gather_fusion.5 = bf16[512,1024]{1,0:T(8,128)(2,1)} fusion(bf16[512,1024]{1,0:T(8,128)(2,1)S(1)} %bitcast.75, s32[1024]{0:T(1024)S(1)} %pad_clamp_fusion.2), kind=kCustom, calls=%fused_computation.5 | custom fusion | bytes 2099200 | tf_op jit(solution)/shard_map/gather | solution.py:118
  105.0 1.9 copy.38
  106.9 1.7 constant_dynamic-slice_fusion.3
  108.6 2.7 %fusion.13 = f32[512,1024]{1,0:T(8,128)} fusion(bf16[128,512]{0,1:T(8,128)(2,1)S(1)} %bitcast.91, bf16[1024,128]{1,0:T(8,128)(2,1)} %fusion), kind=kOutput, calls=%fused_computation.53 | convolution fusion | flops 134217728 | bytes 2490368 | tf_op jit(solution)/shard_map/dot_general | solution.py:23
  111.8 4.6 %all-to-all-done.3 = bf16[8,32,1024]{2,1,0:T(8,128)(2,1)} async-done(((bf16[8,32,1024]{2,1,0:T(8,128)(2,1)}), bf16[8,32,1024]{2,1,0:T(8,128)(2,1)}, u32[]{:S(2)}, u32[]{:S(2)}) %all-to-all-start.3) | async-done | bytes 524320 | tf_op jit(solution)/shard_map/all_to_all | solution.py:64
  116.5 2.4 %pad_maximum_fusion.2 = bf16[896,1024]{1,0:T(8,128)(2,1)} fusion(bf16[256,1024]{1,0:T(8,128)(2,1)} %bitcast.24, bf16[512,1024]{1,0:T(8,128)(2,1)S(1)} %copy-done.4, bf16[128,1024]{1,0:T(8,128)(2,1)S(1)} %get-tuple-element.10), kind=kLoop, calls=%fused_computation.11 | loop fusion | flops 5505024 | bytes 3670016 | tf_op jit(solution)/shard_map/concatenate | solution.py:15
  118.9 2.1 %gather_fusion.7 = bf16[4,128,1024]{2,1,0:T(8,128)(2,1)S(1)} fusion(bf16[7,128,1024]{2,1,0:T(8,128)(2,1)} %bitcast.79, s32[1024]{0:T(1024)S(1)} %pad_clamp_fusion), kind=kCustom, calls=%fused_computation.7 | custom fusion | bytes 2097168 | tf_op jit(solution)/shard_map/gather | solution.py:17
  122.6 2.1 convolution_add_fusion.1
  124.7 1.7 collective-permute-done.1
  126.8 2.5 %pad_maximum_fusion = f32[8,128,1024]{2,1,0:T(8,128)} fusion(f32[8,64,1024]{2,1,0:T(8,128)S(1)} %bitcast.77, f32[8,64,1024]{2,1,0:T(8,128)S(1)} %bitcast.76), kind=kLoop, calls=%fused_computation.9 | loop fusion | flops 1048576 | bytes 8388608 | tf_op jit(solution)/shard_map/concatenate | solution.py:123
  129.4 51.5 %reduce-scatter.5.cloned.1.call-done = f32[1,128,1024]{2,1,0:T(8,128)} async-done(((f32[8,128,1024]{2,1,0:T(8,128)}), f32[1,128,1024]{2,1,0:T(8,128)}) %reduce-scatter.5.cloned.1.call-update) | async-done | bytes 524304 | tf_op jit(solution)/shard_map/reduce_scatter | solution.py:43
  182.4 19.0 %all_to_all.25 = f32[32,4,1024]{2,1,0:T(4,128)S(1)} all-to-all(f32[32,4,1024]{2,1,0:T(4,128)S(1)} %bitcast_select_fusion), channel_id=1, replica_groups=mesh['group'=8,'dom'=32] {'dom'}, dimensions={0} | all-to-all | bytes 1048576 | tf_op jit(solution)/shard_map/all_to_all | solution.py:54
  (72 shorter events, 15.4 us)
Async XLA Ops:
  7.2 12.4 %copy-start = (bf16[1024,1024]{1,0:T(8,128)(2,1)S(1)}, bf16[1024,1024]{1,0:T(8,128)(2,1)}, u32[]{:S(2)}) copy-start(bf16[1024,1024]{1,0:T(8,128)(2,1)} %param.14) | copy-start | bytes 6291460
  7.2 12.4 %copy-start.8 = (bf16[1,4,128,128]{3,2,1,0:T(8,128)(2,1)S(1)}, bf16[1,4,128,128]{3,2,1,0:T(8,128)(2,1)}, u32[]{:S(2)}) copy-start(bf16[1,4,128,128]{3,2,1,0:T(8,128)(2,1)} %param.19) | copy-start | bytes 393220
  7.2 12.4 %copy-start.9 = (bf16[128,1024]{1,0:T(8,128)(2,1)S(1)}, bf16[128,1024]{1,0:T(8,128)(2,1)}, u32[]{:S(2)}) copy-start(bf16[128,1024]{1,0:T(8,128)(2,1)} %param.12) | copy-start | bytes 786436
  10.5 27.0 %all-to-all-start.1 = ((bf16[8,32,1024]{2,1,0:T(8,128)(2,1)}), bf16[8,32,1024]{2,1,0:T(8,128)(2,1)S(1)}, u32[]{:S(2)}, u32[]{:S(2)}) async-start(bf16[8,32,1024]{2,1,0:T(8,128)(2,1)} %broadcast_in_dim.65), calls=%async_computation.1 | async-start | bytes 1048576 | tf_op jit(solution)/shard_map/all_to_all | solution.py:64
  19.5 63.3 %reduce-scatter.3.cloned.1.call-start = ((), (), s32[]{:S(2)}) async-start(), calls=%async_computation.7 | async-start | bytes 1179648 | tf_op jit(solution)/shard_map/reduce_scatter | solution.py:102
  22.1 3.1 %copy-start.15 = (s32[1,4]{1,0:T(1,128)S(1)}, s32[1,4]{1,0:T(1,128)}, u32[]{:S(2)}) copy-start(s32[1,4]{1,0:T(1,128)} %param.18) | copy-start | bytes 52
  29.4 1.9 copy-start.3
  31.9 1.4 copy-start.13
  32.0 1.5 copy-start.1
  36.3 8.8 %copy-start.2 = (bf16[128,1024]{1,0:T(8,128)(2,1)S(1)}, bf16[128,1024]{1,0:T(8,128)(2,1)}, u32[]{:S(2)}) copy-start(bf16[128,1024]{1,0:T(8,128)(2,1)} %param.11) | copy-start | bytes 786436
  37.5 10.5 %copy-start.7 = (bf16[8,32,1024]{2,1,0:T(8,128)(2,1)}, bf16[8,32,1024]{2,1,0:T(8,128)(2,1)S(1)}, u32[]{:S(2)}) copy-start(bf16[8,32,1024]{2,1,0:T(8,128)(2,1)S(1)} %all-to-all-done.1) | copy-start | bytes 1572868
  37.5 24.6 %all-to-all-start = ((bf16[32,16,1024]{2,1,0:T(8,128)(2,1)}), bf16[32,16,1024]{2,1,0:T(8,128)(2,1)}, u32[]{:S(2)}, u32[]{:S(2)}) async-start(bf16[32,16,1024]{2,1,0:T(8,128)(2,1)} %bitcast.82), calls=%async_computation | async-start | bytes 2097152 | tf_op jit(solution)/shard_map/all_to_all | solution.py:105
  45.2 2.8 %copy-start.14 = (s32[512]{0:T(512)S(1)}, s32[512]{0:T(512)}, u32[]{:S(2)}) copy-start(s32[512]{0:T(512)} %param.16) | copy-start | bytes 6148
  48.0 18.1 %copy-start.16 = (s32[1,4]{1,0:T(1,128)S(1)}, s32[1,4]{1,0:T(1,128)}, u32[]{:S(2)}) copy-start(s32[1,4]{1,0:T(1,128)} %param.18) | copy-start | bytes 52
  62.1 28.3 %all-to-all-start.2 = ((bf16[32,16,1024]{2,1,0:T(8,128)(2,1)}), bf16[32,16,1024]{2,1,0:T(8,128)(2,1)S(1)}, u32[]{:S(2)}, u32[]{:S(2)}) async-start(bf16[32,16,1024]{2,1,0:T(8,128)(2,1)} %bitcast.81), calls=%async_computation.3 | async-start | bytes 2097152 | tf_op jit(solution)/shard_map/all_to_all | solution.py:106
  89.1 27.3 %copy-start.5 = (bf16[128,1024]{1,0:T(8,128)(2,1)}, bf16[128,1024]{1,0:T(8,128)(2,1)S(1)}, u32[]{:S(2)}) copy-start(bf16[128,1024]{1,0:T(8,128)(2,1)S(1)} %get-tuple-element.10) | copy-start | bytes 786436
  92.1 24.4 %all-to-all-start.3 = ((bf16[8,32,1024]{2,1,0:T(8,128)(2,1)}), bf16[8,32,1024]{2,1,0:T(8,128)(2,1)}, u32[]{:S(2)}, u32[]{:S(2)}) async-start(bf16[8,32,1024]{2,1,0:T(8,128)(2,1)} %broadcast_in_dim.70), calls=%async_computation.4 | async-start | bytes 1048576 | tf_op jit(solution)/shard_map/all_to_all | solution.py:64
  98.4 82.6 %reduce-scatter.5.cloned.1.call-start = ((), (), s32[]{:S(2)}) async-start(), calls=%async_computation.8 | async-start | bytes 4718592 | tf_op jit(solution)/shard_map/reduce_scatter | solution.py:43
  105.0 11.4 %copy-start.4 = (bf16[512,1024]{1,0:T(8,128)(2,1)S(1)}, bf16[512,1024]{1,0:T(8,128)(2,1)}, u32[]{:S(2)}) copy-start(bf16[512,1024]{1,0:T(8,128)(2,1)} %gather_fusion.5) | copy-start | bytes 3145732
  111.3 11.3 %collective-permute-start = (f32[512,1024]{1,0:T(8,128)}, f32[512,1024]{1,0:T(8,128)}, u32[]{:S(2)}, u32[]{:S(2)}) collective-permute-start(f32[512,1024]{1,0:T(8,128)} %fusion.13), channel_id=1, source_target_pairs={{0,1},{1,0},{2,3},{3,2},{4,5},{5,4},{6,7},{7,6},{8,9},{9,8},{10,11... | collective-permute-start | bytes 6291464 | tf_op jit(solution)/shard_map/ppermute | solution.py:37
  118.9 2.7 %copy-start.11 = (bf16[128,8,16,1,4]{0,4,3,2,1:T(4,128)(2,1)S(1)}, bf16[128,8,16,1,4]{0,4,3,2,1:T(4,128)(2,1)}, u32[]{:S(2)}) copy-start(bf16[128,8,16,1,4]{0,4,3,2,1:T(4,128)(2,1)} %get-tuple-element.14) | copy-start | bytes 393220
  121.1 1.5 copy-start.6
  121.1 1.5 copy-start.12
  122.0 4.4 %collective-permute-start.1 = (f32[512,1024]{1,0:T(8,128)S(1)}, f32[512,1024]{1,0:T(8,128)S(1)}, u32[]{:S(2)}, u32[]{:S(2)}) collective-permute-start(f32[512,1024]{1,0:T(8,128)S(1)} %fusion.14), channel_id=1, source_target_pairs={{0,1},{1,0},{2,3},{3,2},{4,5},{5,4},{6,7},{7,6},{8,9},{9,8},{10,11... | collective-permute-start | bytes 6291464 | tf_op jit(solution)/shard_map/ppermute | solution.py:37
  122.6 3.8 %copy-start.10 = (bf16[128,8,16,1,4]{0,4,3,2,1:T(4,128)(2,1)S(1)}, bf16[128,8,16,1,4]{0,4,3,2,1:T(4,128)(2,1)}, u32[]{:S(2)}) copy-start(bf16[128,8,16,1,4]{0,4,3,2,1:T(4,128)(2,1)} %get-tuple-element.13) | copy-start | bytes 393220
Sparse Core Ops, SparseCore 0:
  33.4 37.1 reduce-scatter.2
  129.4 51.4 reduce-scatter.4
